TPU v7x, 128 devices: a whole 4x4x4 slice. The times are simulated.
128 devices in a mesh: dp: 4 (over y_hi, core), fsdp: 32 (over x, y_lo, z).
Axes of the slice: x: 4, y: 4 (y_hi: 2, y_lo: 2; y = y_hi * 2 + y_lo), z: 4, core: 2. Of those that a mesh axis runs over, the one named last changes fastest.
Arguments:
- activations: bfloat16 [16384, 8192], P(('dp', 'fsdp')), may hold values from -630 to 630, as said below
- gain: bfloat16 [8192], P('fsdp'), may hold values from 0.25 to 1.75
- key_weight: bfloat16 [8192, 512], P('fsdp'), may hold values from -0.0625 to 0.0625
- key_gain: float32 [128], replicated, may hold values from 0.25 to 1.75
- cotangent: bfloat16 [16384, 512], P(('dp', 'fsdp')), may hold values from -6 to 6
- directions: bfloat16 [8192, 8], P('fsdp'), may hold values from -6 to 6
Outputs:
- ortho_basis: float32 [8192, 8], P('fsdp')
- grad: float32 [8192], P('fsdp')
Inputs may be any that keep to these rules, and one draw needn't show every extreme that they name: The block's input activations.
All inputs are finite; a program needn't handle non-finite values.
Results may differ from a plain program's by a relative error of at most 0.01.
Values may be sent and summed in bfloat16 or wider, within the bound.
No kernel may reach another device: no remote copies, remote signals or barrier semaphores. Data moves between devices by JAX's collectives and lax.ppermute only.
A program may use at most 128 MiB of HBM per device.

v0:
```python
import math

import jax
import jax.numpy as jnp
from jax import lax
from jax.sharding import PartitionSpec as P

D = 8192
HEADS_KV = 4
HEAD_DIM = 128


def in_blocks(shard, dim, devices):
    shape = shard.shape
    parts = shard.reshape(*shape[:dim], devices, shape[dim] // devices, *shape[dim + 1 :])
    return jnp.moveaxis(parts, dim, 0)


def sum_at_owner(shard, axis, dim):
    devices = lax.axis_size(axis)
    parts = lax.all_to_all(in_blocks(shard, dim, devices), axis, 0, 0, tiled=True)
    return jnp.sum(parts, axis=0)


def copy_for_each(shard, axis):
    copies = jnp.broadcast_to(shard, (lax.axis_size(axis), *shard.shape))
    return lax.all_to_all(copies, axis, split_axis=0, concat_axis=0, tiled=True)


def of_everyone(shard, axis):
    return copy_for_each(shard, axis).sum(axis=0)


def key_stats(key_rows, weighted_flat):
    shaped = key_rows.reshape(key_rows.shape[0], HEADS_KV, HEAD_DIM)
    key_scale = jnp.sqrt(jnp.mean(shaped * shaped, axis=-1, keepdims=True) + 1e-05)
    unit_keys = shaped / key_scale
    weighted = weighted_flat.reshape(shaped.shape)
    inner_sum = jnp.sum(unit_keys * weighted, axis=-1, keepdims=True)
    grad_keys = (weighted - unit_keys * inner_sum / HEAD_DIM) / key_scale
    return (key_scale, unit_keys, weighted, inner_sum, grad_keys)


def second_order(tangent_keys, key_scale, unit_keys, weighted, inner_sum, grad_keys):
    shift_rate = jnp.sum(unit_keys * tangent_keys, axis=-1, keepdims=True) / HEAD_DIM
    unit_change = (tangent_keys - unit_keys * shift_rate) / key_scale
    along = jnp.sum(unit_change * weighted, axis=-1, keepdims=True)
    return (
        -(unit_change * inner_sum + unit_keys * along) / (HEAD_DIM * key_scale)
        - grad_keys * shift_rate / key_scale
    )


def project_rows(back_rows, normed, weight_rows):
    row_count = weight_rows.shape[0]
    block_width = math.gcd(row_count, 512)

    def project_one_block(position):
        offset = position * block_width
        weight_part = lax.dynamic_slice_in_dim(weight_rows, offset, block_width, 0)
        input_part = lax.dynamic_slice_in_dim(normed, offset, block_width, 1)
        product = jnp.dot(back_rows, weight_part.T, preferred_element_type=jnp.float32)
        product = product.reshape(-1, input_part.shape[0], block_width)
        return jnp.sum(product * input_part[None], axis=1)

    block_parts = lax.map(project_one_block, jnp.arange(row_count // block_width, dtype=jnp.int32))
    return jnp.transpose(block_parts, (1, 0, 2)).reshape(block_parts.shape[1], row_count)


def per_device(activations, gain, key_weight, key_gain, cotangent, directions):
    tokens_dev = activations.shape[0]
    total_tokens = tokens_dev * lax.axis_size("dp") * lax.axis_size("fsdp")
    values = activations.astype(jnp.float32)
    normed = values / jnp.sqrt(jnp.mean(values * values, axis=1, keepdims=True) + 1e-05)
    width_keys = key_weight.shape[1]
    count_dirs = directions.shape[1]
    initial = (
        jnp.zeros((tokens_dev, width_keys), jnp.float32),
        jnp.zeros((count_dirs * tokens_dev, width_keys), jnp.float32),
    )
    whole_weight, whole_dirs, whole_gain = (
        lax.all_gather(key_weight, "fsdp", axis=0, tiled=True),
        lax.all_gather(directions, "fsdp", axis=0, tiled=True),
        lax.all_gather(gain, "fsdp", axis=0, tiled=True),
    )
    row_count = whole_weight.shape[0]
    block_width = math.gcd(row_count, 512)

    def forward_one_block(position, sums_now):
        key_sum, tangent_sum = sums_now
        offset = position * block_width
        weight_part = lax.dynamic_slice_in_dim(whole_weight, offset, block_width, 0)
        direction_part = lax.dynamic_slice_in_dim(whole_dirs, offset, block_width, 0).astype(
            jnp.float32
        )
        gain_part = lax.dynamic_slice_in_dim(whole_gain, offset, block_width, 0).astype(jnp.float32)
        input_part = lax.dynamic_slice_in_dim(normed, offset, block_width, 1)
        scaled_in = (input_part * gain_part[None, :]).astype(jnp.bfloat16)
        key_sum = key_sum + jnp.dot(scaled_in, weight_part, preferred_element_type=jnp.float32)
        lifted = (input_part[None] * direction_part.T[:, None, :]).astype(jnp.bfloat16)
        tangent_sum = tangent_sum + jnp.dot(
            lifted.reshape(-1, block_width), weight_part, preferred_element_type=jnp.float32
        )
        return (key_sum, tangent_sum)

    key_rows, tangent_flat = lax.fori_loop(0, row_count // block_width, forward_one_block, initial)
    weighted_flat = cotangent.astype(jnp.float32) * jnp.tile(key_gain, HEADS_KV)[None, :]
    key_scale, unit_keys, weighted, inner_sum, grad_keys = key_stats(key_rows, weighted_flat)
    tangent_keys = tangent_flat.reshape(count_dirs, tokens_dev, HEADS_KV, HEAD_DIM)
    second = second_order(tangent_keys, key_scale, unit_keys, weighted, inner_sum, grad_keys)
    back_rows = jnp.concatenate([grad_keys[None], second], axis=0).astype(jnp.bfloat16)
    back_rows = back_rows.reshape(-1, width_keys)
    partial_terms = project_rows(back_rows, normed, whole_weight)
    shared_rows = sum_at_owner(partial_terms, "fsdp", 1)
    summed = of_everyone(shared_rows, "dp") / math.sqrt(total_tokens)
    images = summed[1:]
    gram_matrix = of_everyone(jnp.dot(images, images.T), "fsdp")
    factor = jnp.linalg.cholesky(gram_matrix)
    ortho_basis = math.sqrt(D) * jax.scipy.linalg.solve_triangular(factor, images, lower=True)
    return (ortho_basis.T, summed[0])


def solution(mesh):
    placed = (
        P(("dp", "fsdp"), None),
        P("fsdp"),
        P("fsdp", None),
        P(),
        P(("dp", "fsdp"), None),
        P("fsdp", None),
    )
    return jax.shard_map(
        per_device,
        mesh=mesh,
        in_specs=placed,
        out_specs=(P("fsdp", None), P("fsdp")),
        check_vma=False,
    )
```

profile of v0, /device:TPU:0, one launch (start us, length us, event | category | flops | bytes accessed | tf_op | source)
XLA Modules:
  0.0 507.3 jit_solution(15134037678147241008)
XLA Ops:
  11.1 82.8 %all-gather = bf16[32,1,256]{2,1,0:T(2,128)(2,1)S(1)} all-gather(bf16[1,1,256]{2,1,0:T(2,128)(2,1)S(1)} %reshape.125), channel_id=1, replica_groups=mesh['dp'=4,'fsdp'=32] {'fsdp'}, dimensions={0}, use_global_device_ids=true | all-gather | bytes 16896 | tf_op jit(solution)/shard_map/all_gather | solution.py:84
  94.6 76.5 %all_gather.11 = bf16[8192,8]{0,1:T(8,128)(2,1)S(1)} all-gather(bf16[256,8]{0,1:T(8,128)(2,1)} %param.15), channel_id=1, replica_groups=mesh['dp'=4,'fsdp'=32] {'fsdp'}, dimensions={0}, use_global_device_ids=true | all-gather | bytes 135168 | tf_op jit(solution)/shard_map/all_gather | solution.py:83
  171.1 2.1 fusion.8
  173.2 2.5 convert_divide_fusion
  175.6 2.4 all-gather.3.cloned.1.call-done
  178.1 86.6 %while.27 = (s32[]{:T(128)}, f32[128,512]{1,0:T(8,128)S(1)}, f32[1024,512]{1,0:T(8,128)S(1)}, f32[128,8192]{1,0:T(8,128)}, bf16[8192]{0:T(1024)(128)(2,1)}, /*in...) while((s32[]{:T(128)}, f32[128,512]{1,0:T(8,128)S(1)}, ...), condition=%wide.region_2.0_spmd.clone, body=%wide.region_1.0_spmd.clone.sunk | while | flops 606343680 | bytes 8960693 | solution.py:106
  179.3 2.0 select_add_fusion.2
  184.7 2.0 select_add_fusion.2
  190.1 2.0 select_add_fusion.2
  195.5 2.0 select_add_fusion.2
  200.9 2.0 select_add_fusion.2
  203.7 1.4 convolution_add_fusion.2
  206.4 2.0 select_add_fusion.2
  209.1 1.4 convolution_add_fusion.2
  211.8 2.0 select_add_fusion.2
  217.2 2.0 select_add_fusion.2
  222.6 2.0 select_add_fusion.2
  228.0 2.0 select_add_fusion.2
  233.4 2.0 select_add_fusion.2
  238.9 2.0 select_add_fusion.2
  244.3 2.0 select_add_fusion.2
  249.7 2.0 select_add_fusion.2
  255.1 2.0 select_add_fusion.2
  260.5 2.0 select_add_fusion.2
  265.2 1.7 reshape.124
  267.7 2.9 multiply_reduce_fusion.2
  271.0 45.4 %fusion.10 = bf16[8,128,4,128]{3,2,1,0:T(4,128)(2,1)S(1)} fusion(f32[128,4,128]{2,1,0:T(4,128)S(1)} %subtract_divide_fusion.1, f32[128,4]{1,0:T(8,128)S(1)} %get-tuple-element.220, f32[128,4,128]{2,1,0:T(4,128)S(1)} %copy-done.3, f32[128,4]{1,0:T(8,128)S(1)} %get-tuple-element.218, f32[128,4]{1,0:T(8,128)S(1)} %get-tuple-element.221, ...), kind=kOutput, calls=%fused_computation.27 | output fusion | flops 8392831 | bytes 3954688 | tf_op jit(solution)/shard_map/mul | solution.py:49
  317.4 137.3 %while.26 = (s32[]{:T(128)}, f32[16,9,512]{2,1,0:T(8,128)}, s32[16]{0:T(128)S(1)}, bf16[8192,512]{1,0:T(8,128)(2,1)}, bf16[1152,512]{1,0:T(8,128)(2,1)S(1)}, /*i...) while((s32[]{:T(128)}, f32[16,9,512]{2,1,0:T(8,128)}, s32[16]{0:T(128)S(1)}, ...), condition=%wide.region_9.10_spmd, body=%wide.region_7.9_spmd.sunk | while | flops 605154816 | bytes 11997863 | solution.py:66
  318.7 3.4 convolution_bitcast_fusion.2
  322.0 2.0 copy.39
  327.2 3.4 convolution_bitcast_fusion.2
  330.6 2.0 copy.39
  335.8 3.4 convolution_bitcast_fusion.2
  339.2 2.0 copy.39
  344.4 3.4 convolution_bitcast_fusion.2
  347.8 2.0 copy.39
  353.0 3.4 convolution_bitcast_fusion.2
  356.4 2.0 copy.39
  361.6 3.4 convolution_bitcast_fusion.2
  364.9 2.0 copy.39
  370.2 3.4 convolution_bitcast_fusion.2
  373.5 2.0 copy.39
  378.7 3.4 convolution_bitcast_fusion.2
  382.1 2.0 copy.39
  387.3 3.4 convolution_bitcast_fusion.2
  390.7 2.0 copy.39
  395.9 3.4 convolution_bitcast_fusion.2
  399.3 2.0 copy.39
  404.5 3.4 convolution_bitcast_fusion.2
  407.8 2.0 copy.39
  413.1 3.4 convolution_bitcast_fusion.2
  416.4 2.0 copy.39
  421.7 3.4 convolution_bitcast_fusion.2
  425.0 2.0 copy.39
  430.2 3.4 convolution_bitcast_fusion.2
  433.6 2.0 copy.39
  438.8 3.4 convolution_bitcast_fusion.2
  442.2 2.0 copy.39
  447.4 3.4 convolution_bitcast_fusion.2
  450.8 2.0 copy.39
  456.2 17.6 %all_to_all.15 = f32[32,9,256]{2,1,0:T(8,128)S(1)} all-to-all(f32[32,9,256]{2,1,0:T(8,128)S(1)} %copy.27), channel_id=1, replica_groups=mesh['dp'=4,'fsdp'=32] {'fsdp'}, dimensions={0} | all-to-all | bytes 589824 | tf_op jit(solution)/shard_map/all_to_all | solution.py:21
  473.9 9.5 %all_to_all.16 = f32[4,9,256]{2,1,0:T(8,128)S(1)} all-to-all(f32[4,9,256]{2,1,0:T(8,128)S(1)} %broadcast_in_dim.28), channel_id=1, replica_groups=mesh['dp'=4,'fsdp'=32] {'dp'}, dimensions={0} | all-to-all | bytes 73728 | tf_op jit(solution)/shard_map/all_to_all | solution.py:27
  484.2 3.9 all-to-all-start.2
  488.7 8.2 %all-to-all-done.2 = f32[32,8,8]{2,1,0:T(8,128)S(1)} async-done(((f32[32,8,8]{2,1,0:T(8,128)}), f32[32,8,8]{2,1,0:T(8,128)S(1)}, u32[]{:S(2)}, u32[]{:S(2)}) %all-to-all-start.2) | async-done | bytes 8224 | tf_op jit(solution)/shard_map/all_to_all | solution.py:27
  (195 shorter events, 104.6 us)
Async XLA Ops:
  7.2 0.8 copy-start
  7.2 170.9 %all-gather.3.cloned.1.call-start = ((), (), s32[]{:S(2)}) async-start(), calls=%async_computation.3 | async-start | bytes 8650752 | tf_op jit(solution)/shard_map/all_gather | solution.py:82
  94.0 79.2 %copy-start.1 = (bf16[128,8192]{1,0:T(8,128)(2,1)S(1)}, bf16[128,8192]{1,0:T(8,128)(2,1)}, u32[]{:S(2)}) copy-start(bf16[128,8192]{1,0:T(8,128)(2,1)} %param.10) | copy-start | bytes 6291460
  265.2 1.8 copy-start.3
  267.6 3.0 copy-start.4
  267.6 3.4 copy-start.2
  484.2 12.6 %all-to-all-start.2 = ((f32[32,8,8]{2,1,0:T(8,128)}), f32[32,8,8]{2,1,0:T(8,128)S(1)}, u32[]{:S(2)}, u32[]{:S(2)}) async-start(f32[32,8,8]{2,1,0:T(8,128)} %broadcast_in_dim.48), calls=%async_computation.2 | async-start | bytes 262144 | tf_op jit(solution)/shard_map/all_to_all | solution.py:27
Sparse Core Ops, SparseCore 0:
  9.6 168.3 all-gather.2
where the time goes:
time: 512 us; the launch traced here: 507 us
  blocking collectives  186 us (36%)
  matrix products  109 us (21%)
  local copies, waits for them, and re-layouts  90.5 us (18%)
  other arithmetic  80.3 us (16%)
  between operations  14.3 us (3%)
  loops' own time  11.7 us (2%)
  waiting for transfers between devices  11.3 us (2%)
    all_gather x1, blocking collectives, per_device(): lax.all_gather(gain, 'fsdp', axis=0, tiled=True)  82.8 us
    all_gather x1, blocking collectives, per_device(): lax.all_gather(directions, 'fsdp', axis=0, tiled=True)  76.5 us
    dot_general x16, matrix products, project_one_block(): jnp.dot(back_rows, weight_part.T, preferred_element_type=jnp.float32)  53.8 us
    mul x1, other arithmetic, second_order(): unit_keys * along  45.4 us
    dot_general x16, local copies, waits for them, and re-layouts, project_one_block(): jnp.dot(back_rows, weight_part.T, preferred_element_type=jnp.float32)  32.5 us
    dot_general x16, matrix products, forward_one_block(): jnp.dot(lifted.reshape(-1, block_width), weight_part, preferred_element_t...  32.1 us
    dot_general x16, matrix products, forward_one_block(): jnp.dot(scaled_in, weight_part, preferred_element_type=jnp.float32)  22 us
    all_to_all x1, blocking collectives, sum_at_owner(): lax.all_to_all(in_blocks(shard, dim, devices), axis, 0, 0, tiled=True)  17.6 us
  transfers between devices with their start and end apart: 2, of which 2 were waited for; matrix products, arithmetic and copies ran while one was open for 2% of the time, Pallas kernels for 0%

commit v1 on v0

v1 whole, which is shorter than its diff:
```python
import math

import jax
import jax.numpy as jnp
from jax import lax
from jax.experimental import pallas as pl
from jax.experimental.pallas import tpu as pltpu
from jax.sharding import PartitionSpec as P

D = 8192
HEADS_KV = 4
HEAD_DIM = 128
FWD_TILE = 1024
BWD_TILE = 1024


def in_blocks(shard, dim, devices):
    shape = shard.shape
    parts = shard.reshape(*shape[:dim], devices, shape[dim] // devices, *shape[dim + 1 :])
    return jnp.moveaxis(parts, dim, 0)


def sum_at_owner(shard, axis, dim):
    devices = lax.axis_size(axis)
    parts = lax.all_to_all(in_blocks(shard, dim, devices), axis, 0, 0, tiled=True)
    return jnp.sum(parts, axis=0)


def copy_for_each(shard, axis):
    copies = jnp.broadcast_to(shard, (lax.axis_size(axis), *shard.shape))
    return lax.all_to_all(copies, axis, split_axis=0, concat_axis=0, tiled=True)


def of_everyone(shard, axis):
    return copy_for_each(shard, axis).sum(axis=0)


def key_stats(key_rows, weighted_flat):
    shaped = key_rows.reshape(key_rows.shape[0], HEADS_KV, HEAD_DIM)
    key_scale = jnp.sqrt(jnp.mean(shaped * shaped, axis=-1, keepdims=True) + 1e-05)
    unit_keys = shaped / key_scale
    weighted = weighted_flat.reshape(shaped.shape)
    inner_sum = jnp.sum(unit_keys * weighted, axis=-1, keepdims=True)
    grad_keys = (weighted - unit_keys * inner_sum / HEAD_DIM) / key_scale
    return (key_scale, unit_keys, weighted, inner_sum, grad_keys)


def second_order(tangent_keys, key_scale, unit_keys, weighted, inner_sum, grad_keys):
    shift_rate = jnp.sum(unit_keys * tangent_keys, axis=-1, keepdims=True) / HEAD_DIM
    unit_change = (tangent_keys - unit_keys * shift_rate) / key_scale
    along = jnp.sum(unit_change * weighted, axis=-1, keepdims=True)
    return (
        -(unit_change * inner_sum + unit_keys * along) / (HEAD_DIM * key_scale)
        - grad_keys * shift_rate / key_scale
    )


def gather_weight(key_weight, gain, directions):
    rows, width = key_weight.shape
    half = rows // 2
    core = lax.axis_index("dp") % 2
    mine = lax.dynamic_slice_in_dim(key_weight, core * half, half, 0)
    packed = jnp.concatenate([gain[:, None], directions], axis=1).reshape(-1)
    pad_rows = -(-packed.shape[0] // width)
    packed = jnp.pad(packed, (0, pad_rows * width - packed.shape[0])).reshape(pad_rows, width)
    piece = jnp.concatenate([mine, packed], axis=0)
    got = copy_for_each(piece, "fsdp")
    devices = got.shape[0]
    weight_half = got[:, :half, :]
    extras = got[:, half:, :].reshape(devices, -1)[:, : rows * (1 + directions.shape[1])]
    extras = extras.reshape(devices * rows, 1 + directions.shape[1])
    dp = lax.axis_size("dp")
    pairs = [(i, i ^ 1) for i in range(dp)]
    other = lax.ppermute(weight_half, "dp", pairs)
    low = jnp.where(core == 0, weight_half, other)
    high = jnp.where(core == 0, other, weight_half)
    whole = jnp.concatenate([low, high], axis=1).reshape(devices * rows, width)
    return whole, extras


def forward_kernel(act_ref, rms_ref, gd_ref, w_ref, out_ref, lhs_ref):
    k = pl.program_id(0)
    tokens = act_ref.shape[0]
    groups = gd_ref.shape[0]

    @pl.when(k == 0)
    def _():
        out_ref[...] = jnp.zeros_like(out_ref)

    normed = act_ref[...].astype(jnp.float32) / rms_ref[...]
    for j in range(groups):
        lhs_ref[j * tokens : (j + 1) * tokens, :] = (normed * gd_ref[j : j + 1, :]).astype(
            jnp.bfloat16
        )
    out_ref[...] += jnp.dot(lhs_ref[...], w_ref[...], preferred_element_type=jnp.float32)


def forward_rows(activations, rms, gd, whole_weight):
    tokens, width = activations.shape
    groups = gd.shape[0]
    keys = whole_weight.shape[1]
    tile = FWD_TILE
    return pl.pallas_call(
        forward_kernel,
        grid=(width // tile,),
        in_specs=[
            pl.BlockSpec((tokens, tile), lambda k: (0, k)),
            pl.BlockSpec((tokens, 1), lambda k: (0, 0)),
            pl.BlockSpec((groups, tile), lambda k: (0, k)),
            pl.BlockSpec((tile, keys), lambda k: (k, 0)),
        ],
        out_specs=pl.BlockSpec((groups * tokens, keys), lambda k: (0, 0)),
        out_shape=jax.ShapeDtypeStruct((groups * tokens, keys), jnp.float32),
        scratch_shapes=[pltpu.VMEM((groups * tokens, tile), jnp.bfloat16)],
        compiler_params=pltpu.CompilerParams(dimension_semantics=("arbitrary",)),
    )(activations, rms, gd, whole_weight)


def backward_kernel(back_ref, w_ref, act_ref, rms_ref, out_ref):
    tokens = act_ref.shape[0]
    groups = out_ref.shape[0]
    normed = act_ref[...].astype(jnp.float32) / rms_ref[...]
    product = lax.dot_general(
        back_ref[...],
        w_ref[...],
        (((1,), (1,)), ((), ())),
        preferred_element_type=jnp.float32,
    )
    product = product.reshape(groups, tokens, product.shape[1])
    out_ref[...] = jnp.sum(product * normed[None], axis=1)


def backward_terms(back_rows, whole_weight, activations, rms, groups):
    tokens, width = activations.shape
    keys = whole_weight.shape[1]
    tile = BWD_TILE
    return pl.pallas_call(
        backward_kernel,
        grid=(width // tile,),
        in_specs=[
            pl.BlockSpec((groups * tokens, keys), lambda d: (0, 0)),
            pl.BlockSpec((tile, keys), lambda d: (d, 0)),
            pl.BlockSpec((tokens, tile), lambda d: (0, d)),
            pl.BlockSpec((tokens, 1), lambda d: (0, 0)),
        ],
        out_specs=pl.BlockSpec((groups, tile), lambda d: (0, d)),
        out_shape=jax.ShapeDtypeStruct((groups, width), jnp.float32),
        compiler_params=pltpu.CompilerParams(dimension_semantics=("arbitrary",)),
    )(back_rows, whole_weight, activations, rms)


def per_device(activations, gain, key_weight, key_gain, cotangent, directions):
    tokens_dev = activations.shape[0]
    total_tokens = tokens_dev * lax.axis_size("dp") * lax.axis_size("fsdp")
    values = activations.astype(jnp.float32)
    rms = jnp.sqrt(jnp.mean(values * values, axis=1, keepdims=True) + 1e-05)
    width_keys = key_weight.shape[1]
    count_dirs = directions.shape[1]
    groups = count_dirs + 1

    whole_weight, extras = gather_weight(key_weight, gain, directions)
    gd = extras.astype(jnp.float32).T

    forward = forward_rows(activations, rms, gd, whole_weight)
    forward = forward.reshape(groups, tokens_dev, width_keys)
    key_rows = forward[0]
    tangent_flat = forward[1:]
    weighted_flat = cotangent.astype(jnp.float32) * jnp.tile(key_gain, HEADS_KV)[None, :]
    key_scale, unit_keys, weighted, inner_sum, grad_keys = key_stats(key_rows, weighted_flat)
    tangent_keys = tangent_flat.reshape(count_dirs, tokens_dev, HEADS_KV, HEAD_DIM)
    second = second_order(tangent_keys, key_scale, unit_keys, weighted, inner_sum, grad_keys)
    back_rows = jnp.concatenate([grad_keys[None], second], axis=0).astype(jnp.bfloat16)
    back_rows = back_rows.reshape(-1, width_keys)

    partial_terms = backward_terms(back_rows, whole_weight, activations, rms, groups)
    shared_rows = sum_at_owner(partial_terms, "fsdp", 1)
    summed = of_everyone(shared_rows, "dp") / math.sqrt(total_tokens)
    images = summed[1:]
    gram_matrix = of_everyone(
        jnp.dot(images, images.T, precision=lax.Precision.HIGHEST), "fsdp"
    )
    factor = jnp.linalg.cholesky(gram_matrix)
    ortho_basis = math.sqrt(D) * jax.scipy.linalg.solve_triangular(factor, images, lower=True)
    return (ortho_basis.T, summed[0])


def solution(mesh):
    placed = (
        P(("dp", "fsdp"), None),
        P("fsdp"),
        P("fsdp", None),
        P(),
        P(("dp", "fsdp"), None),
        P("fsdp", None),
    )
    return jax.shard_map(
        per_device,
        mesh=mesh,
        in_specs=placed,
        out_specs=(P("fsdp", None), P("fsdp")),
        check_vma=False,
    )
```

time: 512 us -> 222 us (0.43)
  matrix products: 109 us -> 0.93 us
  blocking collectives: 186 us -> 88.6 us
  local copies, waits for them, and re-layouts: 90.5 us -> 24 us
  Pallas kernels: 0 us -> 28.6 us
  other arithmetic: 80.3 us -> 66 us
  between operations: 14.3 us -> 0.93 us
  loops' own time: 11.7 us -> 0 us
    all_gather x2 -> x0, blocking collectives: 159 us -> none  [the longest x1 82.8 us: per_device(): lax.all_gather(gain, 'fsdp', axis=0, tiled=True)]
    dot_general x49 -> x1, matrix products: 108 us -> 0.12 us  [per_device(): jnp.dot(images, images.T, precision=lax.Precision.HIGHEST)]
    all_to_all x1 -> x2, blocking collectives: 9.52 us -> 73 us  [copy_for_each(): return lax.all_to_all(copies, axis, split_axis=0, concat_axis=0, tiled=True)]
    dynamic_slice x48 -> x1, local copies, waits for them, and re-layouts: 40.5 us -> 0.02 us  [gather_weight(): mine = lax.dynamic_slice_in_dim(key_weight, core * half, half, 0)]
    dot_general x16 -> x0, local copies, waits for them, and re-layouts: 32.5 us -> none  [project_one_block(): jnp.dot(back_rows, weight_part.T, preferred_element_type=jnp.float32)]
    pallas_call x0 -> x2, Pallas kernels: none -> 28.6 us  [the longest x1 14.7 us: forward_rows(): pl.pallas_call(forward_kernel, grid=(width // tile,), in_specs=[pl.BlockS...]
    convert_element_type x32 -> x0, other arithmetic: 15.8 us -> none  [the longest x16 12 us: forward_one_block(): lax.dynamic_slice_in_dim(whole_gain, offset, block_width, 0)]
    another operation x2 -> x0, loops' own time: 11.7 us -> none  [the longest x1 10.8 us: project_rows(): lax.map(project_one_block, jnp.arange(row_count // block_width, dtype=jnp...]
  transfers between devices with their start and end apart: 2 -> 2, of which waited for: 2 -> 1; matrix products, arithmetic and copies ran while one was open for 2% -> 5% of each run, Pallas kernels for 0% -> 0%
where the time goes in v1:
time: 222 us; the launch traced here: 221 us
  blocking collectives  88.6 us (40%)
  other arithmetic  66 us (30%)
  Pallas kernels  28.6 us (13%)
  local copies, waits for them, and re-layouts  24 us (11%)
  waiting for transfers between devices  8.18 us (4%)
  starting transfers between devices  3.85 us (2%)
    all_to_all x2, blocking collectives, copy_for_each(): return lax.all_to_all(copies, axis, split_axis=0, concat_axis=0, tiled=True)  73 us
    mul x1, other arithmetic, second_order(): unit_keys * along  45.4 us
    all_to_all x1, blocking collectives, sum_at_owner(): lax.all_to_all(in_blocks(shard, dim, devices), axis, 0, 0, tiled=True)  15.6 us
    pallas_call x1, Pallas kernels, forward_rows(): pl.pallas_call(forward_kernel, grid=(width // tile,), in_specs=[pl.BlockS...  14.7 us
    pallas_call x1, Pallas kernels, backward_terms(): pl.pallas_call(backward_kernel, grid=(width // tile,), in_specs=[pl.Block...  14 us
    transpose x2, local copies, waits for them, and re-layouts, per_device(): gd = extras.astype(jnp.float32).T  8.97 us
    all_to_all x1, waiting for transfers between devices, copy_for_each(): return lax.all_to_all(copies, axis, split_axis=0, concat_axis=0, tiled=True)  8.18 us
    concatenate x1, other arithmetic, gather_weight(): whole = jnp.concatenate([low, high], axis=1).reshape(devices * rows, width)  7.56 us
  transfers between devices with their start and end apart: 2, of which 1 were waited for; matrix products, arithmetic and copies ran while one was open for 5% of the time, Pallas kernels for 0%

profile of v1, /device:TPU:0, one launch (start us, length us, event | category | flops | bytes accessed | tf_op | source)
XLA Modules:
  0.0 221.1 jit_solution(1837394804967604526)
XLA Ops:
  0.6 0.0 copy-start
  0.7 0.7 broadcast_in_dim.9
  1.4 0.7 pad_maximum_fusion.3
  2.1 0.1 copy.32
  2.2 0.2 reshape.132
  2.5 0.0 copy-done
  2.5 0.3 broadcast_in_dim.10
  2.8 63.4 %all_to_all.20 = bf16[32,133,512]{2,1,0:T(8,128)(2,1)S(1)} all-to-all(bf16[32,133,512]{2,1,0:T(8,128)(2,1)S(1)} %broadcast_in_dim.10), channel_id=1, replica_groups=mesh['dp'=4,'fsdp'=32] {'fsdp'}, dimensions={0} | all-to-all | bytes 8716288 | tf_op jit(solution)/shard_map/all_to_all | solution.py:31
  66.2 0.0 copy-start.1
  66.2 0.0 copy-start.6
  66.2 0.0 copy-start.5
  66.2 0.0 copy-start.2
  66.2 2.5 %slice.42 = bf16[32,128,512]{2,1,0:T(8,128)(2,1)} slice(bf16[32,133,512]{2,1,0:T(8,128)(2,1)S(1)} %all_to_all.20), slice={[0:32], [0:128], [0:512]} | slice | bytes 8388608 | tf_op jit(solution)/shard_map/slice | solution.py:69
  68.8 1.1 copy-done.1
  69.8 0.0 collective-permute-start
  69.8 0.0 slice-start
  69.8 0.0 copy-done.6
  69.8 0.0 copy-done.5
  69.9 0.1 reshape.136
  70.0 0.1 reshape.131
  70.1 0.0 copy-done.2
  70.1 0.5 multiply_reduce_fusion
  70.6 0.7 copy.34.rms_ref
  71.3 0.0 slice-done
  71.3 0.1 copy.43
  71.4 5.4 %reshape.139 = f32[8192,9]{1,0:T(8,128)} reshape(f32[32,2304]{1,0:T(8,128)S(1)} %slice_convert_fusion) | data formatting | bytes 589824 | tf_op jit(solution)/shard_map/transpose | solution.py:162
  76.9 3.5 %copy.33 = f32[8192,9]{0,1:T(8,128)} copy(f32[8192,9]{1,0:T(8,128)} %reshape.139) | data formatting | bytes 589824 | tf_op jit(solution)/shard_map/transpose | solution.py:162
  80.4 0.0 collective-permute-done
  80.4 5.7 %broadcast_select_fusion.1 = (bf16[32,128,512]{2,1,0:T(8,128)(2,1)}, bf16[32,128,512]{2,1,0:T(8,128)(2,1)}) fusion(bf16[32,128,512]{2,1,0:T(8,128)(2,1)} %collective-permute-done, pred[]{:T(512)S(6)} %eq.6, bf16[32,133,512]{2,1,0:T(8,128)(2,1)} %copy-done.1), kind=kLoop, calls=%fused_computation.4 | loop fusion | flops 4194304 | bytes 16777216 | tf_op jit(solution)/shard_map/jit(_where)/select_n | solution.py:75
  86.1 7.6 %pad_maximum_fusion = bf16[32,256,512]{2,1,0:T(8,128)(2,1)} fusion(bf16[32,128,512]{2,1,0:T(8,128)(2,1)} %get-tuple-element.5, bf16[32,128,512]{2,1,0:T(8,128)(2,1)} %get-tuple-element.4), kind=kLoop, calls=%fused_computation.1 | loop fusion | flops 16777216 | bytes 16777216 | tf_op jit(solution)/shard_map/concatenate | solution.py:77
  93.7 14.7 %shard_map.77 = f32[1152,512]{1,0:T(8,128)} custom-call(bf16[128,8192]{1,0:T(8,128)(2,1)} %act_ref.3, f32[128,1]{1,0:T(8,128)} %copy.34.rms_ref, f32[9,8192]{1,0:T(8,128)} %bitcast.35, bf16[8192,512]{1,0:T(8,128)(2,1)} %bitcast.30), custom_call_target="tpu_custom_call" | custom-call | tf_op jit(solution)/shard_map/pallas_call | solution.py:103
  108.3 1.0 slice.43
  109.3 0.0 slice-start.1
  109.3 0.1 reshape_squeeze.6
  109.4 0.8 reshape_squeeze.5
  110.2 0.8 slice-done.1
  111.0 1.8 reshape.137
  112.8 0.2 multiply_reduce_fusion.4
  113.0 0.4 multiply_reduce_fusion.3
  113.4 0.3 subtract_divide_fusion.1
  113.7 0.6 copy-done.3
  114.3 1.2 multiply_reduce_fusion.2
  115.6 0.0 copy-done.4
  115.6 0.4 fusion.6
  115.9 45.4 %fusion.2 = bf16[8,128,4,128]{3,2,1,0:T(4,128)(2,1)S(1)} fusion(f32[128,4,128]{2,1,0:T(4,128)S(1)} %subtract_divide_fusion.1, f32[128,4]{1,0:T(8,128)S(1)} %get-tuple-element.6, f32[128,4,128]{2,1,0:T(4,128)S(1)} %reshape.136, f32[128,4]{1,0:T(8,128)S(1)} %get-tuple-element.2, f32[128,4]{1,0:T(8,128)S(1)} %get-tuple-element.7, ...), kind=kOutput, calls=%fused_computation.10 | output fusion | flops 8392831 | bytes 3954688 | tf_op jit(solution)/shard_map/mul | solution.py:53
  161.3 0.8 pad_maximum_fusion.1
  162.1 1.3 copy.48
  163.4 14.0 %shard_map.78 = f32[9,8192]{1,0:T(8,128)} custom-call(bf16[1152,512]{1,0:T(8,128)(2,1)} %bitcast.33, bf16[8192,512]{1,0:T(8,128)(2,1)} %bitcast.31, bf16[128,8192]{1,0:T(8,128)(2,1)} %act_ref.3, f32[128,1]{1,0:T(8,128)} %copy.34.rms_ref), custom_call_target="tpu_custom_call" | custom-call | tf_op jit(solution)/shard_map/pallas_call | solution.py:137
  177.4 1.2 copy.45
  178.6 0.2 copy.49
  178.8 15.6 %all_to_all.21 = f32[32,9,256]{2,1,0:T(8,128)S(1)} all-to-all(f32[32,9,256]{2,1,0:T(8,128)S(1)} %bitcast.37), channel_id=1, replica_groups=mesh['dp'=4,'fsdp'=32] {'fsdp'}, dimensions={0} | all-to-all | bytes 589824 | tf_op jit(solution)/shard_map/all_to_all | solution.py:25
  194.4 0.1 reduce_sum.77
  194.5 9.6 %all_to_all.22 = f32[4,9,256]{2,1,0:T(8,128)S(1)} all-to-all(f32[4,9,256]{2,1,0:T(8,128)S(1)} %broadcast_in_dim.11), channel_id=1, replica_groups=mesh['dp'=4,'fsdp'=32] {'dp'}, dimensions={0} | all-to-all | bytes 73728 | tf_op jit(solution)/shard_map/all_to_all | solution.py:31
  204.1 0.1 fusion.8
  204.2 0.7 broadcast_in_dim.12
  204.9 3.9 %all-to-all-start.3 = ((f32[32,8,8]{2,1,0:T(8,128)}), f32[32,8,8]{2,1,0:T(8,128)S(1)}, u32[]{:S(2)}, u32[]{:S(2)}) async-start(f32[32,8,8]{2,1,0:T(8,128)} %broadcast_in_dim.12), calls=%async_computation.3 | async-start | bytes 262144 | tf_op jit(solution)/shard_map/all_to_all | solution.py:31
  208.7 0.6 slice.45
  209.3 8.2 %all-to-all-done.3 = f32[32,8,8]{2,1,0:T(8,128)S(1)} async-done(((f32[32,8,8]{2,1,0:T(8,128)}), f32[32,8,8]{2,1,0:T(8,128)S(1)}, u32[]{:S(2)}, u32[]{:S(2)}) %all-to-all-start.3) | async-done | bytes 8224 | tf_op jit(solution)/shard_map/all_to_all | solution.py:31
  217.5 0.1 copy.39
  217.6 0.7 cholesky.16
  218.3 0.6 compare_reduce_fusion
  219.0 0.6 fusion.10
  219.6 0.6 custom-call.7
  220.3 0.8 convolution_multiply_fusion
  (19 shorter events, 0.3 us)
Async XLA Ops:
  0.6 1.8 copy-start
  66.2 3.6 %copy-start.1 = (bf16[32,133,512]{2,1,0:T(8,128)(2,1)}, bf16[32,133,512]{2,1,0:T(8,128)(2,1)S(1)}, u32[]{:S(2)}) copy-start(bf16[32,133,512]{2,1,0:T(8,128)(2,1)S(1)} %all_to_all.20) | copy-start | bytes 13074436
  66.2 3.6 %copy-start.6 = (f32[128]{0:T(128)S(1)}, f32[128]{0:T(128)}, u32[]{:S(2)}) copy-start(f32[128]{0:T(128)} %param.9) | copy-start | bytes 1540
  66.2 3.6 %copy-start.5 = (bf16[128,512]{1,0:T(8,128)(2,1)S(1)}, bf16[128,512]{1,0:T(8,128)(2,1)}, u32[]{:S(2)}) copy-start(bf16[128,512]{1,0:T(8,128)(2,1)} %param.10) | copy-start | bytes 393220
  66.2 3.8 %copy-start.2 = (bf16[128,8192]{1,0:T(8,128)(2,1)S(1)}, bf16[128,8192]{1,0:T(8,128)(2,1)}, u32[]{:S(2)}) copy-start(bf16[128,8192]{1,0:T(8,128)(2,1)} %act_ref.3) | copy-start | bytes 6291460
  69.8 10.6 %collective-permute-start = (bf16[32,128,512]{2,1,0:T(8,128)(2,1)}, bf16[32,128,512]{2,1,0:T(8,128)(2,1)}, u32[]{:S(2)}, u32[]{:S(2)}) collective-permute-start(bf16[32,128,512]{2,1,0:T(8,128)(2,1)} %slice.42), channel_id=1, source_target_pairs={{0,32},{32,0},{64,96},{96,64},{1,33},{33,1},{65,97},{97,65},{2,34}... | collective-permute-start | bytes 12582920 | tf_op jit(solution)/shard_map/ppermute | solution.py:74
  69.8 1.5 slice-start
  109.3 1.7 slice-start.1
  112.8 1.6 copy-start.3
  114.3 1.2 copy-start.4
  204.9 12.6 %all-to-all-start.3 = ((f32[32,8,8]{2,1,0:T(8,128)}), f32[32,8,8]{2,1,0:T(8,128)S(1)}, u32[]{:S(2)}, u32[]{:S(2)}) async-start(f32[32,8,8]{2,1,0:T(8,128)} %broadcast_in_dim.12), calls=%async_computation.3 | async-start | bytes 262144 | tf_op jit(solution)/shard_map/all_to_all | solution.py:31

commit v2 on v1

v2 whole, which is shorter than its diff:
```python
import math

import jax
import jax.numpy as jnp
from jax import lax
from jax.experimental import pallas as pl
from jax.experimental.pallas import tpu as pltpu
from jax.sharding import PartitionSpec as P

D = 8192
HEADS_KV = 4
HEAD_DIM = 128
FWD_TILE = 1024
BWD_TILE = 1024


def in_blocks(shard, dim, devices):
    shape = shard.shape
    parts = shard.reshape(*shape[:dim], devices, shape[dim] // devices, *shape[dim + 1 :])
    return jnp.moveaxis(parts, dim, 0)


def sum_at_owner(shard, axis, dim):
    devices = lax.axis_size(axis)
    parts = lax.all_to_all(in_blocks(shard, dim, devices), axis, 0, 0, tiled=True)
    return jnp.sum(parts, axis=0)


def copy_for_each(shard, axis):
    copies = jnp.broadcast_to(shard, (lax.axis_size(axis), *shard.shape))
    return lax.all_to_all(copies, axis, split_axis=0, concat_axis=0, tiled=True)


def of_everyone(shard, axis):
    return copy_for_each(shard, axis).sum(axis=0)


def key_stats(key_rows, weighted_flat):
    shaped = key_rows.reshape(key_rows.shape[0], HEADS_KV, HEAD_DIM)
    key_scale = jnp.sqrt(jnp.mean(shaped * shaped, axis=-1, keepdims=True) + 1e-05)
    unit_keys = shaped / key_scale
    weighted = weighted_flat.reshape(shaped.shape)
    inner_sum = jnp.sum(unit_keys * weighted, axis=-1, keepdims=True)
    grad_keys = (weighted - unit_keys * inner_sum / HEAD_DIM) / key_scale
    return (key_scale, unit_keys, weighted, inner_sum, grad_keys)


def second_order(tangent_keys, key_scale, unit_keys, weighted, inner_sum, grad_keys):
    shift_rate = jnp.sum(unit_keys * tangent_keys, axis=-1, keepdims=True) / HEAD_DIM
    unit_change = (tangent_keys - unit_keys * shift_rate) / key_scale
    along = jnp.sum(unit_change * weighted, axis=-1, keepdims=True)
    return (
        -(unit_change * inner_sum + unit_keys * along) / (HEAD_DIM * key_scale)
        - grad_keys * shift_rate / key_scale
    )


def gather_weight(key_weight, gain, directions):
    rows, width = key_weight.shape
    half = rows // 2
    core = lax.axis_index("dp") % 2
    mine = lax.dynamic_slice_in_dim(key_weight, core * half, half, 0)
    extra = jnp.concatenate([gain[None, :], directions.T], axis=0)
    extra = jnp.pad(extra, ((0, 16 - extra.shape[0]), (0, width - rows)))
    piece = jnp.concatenate([mine, extra], axis=0)
    first = copy_for_each(piece, "fsdp")
    dp = lax.axis_size("dp")
    second = lax.ppermute(first, "dp", [(i, i ^ 1) for i in range(dp)])
    extras = first[:, half : half + 1 + directions.shape[1], :rows]
    extras = jnp.transpose(extras, (1, 0, 2)).reshape(extras.shape[1], -1)
    return first, second, extras.astype(jnp.float32)


def split_halves(values, core):
    lead = values.shape[0]
    blocks = values.reshape(lead, -1, 2, 128)
    low, high = blocks[:, :, 0, :], blocks[:, :, 1, :]
    first = jnp.where(core == 0, low, high).reshape(lead, -1)
    second = jnp.where(core == 0, high, low).reshape(lead, -1)
    return first, second


def join_halves(first, second, core):
    lead = first.shape[0]
    a = first.reshape(lead, -1, 1, 128)
    b = second.reshape(lead, -1, 1, 128)
    low = jnp.where(core == 0, a, b)
    high = jnp.where(core == 0, b, a)
    return jnp.concatenate([low, high], axis=2).reshape(lead, -1)


def middle_rows(acc, cot, key_gain_row, back_ref):
    tokens = cot.shape[0]
    groups = acc.shape[0] // tokens
    weighted_all = cot.astype(jnp.float32) * key_gain_row
    for h in range(HEADS_KV):
        cols = slice(h * HEAD_DIM, (h + 1) * HEAD_DIM)
        key = acc[0:tokens, cols]
        weighted = weighted_all[:, cols]
        key_scale = jnp.sqrt(jnp.sum(key * key, axis=-1, keepdims=True) / HEAD_DIM + 1e-05)
        unit_keys = key / key_scale
        inner_sum = jnp.sum(unit_keys * weighted, axis=-1, keepdims=True)
        grad_keys = (weighted - unit_keys * inner_sum / HEAD_DIM) / key_scale
        back_ref[0:tokens, cols] = grad_keys.astype(back_ref.dtype)
        for j in range(1, groups):
            tangent = acc[j * tokens : (j + 1) * tokens, cols]
            shift_rate = jnp.sum(unit_keys * tangent, axis=-1, keepdims=True) / HEAD_DIM
            unit_change = (tangent - unit_keys * shift_rate) / key_scale
            along = jnp.sum(unit_change * weighted, axis=-1, keepdims=True)
            second = -(unit_change * inner_sum + unit_keys * along) / (
                HEAD_DIM * key_scale
            ) - grad_keys * shift_rate / key_scale
            back_ref[j * tokens : (j + 1) * tokens, cols] = second.astype(back_ref.dtype)


def build_lhs(act_ref, rms_ref, gd_ref, lhs_ref):
    tokens = act_ref.shape[0]
    normed = act_ref[...].astype(jnp.float32) / rms_ref[...]
    for j in range(gd_ref.shape[0]):
        lhs_ref[j * tokens : (j + 1) * tokens, :] = (normed * gd_ref[j : j + 1, :]).astype(
            jnp.bfloat16
        )


def weight_tile(w_ref):
    shards, rows, width = w_ref.shape
    return w_ref[...].reshape(shards * rows, width)


def forward_first_kernel(act_ref, rms_ref, gd_ref, w_ref, out_ref, lhs_ref):
    k = pl.program_id(0)

    @pl.when(k == 0)
    def _():
        out_ref[...] = jnp.zeros_like(out_ref)

    build_lhs(act_ref, rms_ref, gd_ref, lhs_ref)
    out_ref[...] += jnp.dot(lhs_ref[...], weight_tile(w_ref), preferred_element_type=jnp.float32)


def forward_second_kernel(
    act_ref, rms_ref, gd_ref, w_ref, acc_in_ref, cot_ref, kg_ref, back_ref, lhs_ref, acc_ref
):
    k = pl.program_id(0)

    @pl.when(k == 0)
    def _():
        acc_ref[...] = acc_in_ref[...]

    build_lhs(act_ref, rms_ref, gd_ref, lhs_ref)
    acc_ref[...] += jnp.dot(lhs_ref[...], weight_tile(w_ref), preferred_element_type=jnp.float32)

    @pl.when(k == pl.num_programs(0) - 1)
    def _():
        middle_rows(acc_ref[...], cot_ref[...], kg_ref[...], back_ref)


def weight_spec(shards, half, keys):
    return pl.BlockSpec((shards, half, keys), lambda k: (k, 0, 0))


def forward_rows(act_first, act_second, rms, gd_first, gd_second, first, second, cot, kg_row):
    tokens, width = act_first.shape
    groups = gd_first.shape[0]
    keys = first.shape[2]
    half = width // first.shape[0]
    tile = FWD_TILE
    shards = tile // half
    common = [
        pl.BlockSpec((tokens, tile), lambda k: (0, k)),
        pl.BlockSpec((tokens, 1), lambda k: (0, 0)),
        pl.BlockSpec((groups, tile), lambda k: (0, k)),
        weight_spec(shards, half, keys),
    ]
    acc = pl.pallas_call(
        forward_first_kernel,
        grid=(width // tile,),
        in_specs=common,
        out_specs=pl.BlockSpec((groups * tokens, keys), lambda k: (0, 0)),
        out_shape=jax.ShapeDtypeStruct((groups * tokens, keys), jnp.float32),
        scratch_shapes=[pltpu.VMEM((groups * tokens, tile), jnp.bfloat16)],
        compiler_params=pltpu.CompilerParams(dimension_semantics=("arbitrary",)),
    )(act_first, rms, gd_first, first)
    return pl.pallas_call(
        forward_second_kernel,
        grid=(width // tile,),
        in_specs=common
        + [
            pl.BlockSpec((groups * tokens, keys), lambda k: (0, 0)),
            pl.BlockSpec((tokens, keys), lambda k: (0, 0)),
            pl.BlockSpec((1, keys), lambda k: (0, 0)),
        ],
        out_specs=pl.BlockSpec((groups * tokens, keys), lambda k: (0, 0)),
        out_shape=jax.ShapeDtypeStruct((groups * tokens, keys), jnp.bfloat16),
        scratch_shapes=[
            pltpu.VMEM((groups * tokens, tile), jnp.bfloat16),
            pltpu.VMEM((groups * tokens, keys), jnp.float32),
        ],
        compiler_params=pltpu.CompilerParams(dimension_semantics=("arbitrary",)),
    )(act_second, rms, gd_second, second, acc, cot, kg_row)


def backward_kernel(back_ref, w1_ref, w2_ref, act1_ref, act2_ref, rms_ref, out_ref):
    k = pl.program_id(0)
    steps = pl.num_programs(0) // 2
    tokens = act1_ref.shape[0]
    groups = out_ref.shape[0]

    def one(w_ref, act_ref):
        normed = act_ref[...].astype(jnp.float32) / rms_ref[...]
        product = lax.dot_general(
            back_ref[...],
            weight_tile(w_ref),
            (((1,), (1,)), ((), ())),
            preferred_element_type=jnp.float32,
        )
        product = product.reshape(groups, tokens, product.shape[1])
        out_ref[...] = jnp.sum(product * normed[None], axis=1)

    @pl.when(k < steps)
    def _():
        one(w1_ref, act1_ref)

    @pl.when(k >= steps)
    def _():
        one(w2_ref, act2_ref)


def backward_terms(back_rows, first, second, act_first, act_second, rms, groups):
    tokens, width = act_first.shape
    keys = first.shape[2]
    half = width // first.shape[0]
    tile = BWD_TILE
    shards = tile // half
    steps = width // tile
    low = lambda k: jnp.minimum(k, steps - 1)
    high = lambda k: jnp.maximum(k - steps, 0)
    return pl.pallas_call(
        backward_kernel,
        grid=(2 * steps,),
        in_specs=[
            pl.BlockSpec((groups * tokens, keys), lambda k: (0, 0)),
            pl.BlockSpec((shards, half, keys), lambda k: (low(k), 0, 0)),
            pl.BlockSpec((shards, half, keys), lambda k: (high(k), 0, 0)),
            pl.BlockSpec((tokens, tile), lambda k: (0, low(k))),
            pl.BlockSpec((tokens, tile), lambda k: (0, high(k))),
            pl.BlockSpec((tokens, 1), lambda k: (0, 0)),
        ],
        out_specs=pl.BlockSpec((groups, tile), lambda k: (0, k)),
        out_shape=jax.ShapeDtypeStruct((groups, 2 * width), jnp.float32),
        compiler_params=pltpu.CompilerParams(dimension_semantics=("arbitrary",)),
    )(back_rows, first, second, act_first, act_second, rms)


def per_device(activations, gain, key_weight, key_gain, cotangent, directions):
    tokens_dev = activations.shape[0]
    total_tokens = tokens_dev * lax.axis_size("dp") * lax.axis_size("fsdp")
    values = activations.astype(jnp.float32)
    rms = jnp.sqrt(jnp.mean(values * values, axis=1, keepdims=True) + 1e-05)
    width_keys = key_weight.shape[1]
    groups = directions.shape[1] + 1
    core = lax.axis_index("dp") % 2

    first, second, gd = gather_weight(key_weight, gain, directions)
    act_first, act_second = split_halves(activations, core)
    gd_first, gd_second = split_halves(gd, core)
    kg_row = jnp.tile(key_gain, HEADS_KV)[None, :]

    back_rows = forward_rows(
        act_first, act_second, rms, gd_first, gd_second, first, second, cotangent, kg_row
    )
    partial_terms = backward_terms(back_rows, first, second, act_first, act_second, rms, groups)
    half_width = act_first.shape[1]
    partial_terms = join_halves(
        partial_terms[:, :half_width], partial_terms[:, half_width:], core
    )
    shared_rows = sum_at_owner(partial_terms, "fsdp", 1)
    summed = of_everyone(shared_rows, "dp") / math.sqrt(total_tokens)
    images = summed[1:]
    gram_matrix = of_everyone(
        jnp.dot(images, images.T, precision=lax.Precision.HIGHEST), "fsdp"
    )
    factor = jnp.linalg.cholesky(gram_matrix)
    ortho_basis = math.sqrt(D) * jax.scipy.linalg.solve_triangular(factor, images, lower=True)
    return (ortho_basis.T, summed[0])


def solution(mesh):
    placed = (
        P(("dp", "fsdp"), None),
        P("fsdp"),
        P("fsdp", None),
        P(),
        P(("dp", "fsdp"), None),
        P("fsdp", None),
    )
    return jax.shard_map(
        per_device,
        mesh=mesh,
        in_specs=placed,
        out_specs=(P("fsdp", None), P("fsdp")),
        check_vma=False,
    )
```

time: 222 us -> 167 us (0.75)
  other arithmetic: 66 us -> 8.94 us
  local copies, waits for them, and re-layouts: 24 us -> 16.7 us
  Pallas kernels: 28.6 us -> 35.9 us
  blocking collectives: 88.6 us -> 91.6 us
    mul x3 -> x0, other arithmetic: 45.4 us -> none  [the longest x1 45.4 us: second_order(): unit_keys * along]
    transpose x2 -> x1, local copies, waits for them, and re-layouts: 8.97 us -> 0.18 us  [in_blocks(): return jnp.moveaxis(parts, dim, 0)]
    concatenate x4 -> x3, other arithmetic: 9.03 us -> 0.97 us  [the longest x1 0.7 us: gather_weight(): extra = jnp.concatenate([gain[None, :], directions.T], axis=0)]
    pallas_call x2 -> x3, Pallas kernels: 28.6 us -> 35.9 us  [the longest x1 14.7 us: backward_terms(): pl.pallas_call(backward_kernel, grid=(2 * steps,), in_specs=[pl.BlockSpec...]
    select_n x1 -> x3, other arithmetic: 5.72 us -> 2.1 us  [the longest x1 1.07 us: join_halves(): low = jnp.where(core == 0, a, b)]
    all_to_all x2, blocking collectives: 73 us -> 75.5 us  [copy_for_each(): return lax.all_to_all(copies, axis, split_axis=0, concat_axis=0, tiled=True)]
    unnamed x17 -> x10, local copies, waits for them, and re-layouts: 4.28 us -> 1.85 us
    select_n x0 -> x3, local copies, waits for them, and re-layouts: none -> 2.27 us  [the longest x1 2.25 us: split_halves(): first = jnp.where(core == 0, low, high).reshape(lead, -1)]
  transfers between devices with their start and end apart: 2 -> 2, of which waited for: 1 -> 1; matrix products, arithmetic and copies ran while one was open for 5% -> 11% of each run, Pallas kernels for 0% -> 5%
where the time goes in v2:
time: 167 us
  blocking collectives  91.6 us (55%)
  Pallas kernels  35.9 us (21%)
  local copies, waits for them, and re-layouts  16.7 us (10%)
  other arithmetic  8.94 us (5%)
  waiting for transfers between devices  8.18 us (5%)
  starting transfers between devices  3.86 us (2%)
    all_to_all x2, blocking collectives, copy_for_each(): return lax.all_to_all(copies, axis, split_axis=0, concat_axis=0, tiled=True)  75.5 us
    all_to_all x1, blocking collectives, sum_at_owner(): lax.all_to_all(in_blocks(shard, dim, devices), axis, 0, 0, tiled=True)  16.1 us
    pallas_call x1, Pallas kernels, backward_terms(): pl.pallas_call(backward_kernel, grid=(2 * steps,), in_specs=[pl.BlockSpec...  14.7 us
    pallas_call x1, Pallas kernels, forward_rows(): pl.pallas_call(forward_second_kernel, grid=(width // tile,), in_specs=com...  12.5 us
    pallas_call x1, Pallas kernels, forward_rows(): pl.pallas_call(forward_first_kernel, grid=(width // tile,), in_specs=comm...  8.73 us
    all_to_all x1, waiting for transfers between devices, copy_for_each(): return lax.all_to_all(copies, axis, split_axis=0, concat_axis=0, tiled=True)  8.18 us
    slice x2, local copies, waits for them, and re-layouts, split_halves(): low, high = (blocks[:, :, 0, :], blocks[:, :, 1, :])  4.89 us
    all_to_all x1, starting transfers between devices, copy_for_each(): return lax.all_to_all(copies, axis, split_axis=0, concat_axis=0, tiled=True)  3.85 us
  transfers between devices with their start and end apart: 2, of which 1 were waited for; matrix products, arithmetic and copies ran while one was open for 11% of the time, Pallas kernels for 5%

profile of v2, /device:TPU:0, one launch (start us, length us, event | category | flops | bytes accessed | tf_op | source)
XLA Modules:
  0.0 167.0 jit_solution(9498655247182205550)
XLA Ops:
  0.6 0.0 copy-start
  0.7 0.7 broadcast_in_dim.15
  1.4 0.7 fusion.7
  2.1 0.0 copy-done
  2.1 0.5 broadcast_in_dim.16
  2.6 65.9 %all_to_all.20.w_ref.w1_ref = bf16[32,144,512]{2,1,0:T(8,128)(2,1)} all-to-all(bf16[32,144,512]{2,1,0:T(8,128)(2,1)S(1)} %broadcast_in_dim.16), channel_id=1, replica_groups=mesh['dp'=4,'fsdp'=32] {'fsdp'}, dimensions={0} | all-to-all | bytes 9437184 | tf_op jit(solution)/shard_map/all_to_all | solution.py:31
  68.5 0.0 collective-permute-start
  68.5 3.2 %reshape.110 = bf16[128,32,2,128]{3,2,1,0:T(2,128)(2,1)S(1)} reshape(bf16[128,8192]{1,0:T(8,128)(2,1)} %param.6) | data formatting | bytes 4194304 | tf_op jit(solution)/shard_map/reshape | solution.py:76
  71.8 2.1 %multiply_reduce_fusion = f32[128]{0:T(128)S(1)} fusion(bf16[128,8192]{1,0:T(8,128)(2,1)} %param.6), kind=kLoop, calls=%fused_computation | loop fusion | flops 3145600 | bytes 2097664 | tf_op jit(solution)/shard_map/reduce_sum | solution.py:259
  73.9 0.7 copy.53.rms_ref
  74.6 4.7 %fusion.14 = (bf16[128,32,1,128]{3,2,1,0:T(2,128)(2,1)S(1)}, bf16[128,32,1,128]{3,2,1,0:T(2,128)(2,1)S(1)}) fusion(bf16[128,32,2,128]{3,2,1,0:T(2,128)(2,1)S(1)} %reshape.110), kind=kLoop, calls=%fused_computation.40 | loop fusion | bytes 4194304 | tf_op jit(solution)/shard_map/slice | solution.py:77
  79.3 0.3 broadcast_select_fusion
  79.6 2.2 %copy_bitcast_fusion = (bf16[128,4096]{1,0:T(8,128)(2,1)}, bf16[128,4096]{1,0:T(8,128)(2,1)}) fusion(bf16[16,8,32,128]{3,2,1,0:T(8,128)(2,1)S(1)} %bitcast.50, bf16[16,8,32,128]{3,2,1,0:T(8,128)(2,1)S(1)} %bitcast.51), kind=kLoop, calls=%fused_computation.2 | loop fusion | bytes 4194304 | tf_op jit(solution)/shard_map/jit(_where)/select_n | solution.py:78
  81.8 1.0 convert_bitcast_fusion
  82.8 0.2 reshape.112
  83.0 0.2 fusion.15
  83.2 0.8 fusion.1
  84.0 0.8 copy.72
  84.9 0.8 copy.70
  85.8 0.0 copy-start.1
  85.8 8.7 %shard_map.77.acc_in_ref = f32[1152,512]{1,0:T(8,128)} custom-call(bf16[128,4096]{1,0:T(8,128)(2,1)} %get-tuple-element.12.act_ref.act1_ref, f32[128,1]{1,0:T(8,128)} %copy.53.rms_ref, f32[9,4096]{1,0:T(8,128)} %bitcast.54, bf16[32,144,512]{2,1,0:T(8,128)(2,1)} %all_to_all.20.w_ref.w1_ref), custom_call_target="tpu_custom_call" | custom-call | tf_op jit(solution)/shard_map/pallas_call | solution.py:175
  94.5 0.0 collective-permute-done.w_ref.w2_ref
  94.5 0.0 copy-done.1
  94.5 0.6 tile.2
  95.1 12.5 %shard_map.78.back_ref = bf16[1152,512]{1,0:T(8,128)(2,1)} custom-call(bf16[128,4096]{1,0:T(8,128)(2,1)} %get-tuple-element.13.act_ref.act2_ref, f32[128,1]{1,0:T(8,128)} %copy.53.rms_ref, f32[9,4096]{1,0:T(8,128)} %bitcast.53, bf16[32,144,512]{2,1,0:T(8,128)(2,1)} %collective-permute-done.w_ref.w2_ref, f32[1152,512]{1,0:T(8,128)} %shard_map.77.acc_in_ref, ...), custom_call_target="tpu_custom_call" | custom-call | tf_op jit(solution)/shard_map/pallas_call | solution.py:184
  107.6 14.7 %shard_map.79 = f32[9,8192]{1,0:T(8,128)} custom-call(bf16[1152,512]{1,0:T(8,128)(2,1)} %shard_map.78.back_ref, bf16[32,144,512]{2,1,0:T(8,128)(2,1)} %all_to_all.20.w_ref.w1_ref, bf16[32,144,512]{2,1,0:T(8,128)(2,1)} %collective-permute-done.w_ref.w2_ref, bf16[128,4096]{1,0:T(8,128)(2,1)} %get-tuple-element.12.act_ref.act1_ref, ...), custom_call_target="tpu_custom_call" | custom-call | tf_op jit(solution)/shard_map/pallas_call | solution.py:238
  122.2 1.1 slice_select_fusion.1
  123.3 0.1 copy.73
  123.4 0.1 copy.74
  123.5 0.3 pad_maximum_fusion
  123.7 0.2 reshape_reshape.3
  124.0 0.2 copy.57
  124.2 16.1 %all_to_all.21 = f32[32,9,256]{2,1,0:T(8,128)S(1)} all-to-all(f32[32,9,256]{2,1,0:T(8,128)S(1)} %copy.57), channel_id=1, replica_groups=mesh['dp'=4,'fsdp'=32] {'fsdp'}, dimensions={0} | all-to-all | bytes 589824 | tf_op jit(solution)/shard_map/all_to_all | solution.py:25
  140.3 0.1 reduce_sum.37
  140.3 9.6 %all_to_all.22 = f32[4,9,256]{2,1,0:T(8,128)S(1)} all-to-all(f32[4,9,256]{2,1,0:T(8,128)S(1)} %broadcast_in_dim.17), channel_id=1, replica_groups=mesh['dp'=4,'fsdp'=32] {'dp'}, dimensions={0} | all-to-all | bytes 73728 | tf_op jit(solution)/shard_map/all_to_all | solution.py:31
  150.0 0.1 fusion.9
  150.1 0.7 broadcast_in_dim.18
  150.8 3.9 %all-to-all-start.3 = ((f32[32,8,8]{2,1,0:T(8,128)}), f32[32,8,8]{2,1,0:T(8,128)S(1)}, u32[]{:S(2)}, u32[]{:S(2)}) async-start(f32[32,8,8]{2,1,0:T(8,128)} %broadcast_in_dim.18), calls=%async_computation.3 | async-start | bytes 262144 | tf_op jit(solution)/shard_map/all_to_all | solution.py:31
  154.6 0.6 slice.53
  155.2 8.2 %all-to-all-done.3 = f32[32,8,8]{2,1,0:T(8,128)S(1)} async-done(((f32[32,8,8]{2,1,0:T(8,128)}), f32[32,8,8]{2,1,0:T(8,128)S(1)}, u32[]{:S(2)}, u32[]{:S(2)}) %all-to-all-start.3) | async-done | bytes 8224 | tf_op jit(solution)/shard_map/all_to_all | solution.py:31
  163.4 0.1 copy.60
  163.5 0.7 cholesky.16
  164.2 0.6 compare_reduce_fusion
  164.9 0.6 fusion.11
  165.5 0.6 custom-call.7
  166.2 0.8 convolution_multiply_fusion
  (13 shorter events, 0.2 us)
Async XLA Ops:
  0.6 1.4 copy-start
  68.5 26.0 %collective-permute-start = (bf16[32,144,512]{2,1,0:T(8,128)(2,1)}, bf16[32,144,512]{2,1,0:T(8,128)(2,1)}, u32[]{:S(2)}, u32[]{:S(2)}) collective-permute-start(bf16[32,144,512]{2,1,0:T(8,128)(2,1)} %all_to_all.20.w_ref.w1_ref), channel_id=1, source_target_pairs={{0,32},{32,0},{64,96},{96,64},{1,33},{33,1},{65,97},{97,65},{2,34}... | collective-permute-start | bytes 14155784 | tf_op jit(solution)/shard_map/ppermute | solution.py:68
  85.8 8.7 %copy-start.1 = (f32[128]{0:T(128)S(1)}, f32[128]{0:T(128)}, u32[]{:S(2)}) copy-start(f32[128]{0:T(128)} %param.9) | copy-start | bytes 1540
  150.8 12.6 %all-to-all-start.3 = ((f32[32,8,8]{2,1,0:T(8,128)}), f32[32,8,8]{2,1,0:T(8,128)S(1)}, u32[]{:S(2)}, u32[]{:S(2)}) async-start(f32[32,8,8]{2,1,0:T(8,128)} %broadcast_in_dim.18), calls=%async_computation.3 | async-start | bytes 262144 | tf_op jit(solution)/shard_map/all_to_all | solution.py:31

commit v3 on v2

v3 whole, which is shorter than its diff:
```python
import math

import jax
import jax.numpy as jnp
from jax import lax
from jax.experimental import pallas as pl
from jax.experimental.pallas import tpu as pltpu
from jax.sharding import PartitionSpec as P

D = 8192
HEADS_KV = 4
HEAD_DIM = 128
HALF = 128
FWD_TILE = 1024
BWD_TILE = 1024


def in_blocks(shard, dim, devices):
    shape = shard.shape
    parts = shard.reshape(*shape[:dim], devices, shape[dim] // devices, *shape[dim + 1 :])
    return jnp.moveaxis(parts, dim, 0)


def sum_at_owner(shard, axis, dim):
    devices = lax.axis_size(axis)
    parts = lax.all_to_all(in_blocks(shard, dim, devices), axis, 0, 0, tiled=True)
    return jnp.sum(parts, axis=0)


def copy_for_each(shard, axis):
    copies = jnp.broadcast_to(shard, (lax.axis_size(axis), *shard.shape))
    return lax.all_to_all(copies, axis, split_axis=0, concat_axis=0, tiled=True)


def of_everyone(shard, axis):
    return copy_for_each(shard, axis).sum(axis=0)


def gather_weight(key_weight, gain, directions):
    rows, width = key_weight.shape
    half = rows // 2
    core = lax.axis_index("dp") % 2
    mine = lax.dynamic_slice_in_dim(key_weight, core * half, half, 0)
    extra = jnp.concatenate([gain[None, :], directions.T], axis=0)
    extra = jnp.pad(extra, ((0, 16 - extra.shape[0]), (0, width - rows)))
    piece = jnp.concatenate([mine, extra], axis=0)
    first = copy_for_each(piece, "fsdp")
    dp = lax.axis_size("dp")
    second = lax.ppermute(first, "dp", [(i, i ^ 1) for i in range(dp)])
    extras = first[:, half : half + 1 + directions.shape[1], :rows]
    extras = jnp.transpose(extras, (1, 0, 2)).reshape(extras.shape[1], -1)
    return first, second, extras.astype(jnp.float32)


def middle_rows(acc, cot, key_gain_row, back_ref):
    tokens = cot.shape[0]
    groups = acc.shape[0] // tokens
    weighted_all = cot.astype(jnp.float32) * key_gain_row
    for h in range(HEADS_KV):
        cols = slice(h * HEAD_DIM, (h + 1) * HEAD_DIM)
        key = acc[0:tokens, cols]
        weighted = weighted_all[:, cols]
        key_scale = jnp.sqrt(jnp.sum(key * key, axis=-1, keepdims=True) / HEAD_DIM + 1e-05)
        unit_keys = key / key_scale
        inner_sum = jnp.sum(unit_keys * weighted, axis=-1, keepdims=True)
        grad_keys = (weighted - unit_keys * inner_sum / HEAD_DIM) / key_scale
        back_ref[0:tokens, cols] = grad_keys.astype(back_ref.dtype)
        for j in range(1, groups):
            tangent = acc[j * tokens : (j + 1) * tokens, cols]
            shift_rate = jnp.sum(unit_keys * tangent, axis=-1, keepdims=True) / HEAD_DIM
            unit_change = (tangent - unit_keys * shift_rate) / key_scale
            along = jnp.sum(unit_change * weighted, axis=-1, keepdims=True)
            second = -(unit_change * inner_sum + unit_keys * along) / (
                HEAD_DIM * key_scale
            ) - grad_keys * shift_rate / key_scale
            back_ref[j * tokens : (j + 1) * tokens, cols] = second.astype(back_ref.dtype)


def build_lhs(act_ref, rms_ref, gd_ref, lhs_ref, offset):
    tokens = act_ref.shape[0]
    shard = 2 * HALF
    for g in range(act_ref.shape[1] // shard):
        cols = slice(g * shard + offset, g * shard + offset + HALF)
        normed = act_ref[:, cols].astype(jnp.float32) / rms_ref[...]
        for j in range(gd_ref.shape[0]):
            lhs_ref[j * tokens : (j + 1) * tokens, g * HALF : (g + 1) * HALF] = (
                normed * gd_ref[j : j + 1, cols]
            ).astype(jnp.bfloat16)


def build_for(core_ref, act_ref, rms_ref, gd_ref, lhs_ref, own):
    for core in range(2):
        offset = (core if own else 1 - core) * HALF

        @pl.when(core_ref[0] == core)
        def _():
            build_lhs(act_ref, rms_ref, gd_ref, lhs_ref, offset)


def weight_tile(w_ref):
    shards, rows, width = w_ref.shape
    return w_ref[...].reshape(shards * rows, width)


def forward_first_kernel(core_ref, act_ref, rms_ref, gd_ref, w_ref, out_ref, lhs_ref):
    k = pl.program_id(0)

    @pl.when(k == 0)
    def _():
        out_ref[...] = jnp.zeros_like(out_ref)

    build_for(core_ref, act_ref, rms_ref, gd_ref, lhs_ref, True)
    out_ref[...] += jnp.dot(lhs_ref[...], weight_tile(w_ref), preferred_element_type=jnp.float32)


def forward_second_kernel(
    core_ref, act_ref, rms_ref, gd_ref, w_ref, acc_in_ref, cot_ref, kg_ref, back_ref, lhs_ref, acc_ref
):
    k = pl.program_id(0)

    @pl.when(k == 0)
    def _():
        acc_ref[...] = acc_in_ref[...]

    build_for(core_ref, act_ref, rms_ref, gd_ref, lhs_ref, False)
    acc_ref[...] += jnp.dot(lhs_ref[...], weight_tile(w_ref), preferred_element_type=jnp.float32)

    @pl.when(k == pl.num_programs(0) - 1)
    def _():
        middle_rows(acc_ref[...], cot_ref[...], kg_ref[...], back_ref)


def forward_rows(core, activations, rms, gd, first, second, cot, kg_row):
    tokens, width = activations.shape
    groups = gd.shape[0]
    keys = first.shape[2]
    tile = 2 * FWD_TILE
    shards = tile // (2 * HALF)
    common = [
        pl.BlockSpec((tokens, tile), lambda k, c: (0, k)),
        pl.BlockSpec((tokens, 1), lambda k, c: (0, 0)),
        pl.BlockSpec((groups, tile), lambda k, c: (0, k)),
        pl.BlockSpec((shards, HALF, keys), lambda k, c: (k, 0, 0)),
    ]
    params = pltpu.CompilerParams(dimension_semantics=("arbitrary",))
    acc = pl.pallas_call(
        forward_first_kernel,
        grid_spec=pltpu.PrefetchScalarGridSpec(
            num_scalar_prefetch=1,
            grid=(width // tile,),
            in_specs=common,
            out_specs=pl.BlockSpec((groups * tokens, keys), lambda k, c: (0, 0)),
            scratch_shapes=[pltpu.VMEM((groups * tokens, FWD_TILE), jnp.bfloat16)],
        ),
        out_shape=jax.ShapeDtypeStruct((groups * tokens, keys), jnp.float32),
        compiler_params=params,
    )(core, activations, rms, gd, first)
    return pl.pallas_call(
        forward_second_kernel,
        grid_spec=pltpu.PrefetchScalarGridSpec(
            num_scalar_prefetch=1,
            grid=(width // tile,),
            in_specs=common
            + [
                pl.BlockSpec((groups * tokens, keys), lambda k, c: (0, 0)),
                pl.BlockSpec((tokens, keys), lambda k, c: (0, 0)),
                pl.BlockSpec((1, keys), lambda k, c: (0, 0)),
            ],
            out_specs=pl.BlockSpec((groups * tokens, keys), lambda k, c: (0, 0)),
            scratch_shapes=[
                pltpu.VMEM((groups * tokens, FWD_TILE), jnp.bfloat16),
                pltpu.VMEM((groups * tokens, keys), jnp.float32),
            ],
        ),
        out_shape=jax.ShapeDtypeStruct((groups * tokens, keys), jnp.bfloat16),
        compiler_params=params,
    )(core, activations, rms, gd, second, acc, cot, kg_row)


def backward_kernel(core_ref, back_ref, w1_ref, w2_ref, act_ref, rms_ref, out_ref):
    tokens = act_ref.shape[0]
    groups = out_ref.shape[0]
    shard = 2 * HALF

    def product_of(w_ref):
        return lax.dot_general(
            back_ref[...],
            weight_tile(w_ref),
            (((1,), (1,)), ((), ())),
            preferred_element_type=jnp.float32,
        )

    own = product_of(w1_ref)
    other = product_of(w2_ref)

    def emit(product, offset):
        for g in range(act_ref.shape[1] // shard):
            cols = slice(g * shard + offset, g * shard + offset + HALF)
            normed = act_ref[:, cols].astype(jnp.float32) / rms_ref[...]
            part = product[:, g * HALF : (g + 1) * HALF].reshape(groups, tokens, HALF)
            out_ref[:, cols] = jnp.sum(part * normed[None], axis=1)

    for core in range(2):

        @pl.when(core_ref[0] == core)
        def _():
            emit(own, core * HALF)
            emit(other, (1 - core) * HALF)


def backward_terms(core, back_rows, first, second, activations, rms, groups):
    tokens, width = activations.shape
    keys = first.shape[2]
    tile = 2 * BWD_TILE
    shards = tile // (2 * HALF)
    return pl.pallas_call(
        backward_kernel,
        grid_spec=pltpu.PrefetchScalarGridSpec(
            num_scalar_prefetch=1,
            grid=(width // tile,),
            in_specs=[
                pl.BlockSpec((groups * tokens, keys), lambda k, c: (0, 0)),
                pl.BlockSpec((shards, HALF, keys), lambda k, c: (k, 0, 0)),
                pl.BlockSpec((shards, HALF, keys), lambda k, c: (k, 0, 0)),
                pl.BlockSpec((tokens, tile), lambda k, c: (0, k)),
                pl.BlockSpec((tokens, 1), lambda k, c: (0, 0)),
            ],
            out_specs=pl.BlockSpec((groups, tile), lambda k, c: (0, k)),
        ),
        out_shape=jax.ShapeDtypeStruct((groups, width), jnp.float32),
        compiler_params=pltpu.CompilerParams(dimension_semantics=("arbitrary",)),
    )(core, back_rows, first, second, activations, rms)


def per_device(activations, gain, key_weight, key_gain, cotangent, directions):
    tokens_dev = activations.shape[0]
    total_tokens = tokens_dev * lax.axis_size("dp") * lax.axis_size("fsdp")
    values = activations.astype(jnp.float32)
    rms = jnp.sqrt(jnp.mean(values * values, axis=1, keepdims=True) + 1e-05)
    groups = directions.shape[1] + 1
    core = (lax.axis_index("dp") % 2).astype(jnp.int32).reshape(1)

    first, second, gd = gather_weight(key_weight, gain, directions)
    kg_row = jnp.tile(key_gain, HEADS_KV)[None, :]

    back_rows = forward_rows(core, activations, rms, gd, first, second, cotangent, kg_row)
    partial_terms = backward_terms(core, back_rows, first, second, activations, rms, groups)
    shared_rows = sum_at_owner(partial_terms, "fsdp", 1)
    summed = of_everyone(shared_rows, "dp") / math.sqrt(total_tokens)
    images = summed[1:]
    gram_matrix = of_everyone(
        jnp.dot(images, images.T, precision=lax.Precision.HIGHEST), "fsdp"
    )
    factor = jnp.linalg.cholesky(gram_matrix)
    ortho_basis = math.sqrt(D) * jax.scipy.linalg.solve_triangular(factor, images, lower=True)
    return (ortho_basis.T, summed[0])


def solution(mesh):
    placed = (
        P(("dp", "fsdp"), None),
        P("fsdp"),
        P("fsdp", None),
        P(),
        P(("dp", "fsdp"), None),
        P("fsdp", None),
    )
    return jax.shard_map(
        per_device,
        mesh=mesh,
        in_specs=placed,
        out_specs=(P("fsdp", None), P("fsdp")),
        check_vma=False,
    )
```

time: 167 us -> 163 us (0.976)
  local copies, waits for them, and re-layouts: 16.7 us -> 6.67 us
  Pallas kernels: 35.9 us -> 45.2 us
  other arithmetic: 8.94 us -> 4.98 us
    pallas_call x3, Pallas kernels: 35.9 us -> 45.2 us  [the longest x1 18.4 us: backward_terms(): pl.pallas_call(backward_kernel, grid_spec=pltpu.PrefetchScalarGridSpec(nu...]
    slice x2 -> x0, local copies, waits for them, and re-layouts: 4.89 us -> none  [split_halves(): low, high = (blocks[:, :, 0, :], blocks[:, :, 1, :])]
    reshape x1 -> x2, local copies, waits for them, and re-layouts: 3.23 us -> 0.2 us  [in_blocks(): shard.reshape(*shape[:dim], devices, shape[dim] // devices, *shape[dim +...]
    select_n x3 -> x0, local copies, waits for them, and re-layouts: 2.27 us -> none  [the longest x1 2.25 us: split_halves(): first = jnp.where(core == 0, low, high).reshape(lead, -1)]
    select_n x3 -> x0, other arithmetic: 2.1 us -> none  [the longest x1 1.07 us: join_halves(): low = jnp.where(core == 0, a, b)]
  transfers between devices with their start and end apart: 2 -> 2, of which waited for: 1 -> 1; matrix products, arithmetic and copies ran while one was open for 11% -> 3% of each run, Pallas kernels for 5% -> 7%
where the time goes in v3:
time: 163 us; the launch traced here: 162 us
  blocking collectives  91.8 us (56%)
  Pallas kernels  45.2 us (28%)
  waiting for transfers between devices  8.18 us (5%)
  local copies, waits for them, and re-layouts  6.67 us (4%)
  other arithmetic  4.98 us (3%)
  starting transfers between devices  3.86 us (2%)
    all_to_all x2, blocking collectives, copy_for_each(): return lax.all_to_all(copies, axis, split_axis=0, concat_axis=0, tiled=True)  75.6 us
    pallas_call x1, Pallas kernels, backward_terms(): pl.pallas_call(backward_kernel, grid_spec=pltpu.PrefetchScalarGridSpec(nu...  18.4 us
    all_to_all x1, blocking collectives, sum_at_owner(): lax.all_to_all(in_blocks(shard, dim, devices), axis, 0, 0, tiled=True)  16.1 us
    pallas_call x1, Pallas kernels, forward_rows(): pl.pallas_call(forward_second_kernel, grid_spec=pltpu.PrefetchScalarGridS...  15.3 us
    pallas_call x1, Pallas kernels, forward_rows(): pl.pallas_call(forward_first_kernel, grid_spec=pltpu.PrefetchScalarGridSp...  11.5 us
    all_to_all x1, waiting for transfers between devices, copy_for_each(): return lax.all_to_all(copies, axis, split_axis=0, concat_axis=0, tiled=True)  8.18 us
    all_to_all x1, starting transfers between devices, copy_for_each(): return lax.all_to_all(copies, axis, split_axis=0, concat_axis=0, tiled=True)  3.85 us
  transfers between devices with their start and end apart: 2, of which 1 were waited for; matrix products, arithmetic and copies ran while one was open for 3% of the time, Pallas kernels for 7%

profile of v3, /device:TPU:0, one launch (start us, length us, event | category | flops | bytes accessed | tf_op | source)
XLA Modules:
  0.0 162.4 jit_solution(8475614890872252497)
XLA Ops:
  0.6 0.0 copy-start
  0.7 0.7 broadcast_in_dim.15
  1.4 0.7 fusion.5
  2.1 0.0 copy-done
  2.1 0.5 broadcast_in_dim.16
  2.6 0.0 copy-start.1
  2.6 66.0 %all_to_all.20.w_ref.w1_ref = bf16[32,144,512]{2,1,0:T(8,128)(2,1)} all-to-all(bf16[32,144,512]{2,1,0:T(8,128)(2,1)S(1)} %broadcast_in_dim.16), channel_id=1, replica_groups=mesh['dp'=4,'fsdp'=32] {'fsdp'}, dimensions={0} | all-to-all | bytes 9437184 | tf_op jit(solution)/shard_map/all_to_all | solution.py:32
  68.7 0.0 collective-permute-start
  68.7 0.0 copy-done.1
  68.7 0.5 multiply_reduce_fusion
  69.2 0.7 copy.35.rms_ref
  69.9 1.0 convert_bitcast_fusion
  70.9 0.2 copy.33
  71.2 1.2 copy.44
  72.3 0.0 copy-start.2
  72.3 11.5 %shard_map.77.acc_in_ref = f32[1152,512]{1,0:T(8,128)} custom-call(s32[1]{0:T(128)} %bitcast.core_ref, bf16[128,8192]{1,0:T(8,128)(2,1)} %act_ref.5, f32[128,1]{1,0:T(8,128)} %copy.35.rms_ref, f32[9,8192]{1,0:T(8,128)} %bitcast.27, bf16[32,144,512]{2,1,0:T(8,128)(2,1)} %all_to_all.20.w_ref.w1_ref), custom_call_target="tpu_custom_call" | custom-call | tf_op jit(solution)/shard_map/pallas_call | solution.py:146
  83.9 0.0 collective-permute-done.w_ref.w2_ref
  83.9 0.0 copy-done.2
  83.9 0.6 tile.2
  84.5 15.3 %shard_map.78.back_ref = bf16[1152,512]{1,0:T(8,128)(2,1)} custom-call(s32[1]{0:T(128)} %bitcast.core_ref, bf16[128,8192]{1,0:T(8,128)(2,1)} %act_ref.5, f32[128,1]{1,0:T(8,128)} %copy.35.rms_ref, f32[9,8192]{1,0:T(8,128)} %bitcast.28, bf16[32,144,512]{2,1,0:T(8,128)(2,1)} %collective-permute-done.w_ref.w2_ref, f32[1152,512]{1,0:T(8,128)} %shard_map.77.acc_in_ref, ...), custom_call_target="tpu_custom_call" | custom-call | tf_op jit(solution)/shard_map/pallas_call | solution.py:158
  99.7 18.4 %shard_map.79 = f32[9,8192]{1,0:T(8,128)} custom-call(s32[1]{0:T(128)} %bitcast.core_ref, bf16[1152,512]{1,0:T(8,128)(2,1)} %shard_map.78.back_ref, bf16[32,144,512]{2,1,0:T(8,128)(2,1)} %all_to_all.20.w_ref.w1_ref, bf16[32,144,512]{2,1,0:T(8,128)(2,1)} %collective-permute-done.w_ref.w2_ref, bf16[128,8192]{1,0:T(8,128)(2,1)} %act_ref.5, f32[128,1]{1,0:T(8,128)} %copy.35.rms_ref), custom_call_target="tpu_custom_call" | custom-call | tf_op jit(solution)/shard_map/pallas_call | solution.py:216
  118.1 1.2 copy.45
  119.4 0.2 copy.47
  119.6 16.1 %all_to_all.21 = f32[32,9,256]{2,1,0:T(8,128)S(1)} all-to-all(f32[32,9,256]{2,1,0:T(8,128)S(1)} %bitcast.31), channel_id=1, replica_groups=mesh['dp'=4,'fsdp'=32] {'fsdp'}, dimensions={0} | all-to-all | bytes 589824 | tf_op jit(solution)/shard_map/all_to_all | solution.py:26
  135.7 0.1 reduce_sum.37
  135.8 9.6 %all_to_all.22 = f32[4,9,256]{2,1,0:T(8,128)S(1)} all-to-all(f32[4,9,256]{2,1,0:T(8,128)S(1)} %broadcast_in_dim.17), channel_id=1, replica_groups=mesh['dp'=4,'fsdp'=32] {'dp'}, dimensions={0} | all-to-all | bytes 73728 | tf_op jit(solution)/shard_map/all_to_all | solution.py:32
  145.4 0.1 fusion.7
  145.5 0.7 broadcast_in_dim.18
  146.2 3.9 %all-to-all-start.3 = ((f32[32,8,8]{2,1,0:T(8,128)}), f32[32,8,8]{2,1,0:T(8,128)S(1)}, u32[]{:S(2)}, u32[]{:S(2)}) async-start(f32[32,8,8]{2,1,0:T(8,128)} %broadcast_in_dim.18), calls=%async_computation.3 | async-start | bytes 262144 | tf_op jit(solution)/shard_map/all_to_all | solution.py:32
  150.0 0.6 slice.23
  150.6 8.2 %all-to-all-done.3 = f32[32,8,8]{2,1,0:T(8,128)S(1)} async-done(((f32[32,8,8]{2,1,0:T(8,128)}), f32[32,8,8]{2,1,0:T(8,128)S(1)}, u32[]{:S(2)}, u32[]{:S(2)}) %all-to-all-start.3) | async-done | bytes 8224 | tf_op jit(solution)/shard_map/all_to_all | solution.py:32
  158.8 0.1 copy.40
  158.9 0.7 cholesky.16
  159.6 0.6 compare_reduce_fusion
  160.3 0.6 fusion.9
  160.9 0.6 custom-call.7
  161.6 0.8 convolution_multiply_fusion
  (11 shorter events, 0.2 us)
Async XLA Ops:
  0.6 1.4 copy-start
  2.6 66.0 %copy-start.1 = (bf16[128,8192]{1,0:T(8,128)(2,1)S(1)}, bf16[128,8192]{1,0:T(8,128)(2,1)}, u32[]{:S(2)}) copy-start(bf16[128,8192]{1,0:T(8,128)(2,1)} %act_ref.5) | copy-start | bytes 6291460
  68.7 15.2 %collective-permute-start = (bf16[32,144,512]{2,1,0:T(8,128)(2,1)}, bf16[32,144,512]{2,1,0:T(8,128)(2,1)}, u32[]{:S(2)}, u32[]{:S(2)}) collective-permute-start(bf16[32,144,512]{2,1,0:T(8,128)(2,1)} %all_to_all.20.w_ref.w1_ref), channel_id=1, source_target_pairs={{0,32},{32,0},{64,96},{96,64},{1,33},{33,1},{65,97},{97,65},{2,34}... | collective-permute-start | bytes 14155784 | tf_op jit(solution)/shard_map/ppermute | solution.py:49
  72.3 11.5 %copy-start.2 = (f32[128]{0:T(128)S(1)}, f32[128]{0:T(128)}, u32[]{:S(2)}) copy-start(f32[128]{0:T(128)} %param.9) | copy-start | bytes 1540
  146.2 12.6 %all-to-all-start.3 = ((f32[32,8,8]{2,1,0:T(8,128)}), f32[32,8,8]{2,1,0:T(8,128)S(1)}, u32[]{:S(2)}, u32[]{:S(2)}) async-start(f32[32,8,8]{2,1,0:T(8,128)} %broadcast_in_dim.18), calls=%async_computation.3 | async-start | bytes 262144 | tf_op jit(solution)/shard_map/all_to_all | solution.py:32

commit v4 on v3

--- a/solution.py
+++ b/solution.py
@@ -34,6 +34,15 @@
 
 def of_everyone(shard, axis):
     return copy_for_each(shard, axis).sum(axis=0)
+
+
+def sum_over_pairs(shard, axis):
+    devices = lax.axis_size(axis)
+    step = 1
+    while step < devices:
+        shard = shard + lax.ppermute(shard, axis, [(i, i ^ step) for i in range(devices)])
+        step *= 2
+    return shard
 
 
 def gather_weight(key_weight, gain, directions):
@@ -246,7 +255,7 @@
     back_rows = forward_rows(core, activations, rms, gd, first, second, cotangent, kg_row)
     partial_terms = backward_terms(core, back_rows, first, second, activations, rms, groups)
     shared_rows = sum_at_owner(partial_terms, "fsdp", 1)
-    summed = of_everyone(shared_rows, "dp") / math.sqrt(total_tokens)
+    summed = sum_over_pairs(shared_rows, "dp") / math.sqrt(total_tokens)
     images = summed[1:]
     gram_matrix = of_everyone(
         jnp.dot(images, images.T, precision=lax.Precision.HIGHEST), "fsdp"

time: 163 us -> 160 us (0.982)
  blocking collectives: 91.8 us -> 82.2 us
  waiting for transfers between devices: 8.18 us -> 11.7 us
  starting transfers between devices: 3.86 us -> 7.15 us
    all_to_all x2 -> x1, blocking collectives: 75.6 us -> 66 us  [copy_for_each(): return lax.all_to_all(copies, axis, split_axis=0, concat_axis=0, tiled=True)]
    ppermute x0 -> x2, waiting for transfers between devices: none -> 3.51 us  [sum_over_pairs(): lax.ppermute(shard, axis, [(i, i ^ step) for i in range(devices)])]
    ppermute x0 -> x2, starting transfers between devices: none -> 2.99 us  [sum_over_pairs(): lax.ppermute(shard, axis, [(i, i ^ step) for i in range(devices)])]
  transfers between devices with their start and end apart: 2 -> 4, of which waited for: 1 -> 3; matrix products, arithmetic and copies ran while one was open for 3% -> 3% of each run, Pallas kernels for 7% -> 7%
where the time goes in v4:
time: 160 us
  blocking collectives  82.2 us (51%)
  Pallas kernels  45.2 us (28%)
  waiting for transfers between devices  11.7 us (7%)
  starting transfers between devices  7.15 us (4%)
  local copies, waits for them, and re-layouts  6.66 us (4%)
  other arithmetic  4.98 us (3%)
    all_to_all x1, blocking collectives, copy_for_each(): return lax.all_to_all(copies, axis, split_axis=0, concat_axis=0, tiled=True)  66 us
    pallas_call x1, Pallas kernels, backward_terms(): pl.pallas_call(backward_kernel, grid_spec=pltpu.PrefetchScalarGridSpec(nu...  18.4 us
    all_to_all x1, blocking collectives, sum_at_owner(): lax.all_to_all(in_blocks(shard, dim, devices), axis, 0, 0, tiled=True)  16.1 us
    pallas_call x1, Pallas kernels, forward_rows(): pl.pallas_call(forward_second_kernel, grid_spec=pltpu.PrefetchScalarGridS...  15.3 us
    pallas_call x1, Pallas kernels, forward_rows(): pl.pallas_call(forward_first_kernel, grid_spec=pltpu.PrefetchScalarGridSp...  11.5 us
    all_to_all x1, waiting for transfers between devices, copy_for_each(): return lax.all_to_all(copies, axis, split_axis=0, concat_axis=0, tiled=True)  8.18 us
    all_to_all x1, starting transfers between devices, copy_for_each(): return lax.all_to_all(copies, axis, split_axis=0, concat_axis=0, tiled=True)  4.17 us
    ppermute x2, waiting for transfers between devices, sum_over_pairs(): lax.ppermute(shard, axis, [(i, i ^ step) for i in range(devices)])  3.51 us
  transfers between devices with their start and end apart: 4, of which 3 were waited for; matrix products, arithmetic and copies ran while one was open for 3% of the time, Pallas kernels for 7%

profile of v4, /device:TPU:0, one launch (start us, length us, event | category | flops | bytes accessed | tf_op | source)
XLA Modules:
  0.0 159.6 jit_solution(17390587556390401205)
XLA Ops:
  0.6 0.0 copy-start
  0.7 0.7 broadcast_in_dim.12
  1.4 0.7 fusion.5
  2.1 0.0 copy-done
  2.1 0.5 broadcast_in_dim.13
  2.6 0.0 copy-start.1
  2.6 66.0 %all_to_all.15.w_ref.w1_ref = bf16[32,144,512]{2,1,0:T(8,128)(2,1)} all-to-all(bf16[32,144,512]{2,1,0:T(8,128)(2,1)S(1)} %broadcast_in_dim.13), channel_id=1, replica_groups=mesh['dp'=4,'fsdp'=32] {'fsdp'}, dimensions={0} | all-to-all | bytes 9437184 | tf_op jit(solution)/shard_map/all_to_all | solution.py:32
  68.7 0.0 collective-permute-start
  68.7 0.0 copy-done.1
  68.7 0.5 multiply_reduce_fusion
  69.2 0.7 copy.35.rms_ref
  69.9 1.0 convert_bitcast_fusion
  70.9 0.2 copy.33
  71.2 1.2 copy.42
  72.3 0.0 copy-start.2
  72.3 11.5 %shard_map.77.acc_in_ref = f32[1152,512]{1,0:T(8,128)} custom-call(s32[1]{0:T(128)} %bitcast.core_ref, bf16[128,8192]{1,0:T(8,128)(2,1)} %act_ref.5, f32[128,1]{1,0:T(8,128)} %copy.35.rms_ref, f32[9,8192]{1,0:T(8,128)} %bitcast.27, bf16[32,144,512]{2,1,0:T(8,128)(2,1)} %all_to_all.15.w_ref.w1_ref), custom_call_target="tpu_custom_call" | custom-call | tf_op jit(solution)/shard_map/pallas_call | solution.py:155
  83.9 0.0 collective-permute-done.w_ref.w2_ref
  83.9 0.0 copy-done.2
  83.9 0.6 tile.2
  84.5 15.3 %shard_map.78.back_ref = bf16[1152,512]{1,0:T(8,128)(2,1)} custom-call(s32[1]{0:T(128)} %bitcast.core_ref, bf16[128,8192]{1,0:T(8,128)(2,1)} %act_ref.5, f32[128,1]{1,0:T(8,128)} %copy.35.rms_ref, f32[9,8192]{1,0:T(8,128)} %bitcast.28, bf16[32,144,512]{2,1,0:T(8,128)(2,1)} %collective-permute-done.w_ref.w2_ref, f32[1152,512]{1,0:T(8,128)} %shard_map.77.acc_in_ref, ...), custom_call_target="tpu_custom_call" | custom-call | tf_op jit(solution)/shard_map/pallas_call | solution.py:167
  99.7 18.4 %shard_map.79 = f32[9,8192]{1,0:T(8,128)} custom-call(s32[1]{0:T(128)} %bitcast.core_ref, bf16[1152,512]{1,0:T(8,128)(2,1)} %shard_map.78.back_ref, bf16[32,144,512]{2,1,0:T(8,128)(2,1)} %all_to_all.15.w_ref.w1_ref, bf16[32,144,512]{2,1,0:T(8,128)(2,1)} %collective-permute-done.w_ref.w2_ref, bf16[128,8192]{1,0:T(8,128)(2,1)} %act_ref.5, f32[128,1]{1,0:T(8,128)} %copy.35.rms_ref), custom_call_target="tpu_custom_call" | custom-call | tf_op jit(solution)/shard_map/pallas_call | solution.py:225
  118.1 1.2 copy.43
  119.4 0.2 copy.45
  119.6 16.1 %all_to_all.16 = f32[32,9,256]{2,1,0:T(8,128)S(1)} all-to-all(f32[32,9,256]{2,1,0:T(8,128)S(1)} %bitcast.31), channel_id=1, replica_groups=mesh['dp'=4,'fsdp'=32] {'fsdp'}, dimensions={0} | all-to-all | bytes 589824 | tf_op jit(solution)/shard_map/all_to_all | solution.py:26
  135.7 0.1 reduce_sum.28
  135.7 0.1 collective-permute-start.1
  135.8 1.2 collective-permute-done.1
  137.0 2.9 %collective-permute-start.2 = (f32[9,256]{1,0:T(8,128)S(1)}, f32[9,256]{1,0:T(8,128)S(1)}, u32[]{:S(2)}, u32[]{:S(2)}) collective-permute-start(f32[9,256]{1,0:T(8,128)S(1)} %add.47), channel_id=1, source_target_pairs={{0,64},{32,96},{64,0},{96,32},{1,65},{33,97},{65,1},{97,33},{2,66}... | collective-permute-start | bytes 27656 | tf_op jit(solution)/shard_map/ppermute | solution.py:43
  139.9 2.3 %collective-permute-done.2 = f32[9,256]{1,0:T(8,128)S(1)} collective-permute-done((f32[9,256]{1,0:T(8,128)S(1)}, f32[9,256]{1,0:T(8,128)S(1)}, u32[]{:S(2)}, u32[]{:S(2)}) %collective-permute-start.2) | collective-permute-done | bytes 9248 | tf_op jit(solution)/shard_map/ppermute | solution.py:43
  142.3 0.1 fusion.7
  142.4 0.7 broadcast_in_dim.14
  143.0 4.2 %all-to-all-start.2 = ((f32[32,8,8]{2,1,0:T(8,128)}), f32[32,8,8]{2,1,0:T(8,128)S(1)}, u32[]{:S(2)}, u32[]{:S(2)}) async-start(f32[32,8,8]{2,1,0:T(8,128)} %broadcast_in_dim.14), calls=%async_computation.2 | async-start | bytes 262144 | tf_op jit(solution)/shard_map/all_to_all | solution.py:32
  147.2 0.6 slice.23
  147.8 8.2 %all-to-all-done.2 = f32[32,8,8]{2,1,0:T(8,128)S(1)} async-done(((f32[32,8,8]{2,1,0:T(8,128)}), f32[32,8,8]{2,1,0:T(8,128)S(1)}, u32[]{:S(2)}, u32[]{:S(2)}) %all-to-all-start.2) | async-done | bytes 8224 | tf_op jit(solution)/shard_map/all_to_all | solution.py:32
  156.0 0.1 copy.39
  156.1 0.7 cholesky.16
  156.8 0.6 compare_reduce_fusion
  157.5 0.6 fusion.9
  158.1 0.6 custom-call.7
  158.8 0.8 convolution_multiply_fusion
  (10 shorter events, 0.2 us)
Async XLA Ops:
  0.6 1.4 copy-start
  2.6 66.0 %copy-start.1 = (bf16[128,8192]{1,0:T(8,128)(2,1)S(1)}, bf16[128,8192]{1,0:T(8,128)(2,1)}, u32[]{:S(2)}) copy-start(bf16[128,8192]{1,0:T(8,128)(2,1)} %act_ref.5) | copy-start | bytes 6291460
  68.7 15.2 %collective-permute-start = (bf16[32,144,512]{2,1,0:T(8,128)(2,1)}, bf16[32,144,512]{2,1,0:T(8,128)(2,1)}, u32[]{:S(2)}, u32[]{:S(2)}) collective-permute-start(bf16[32,144,512]{2,1,0:T(8,128)(2,1)} %all_to_all.15.w_ref.w1_ref), channel_id=1, source_target_pairs={{0,32},{32,0},{64,96},{96,64},{1,33},{33,1},{65,97},{97,65},{2,34}... | collective-permute-start | bytes 14155784 | tf_op jit(solution)/shard_map/ppermute | solution.py:58
  72.3 11.5 %copy-start.2 = (f32[128]{0:T(128)S(1)}, f32[128]{0:T(128)}, u32[]{:S(2)}) copy-start(f32[128]{0:T(128)} %param.9) | copy-start | bytes 1540
  135.7 1.3 collective-permute-start.1
  137.0 5.2 %collective-permute-start.2 = (f32[9,256]{1,0:T(8,128)S(1)}, f32[9,256]{1,0:T(8,128)S(1)}, u32[]{:S(2)}, u32[]{:S(2)}) collective-permute-start(f32[9,256]{1,0:T(8,128)S(1)} %add.47), channel_id=1, source_target_pairs={{0,64},{32,96},{64,0},{96,32},{1,65},{33,97},{65,1},{97,33},{2,66}... | collective-permute-start | bytes 27656 | tf_op jit(solution)/shard_map/ppermute | solution.py:43
  143.0 12.9 %all-to-all-start.2 = ((f32[32,8,8]{2,1,0:T(8,128)}), f32[32,8,8]{2,1,0:T(8,128)S(1)}, u32[]{:S(2)}, u32[]{:S(2)}) async-start(f32[32,8,8]{2,1,0:T(8,128)} %broadcast_in_dim.14), calls=%async_computation.2 | async-start | bytes 262144 | tf_op jit(solution)/shard_map/all_to_all | solution.py:32

commit v5 on v4

--- a/solution.py
+++ b/solution.py
@@ -89,21 +89,18 @@
     tokens = act_ref.shape[0]
     shard = 2 * HALF
     for g in range(act_ref.shape[1] // shard):
-        cols = slice(g * shard + offset, g * shard + offset + HALF)
+        cols = pl.ds(pl.multiple_of(g * shard + offset, HALF), HALF)
         normed = act_ref[:, cols].astype(jnp.float32) / rms_ref[...]
+        gd = gd_ref[:, cols]
         for j in range(gd_ref.shape[0]):
             lhs_ref[j * tokens : (j + 1) * tokens, g * HALF : (g + 1) * HALF] = (
-                normed * gd_ref[j : j + 1, cols]
+                normed * gd[j : j + 1, :]
             ).astype(jnp.bfloat16)
 
 
 def build_for(core_ref, act_ref, rms_ref, gd_ref, lhs_ref, own):
-    for core in range(2):
-        offset = (core if own else 1 - core) * HALF
-
-        @pl.when(core_ref[0] == core)
-        def _():
-            build_lhs(act_ref, rms_ref, gd_ref, lhs_ref, offset)
+    core = core_ref[0] if own else 1 - core_ref[0]
+    build_lhs(act_ref, rms_ref, gd_ref, lhs_ref, core * HALF)
 
 
 def weight_tile(w_ref):
@@ -204,17 +201,14 @@
 
     def emit(product, offset):
         for g in range(act_ref.shape[1] // shard):
-            cols = slice(g * shard + offset, g * shard + offset + HALF)
+            cols = pl.ds(pl.multiple_of(g * shard + offset, HALF), HALF)
             normed = act_ref[:, cols].astype(jnp.float32) / rms_ref[...]
             part = product[:, g * HALF : (g + 1) * HALF].reshape(groups, tokens, HALF)
             out_ref[:, cols] = jnp.sum(part * normed[None], axis=1)
 
-    for core in range(2):
-
-        @pl.when(core_ref[0] == core)
-        def _():
-            emit(own, core * HALF)
-            emit(other, (1 - core) * HALF)
+    core = core_ref[0]
+    emit(own, core * HALF)
+    emit(other, (1 - core) * HALF)
 
 
 def backward_terms(core, back_rows, first, second, activations, rms, groups):

time: 160 us -> 150 us (0.938)
  Pallas kernels: 45.2 us -> 35.5 us
    pallas_call x1, Pallas kernels: 18.4 us -> 13.5 us  [backward_terms(): pl.pallas_call(backward_kernel, grid_spec=pltpu.PrefetchScalarGridSpec(nu...]
    pallas_call x1, Pallas kernels: 11.5 us -> 9.1 us  [forward_rows(): pl.pallas_call(forward_first_kernel, grid_spec=pltpu.PrefetchScalarGridSp...]
    pallas_call x1, Pallas kernels: 15.3 us -> 12.9 us  [forward_rows(): pl.pallas_call(forward_second_kernel, grid_spec=pltpu.PrefetchScalarGridS...]
  transfers between devices with their start and end apart: 4 -> 4, of which waited for: 3 -> 3; matrix products, arithmetic and copies ran while one was open for 3% -> 3% of each run, Pallas kernels for 7% -> 6%
where the time goes in v5:
time: 150 us
  blocking collectives  82.1 us (55%)
  Pallas kernels  35.5 us (24%)
  waiting for transfers between devices  11.7 us (8%)
  starting transfers between devices  7.16 us (5%)
  local copies, waits for them, and re-layouts  6.66 us (4%)
  other arithmetic  4.98 us (3%)
    all_to_all x1, blocking collectives, copy_for_each(): return lax.all_to_all(copies, axis, split_axis=0, concat_axis=0, tiled=True)  66 us
    all_to_all x1, blocking collectives, sum_at_owner(): lax.all_to_all(in_blocks(shard, dim, devices), axis, 0, 0, tiled=True)  16.1 us
    pallas_call x1, Pallas kernels, backward_terms(): pl.pallas_call(backward_kernel, grid_spec=pltpu.PrefetchScalarGridSpec(nu...  13.5 us
    pallas_call x1, Pallas kernels, forward_rows(): pl.pallas_call(forward_second_kernel, grid_spec=pltpu.PrefetchScalarGridS...  12.9 us
    pallas_call x1, Pallas kernels, forward_rows(): pl.pallas_call(forward_first_kernel, grid_spec=pltpu.PrefetchScalarGridSp...  9.1 us
    all_to_all x1, waiting for transfers between devices, copy_for_each(): return lax.all_to_all(copies, axis, split_axis=0, concat_axis=0, tiled=True)  8.18 us
    all_to_all x1, starting transfers between devices, copy_for_each(): return lax.all_to_all(copies, axis, split_axis=0, concat_axis=0, tiled=True)  4.17 us
    ppermute x2, waiting for transfers between devices, sum_over_pairs(): lax.ppermute(shard, axis, [(i, i ^ step) for i in range(devices)])  3.5 us
  transfers between devices with their start and end apart: 4, of which 3 were waited for; matrix products, arithmetic and copies ran while one was open for 3% of the time, Pallas kernels for 6%

profile of v5, /device:TPU:0, one launch (start us, length us, event | category | flops | bytes accessed | tf_op | source)
XLA Modules:
  0.0 149.8 jit_solution(12624172223725092128)
XLA Ops:
  0.6 0.0 copy-start
  0.7 0.7 broadcast_in_dim.12
  1.4 0.7 fusion.5
  2.1 0.0 copy-done
  2.1 0.5 broadcast_in_dim.13
  2.6 0.0 copy-start.1
  2.6 66.0 %all_to_all.15.w_ref.w1_ref = bf16[32,144,512]{2,1,0:T(8,128)(2,1)} all-to-all(bf16[32,144,512]{2,1,0:T(8,128)(2,1)S(1)} %broadcast_in_dim.13), channel_id=1, replica_groups=mesh['dp'=4,'fsdp'=32] {'fsdp'}, dimensions={0} | all-to-all | bytes 9437184 | tf_op jit(solution)/shard_map/all_to_all | solution.py:32
  68.7 0.0 collective-permute-start
  68.7 0.0 copy-done.1
  68.7 0.5 multiply_reduce_fusion
  69.2 0.7 copy.35.rms_ref
  69.9 1.0 convert_bitcast_fusion
  70.9 0.2 copy.33
  71.2 1.2 copy.42
  72.3 0.0 copy-start.2
  72.3 9.1 %shard_map.77.acc_in_ref = f32[1152,512]{1,0:T(8,128)} custom-call(s32[1]{0:T(128)} %bitcast.core_ref, bf16[128,8192]{1,0:T(8,128)(2,1)} %act_ref.5, f32[128,1]{1,0:T(8,128)} %copy.35.rms_ref, f32[9,8192]{1,0:T(8,128)} %bitcast.27, bf16[32,144,512]{2,1,0:T(8,128)(2,1)} %all_to_all.15.w_ref.w1_ref), custom_call_target="tpu_custom_call" | custom-call | tf_op jit(solution)/shard_map/pallas_call | solution.py:152
  81.4 0.0 collective-permute-done.w_ref.w2_ref
  81.4 0.0 copy-done.2
  81.4 0.6 tile.2
  82.0 12.9 %shard_map.78.back_ref = bf16[1152,512]{1,0:T(8,128)(2,1)} custom-call(s32[1]{0:T(128)} %bitcast.core_ref, bf16[128,8192]{1,0:T(8,128)(2,1)} %act_ref.5, f32[128,1]{1,0:T(8,128)} %copy.35.rms_ref, f32[9,8192]{1,0:T(8,128)} %bitcast.28, bf16[32,144,512]{2,1,0:T(8,128)(2,1)} %collective-permute-done.w_ref.w2_ref, f32[1152,512]{1,0:T(8,128)} %shard_map.77.acc_in_ref, ...), custom_call_target="tpu_custom_call" | custom-call | tf_op jit(solution)/shard_map/pallas_call | solution.py:164
  94.9 13.5 %shard_map.79 = f32[9,8192]{1,0:T(8,128)} custom-call(s32[1]{0:T(128)} %bitcast.core_ref, bf16[1152,512]{1,0:T(8,128)(2,1)} %shard_map.78.back_ref, bf16[32,144,512]{2,1,0:T(8,128)(2,1)} %all_to_all.15.w_ref.w1_ref, bf16[32,144,512]{2,1,0:T(8,128)(2,1)} %collective-permute-done.w_ref.w2_ref, bf16[128,8192]{1,0:T(8,128)(2,1)} %act_ref.5, f32[128,1]{1,0:T(8,128)} %copy.35.rms_ref), custom_call_target="tpu_custom_call" | custom-call | tf_op jit(solution)/shard_map/pallas_call | solution.py:219
  108.4 1.2 copy.43
  109.6 0.2 copy.45
  109.8 16.1 %all_to_all.16 = f32[32,9,256]{2,1,0:T(8,128)S(1)} all-to-all(f32[32,9,256]{2,1,0:T(8,128)S(1)} %bitcast.31), channel_id=1, replica_groups=mesh['dp'=4,'fsdp'=32] {'fsdp'}, dimensions={0} | all-to-all | bytes 589824 | tf_op jit(solution)/shard_map/all_to_all | solution.py:26
  125.9 0.1 reduce_sum.28
  126.0 0.1 collective-permute-start.1
  126.1 1.2 collective-permute-done.1
  127.2 2.9 %collective-permute-start.2 = (f32[9,256]{1,0:T(8,128)S(1)}, f32[9,256]{1,0:T(8,128)S(1)}, u32[]{:S(2)}, u32[]{:S(2)}) collective-permute-start(f32[9,256]{1,0:T(8,128)S(1)} %add.47), channel_id=1, source_target_pairs={{0,64},{32,96},{64,0},{96,32},{1,65},{33,97},{65,1},{97,33},{2,66}... | collective-permute-start | bytes 27656 | tf_op jit(solution)/shard_map/ppermute | solution.py:43
  130.1 2.3 %collective-permute-done.2 = f32[9,256]{1,0:T(8,128)S(1)} collective-permute-done((f32[9,256]{1,0:T(8,128)S(1)}, f32[9,256]{1,0:T(8,128)S(1)}, u32[]{:S(2)}, u32[]{:S(2)}) %collective-permute-start.2) | collective-permute-done | bytes 9248 | tf_op jit(solution)/shard_map/ppermute | solution.py:43
  132.5 0.1 fusion.7
  132.6 0.7 broadcast_in_dim.14
  133.3 4.2 %all-to-all-start.2 = ((f32[32,8,8]{2,1,0:T(8,128)}), f32[32,8,8]{2,1,0:T(8,128)S(1)}, u32[]{:S(2)}, u32[]{:S(2)}) async-start(f32[32,8,8]{2,1,0:T(8,128)} %broadcast_in_dim.14), calls=%async_computation.2 | async-start | bytes 262144 | tf_op jit(solution)/shard_map/all_to_all | solution.py:32
  137.4 0.6 slice.23
  138.0 8.2 %all-to-all-done.2 = f32[32,8,8]{2,1,0:T(8,128)S(1)} async-done(((f32[32,8,8]{2,1,0:T(8,128)}), f32[32,8,8]{2,1,0:T(8,128)S(1)}, u32[]{:S(2)}, u32[]{:S(2)}) %all-to-all-start.2) | async-done | bytes 8224 | tf_op jit(solution)/shard_map/all_to_all | solution.py:32
  146.2 0.1 copy.39
  146.3 0.7 cholesky.16
  147.1 0.6 compare_reduce_fusion
  147.7 0.6 fusion.9
  148.4 0.6 custom-call.7
  149.0 0.8 convolution_multiply_fusion
  (10 shorter events, 0.2 us)
Async XLA Ops:
  0.6 1.4 copy-start
  2.6 66.0 %copy-start.1 = (bf16[128,8192]{1,0:T(8,128)(2,1)S(1)}, bf16[128,8192]{1,0:T(8,128)(2,1)}, u32[]{:S(2)}) copy-start(bf16[128,8192]{1,0:T(8,128)(2,1)} %act_ref.5) | copy-start | bytes 6291460
  68.7 12.8 %collective-permute-start = (bf16[32,144,512]{2,1,0:T(8,128)(2,1)}, bf16[32,144,512]{2,1,0:T(8,128)(2,1)}, u32[]{:S(2)}, u32[]{:S(2)}) collective-permute-start(bf16[32,144,512]{2,1,0:T(8,128)(2,1)} %all_to_all.15.w_ref.w1_ref), channel_id=1, source_target_pairs={{0,32},{32,0},{64,96},{96,64},{1,33},{33,1},{65,97},{97,65},{2,34}... | collective-permute-start | bytes 14155784 | tf_op jit(solution)/shard_map/ppermute | solution.py:58
  72.3 9.1 %copy-start.2 = (f32[128]{0:T(128)S(1)}, f32[128]{0:T(128)}, u32[]{:S(2)}) copy-start(f32[128]{0:T(128)} %param.9) | copy-start | bytes 1540
  126.0 1.3 collective-permute-start.1
  127.2 5.2 %collective-permute-start.2 = (f32[9,256]{1,0:T(8,128)S(1)}, f32[9,256]{1,0:T(8,128)S(1)}, u32[]{:S(2)}, u32[]{:S(2)}) collective-permute-start(f32[9,256]{1,0:T(8,128)S(1)} %add.47), channel_id=1, source_target_pairs={{0,64},{32,96},{64,0},{96,32},{1,65},{33,97},{65,1},{97,33},{2,66}... | collective-permute-start | bytes 27656 | tf_op jit(solution)/shard_map/ppermute | solution.py:43
  133.3 12.9 %all-to-all-start.2 = ((f32[32,8,8]{2,1,0:T(8,128)}), f32[32,8,8]{2,1,0:T(8,128)S(1)}, u32[]{:S(2)}, u32[]{:S(2)}) async-start(f32[32,8,8]{2,1,0:T(8,128)} %broadcast_in_dim.14), calls=%async_computation.2 | async-start | bytes 262144 | tf_op jit(solution)/shard_map/all_to_all | solution.py:32

commit v6 on v5

--- a/solution.py
+++ b/solution.py
@@ -70,27 +70,29 @@
         key = acc[0:tokens, cols]
         weighted = weighted_all[:, cols]
         key_scale = jnp.sqrt(jnp.sum(key * key, axis=-1, keepdims=True) / HEAD_DIM + 1e-05)
-        unit_keys = key / key_scale
+        inv_scale = 1.0 / key_scale
+        unit_keys = key * inv_scale
         inner_sum = jnp.sum(unit_keys * weighted, axis=-1, keepdims=True)
-        grad_keys = (weighted - unit_keys * inner_sum / HEAD_DIM) / key_scale
+        grad_keys = (weighted - unit_keys * inner_sum / HEAD_DIM) * inv_scale
         back_ref[0:tokens, cols] = grad_keys.astype(back_ref.dtype)
+        inv_outer = 1.0 / (HEAD_DIM * key_scale)
         for j in range(1, groups):
             tangent = acc[j * tokens : (j + 1) * tokens, cols]
             shift_rate = jnp.sum(unit_keys * tangent, axis=-1, keepdims=True) / HEAD_DIM
-            unit_change = (tangent - unit_keys * shift_rate) / key_scale
+            unit_change = (tangent - unit_keys * shift_rate) * inv_scale
             along = jnp.sum(unit_change * weighted, axis=-1, keepdims=True)
-            second = -(unit_change * inner_sum + unit_keys * along) / (
-                HEAD_DIM * key_scale
-            ) - grad_keys * shift_rate / key_scale
+            second = -(unit_change * inner_sum + unit_keys * along) * inv_outer - grad_keys * (
+                shift_rate * inv_scale
+            )
             back_ref[j * tokens : (j + 1) * tokens, cols] = second.astype(back_ref.dtype)
 
 
-def build_lhs(act_ref, rms_ref, gd_ref, lhs_ref, offset):
+def build_lhs(act_ref, inv_rms_ref, gd_ref, lhs_ref, offset):
     tokens = act_ref.shape[0]
     shard = 2 * HALF
     for g in range(act_ref.shape[1] // shard):
         cols = pl.ds(pl.multiple_of(g * shard + offset, HALF), HALF)
-        normed = act_ref[:, cols].astype(jnp.float32) / rms_ref[...]
+        normed = act_ref[:, cols].astype(jnp.float32) * inv_rms_ref[...]
         gd = gd_ref[:, cols]
         for j in range(gd_ref.shape[0]):
             lhs_ref[j * tokens : (j + 1) * tokens, g * HALF : (g + 1) * HALF] = (
@@ -98,9 +100,9 @@
             ).astype(jnp.bfloat16)
 
 
-def build_for(core_ref, act_ref, rms_ref, gd_ref, lhs_ref, own):
+def build_for(core_ref, act_ref, inv_rms_ref, gd_ref, lhs_ref, own):
     core = core_ref[0] if own else 1 - core_ref[0]
-    build_lhs(act_ref, rms_ref, gd_ref, lhs_ref, core * HALF)
+    build_lhs(act_ref, inv_rms_ref, gd_ref, lhs_ref, core * HALF)
 
 
 def weight_tile(w_ref):
@@ -108,19 +110,19 @@
     return w_ref[...].reshape(shards * rows, width)
 
 
-def forward_first_kernel(core_ref, act_ref, rms_ref, gd_ref, w_ref, out_ref, lhs_ref):
+def forward_first_kernel(core_ref, act_ref, inv_rms_ref, gd_ref, w_ref, out_ref, lhs_ref):
     k = pl.program_id(0)
 
     @pl.when(k == 0)
     def _():
         out_ref[...] = jnp.zeros_like(out_ref)
 
-    build_for(core_ref, act_ref, rms_ref, gd_ref, lhs_ref, True)
+    build_for(core_ref, act_ref, inv_rms_ref, gd_ref, lhs_ref, True)
     out_ref[...] += jnp.dot(lhs_ref[...], weight_tile(w_ref), preferred_element_type=jnp.float32)
 
 
 def forward_second_kernel(
-    core_ref, act_ref, rms_ref, gd_ref, w_ref, acc_in_ref, cot_ref, kg_ref, back_ref, lhs_ref, acc_ref
+    core_ref, act_ref, inv_rms_ref, gd_ref, w_ref, acc_in_ref, cot_ref, kg_ref, back_ref, lhs_ref, acc_ref
 ):
     k = pl.program_id(0)
 
@@ -128,7 +130,7 @@
     def _():
         acc_ref[...] = acc_in_ref[...]
 
-    build_for(core_ref, act_ref, rms_ref, gd_ref, lhs_ref, False)
+    build_for(core_ref, act_ref, inv_rms_ref, gd_ref, lhs_ref, False)
     acc_ref[...] += jnp.dot(lhs_ref[...], weight_tile(w_ref), preferred_element_type=jnp.float32)
 
     @pl.when(k == pl.num_programs(0) - 1)
@@ -136,7 +138,7 @@
         middle_rows(acc_ref[...], cot_ref[...], kg_ref[...], back_ref)
 
 
-def forward_rows(core, activations, rms, gd, first, second, cot, kg_row):
+def forward_rows(core, activations, inv_rms, gd, first, second, cot, kg_row):
     tokens, width = activations.shape
     groups = gd.shape[0]
     keys = first.shape[2]
@@ -160,7 +162,7 @@
         ),
         out_shape=jax.ShapeDtypeStruct((groups * tokens, keys), jnp.float32),
         compiler_params=params,
-    )(core, activations, rms, gd, first)
+    )(core, activations, inv_rms, gd, first)
     return pl.pallas_call(
         forward_second_kernel,
         grid_spec=pltpu.PrefetchScalarGridSpec(
@@ -180,10 +182,10 @@
         ),
         out_shape=jax.ShapeDtypeStruct((groups * tokens, keys), jnp.bfloat16),
         compiler_params=params,
-    )(core, activations, rms, gd, second, acc, cot, kg_row)
-
-
-def backward_kernel(core_ref, back_ref, w1_ref, w2_ref, act_ref, rms_ref, out_ref):
+    )(core, activations, inv_rms, gd, second, acc, cot, kg_row)
+
+
+def backward_kernel(core_ref, back_ref, w1_ref, w2_ref, act_ref, inv_rms_ref, out_ref):
     tokens = act_ref.shape[0]
     groups = out_ref.shape[0]
     shard = 2 * HALF
@@ -202,7 +204,7 @@
     def emit(product, offset):
         for g in range(act_ref.shape[1] // shard):
             cols = pl.ds(pl.multiple_of(g * shard + offset, HALF), HALF)
-            normed = act_ref[:, cols].astype(jnp.float32) / rms_ref[...]
+            normed = act_ref[:, cols].astype(jnp.float32) * inv_rms_ref[...]
             part = product[:, g * HALF : (g + 1) * HALF].reshape(groups, tokens, HALF)
             out_ref[:, cols] = jnp.sum(part * normed[None], axis=1)
 
@@ -211,7 +213,7 @@
     emit(other, (1 - core) * HALF)
 
 
-def backward_terms(core, back_rows, first, second, activations, rms, groups):
+def backward_terms(core, back_rows, first, second, activations, inv_rms, groups):
     tokens, width = activations.shape
     keys = first.shape[2]
     tile = 2 * BWD_TILE
@@ -232,22 +234,22 @@
         ),
         out_shape=jax.ShapeDtypeStruct((groups, width), jnp.float32),
         compiler_params=pltpu.CompilerParams(dimension_semantics=("arbitrary",)),
-    )(core, back_rows, first, second, activations, rms)
+    )(core, back_rows, first, second, activations, inv_rms)
 
 
 def per_device(activations, gain, key_weight, key_gain, cotangent, directions):
     tokens_dev = activations.shape[0]
     total_tokens = tokens_dev * lax.axis_size("dp") * lax.axis_size("fsdp")
     values = activations.astype(jnp.float32)
-    rms = jnp.sqrt(jnp.mean(values * values, axis=1, keepdims=True) + 1e-05)
+    inv_rms = 1.0 / jnp.sqrt(jnp.mean(values * values, axis=1, keepdims=True) + 1e-05)
     groups = directions.shape[1] + 1
     core = (lax.axis_index("dp") % 2).astype(jnp.int32).reshape(1)
 
     first, second, gd = gather_weight(key_weight, gain, directions)
     kg_row = jnp.tile(key_gain, HEADS_KV)[None, :]
 
-    back_rows = forward_rows(core, activations, rms, gd, first, second, cotangent, kg_row)
-    partial_terms = backward_terms(core, back_rows, first, second, activations, rms, groups)
+    back_rows = forward_rows(core, activations, inv_rms, gd, first, second, cotangent, kg_row)
+    partial_terms = backward_terms(core, back_rows, first, second, activations, inv_rms, groups)
     shared_rows = sum_at_owner(partial_terms, "fsdp", 1)
     summed = sum_over_pairs(shared_rows, "dp") / math.sqrt(total_tokens)
     images = summed[1:]

time: 150 us -> 150 us (level)
  no operation moved by 1% of the time
where the time goes in v6:
time: 150 us
  blocking collectives  82.1 us (55%)
  Pallas kernels  35.6 us (24%)
  waiting for transfers between devices  11.7 us (8%)
  starting transfers between devices  7.1 us (5%)
  local copies, waits for them, and re-layouts  6.66 us (4%)
  other arithmetic  4.98 us (3%)
    all_to_all x1, blocking collectives, copy_for_each(): return lax.all_to_all(copies, axis, split_axis=0, concat_axis=0, tiled=True)  66 us
    all_to_all x1, blocking collectives, sum_at_owner(): lax.all_to_all(in_blocks(shard, dim, devices), axis, 0, 0, tiled=True)  16.1 us
    pallas_call x1, Pallas kernels, backward_terms(): pl.pallas_call(backward_kernel, grid_spec=pltpu.PrefetchScalarGridSpec(nu...  13.5 us
    pallas_call x1, Pallas kernels, forward_rows(): pl.pallas_call(forward_second_kernel, grid_spec=pltpu.PrefetchScalarGridS...  12.9 us
    pallas_call x1, Pallas kernels, forward_rows(): pl.pallas_call(forward_first_kernel, grid_spec=pltpu.PrefetchScalarGridSp...  9.15 us
    all_to_all x1, waiting for transfers between devices, copy_for_each(): return lax.all_to_all(copies, axis, split_axis=0, concat_axis=0, tiled=True)  8.18 us
    all_to_all x1, starting transfers between devices, copy_for_each(): return lax.all_to_all(copies, axis, split_axis=0, concat_axis=0, tiled=True)  4.11 us
    ppermute x2, waiting for transfers between devices, sum_over_pairs(): lax.ppermute(shard, axis, [(i, i ^ step) for i in range(devices)])  3.51 us
  transfers between devices with their start and end apart: 4, of which 3 were waited for; matrix products, arithmetic and copies ran while one was open for 3% of the time, Pallas kernels for 6%

profile of v6, /device:TPU:0, one launch (start us, length us, event | category | flops | bytes accessed | tf_op | source)
XLA Modules:
  0.0 149.8 jit_solution(15499460253076816619)
XLA Ops:
  0.6 0.0 copy-start
  0.7 0.7 broadcast_in_dim.12
  1.4 0.7 fusion.5
  2.1 0.0 copy-done
  2.1 0.5 broadcast_in_dim.13
  2.6 0.0 copy-start.1
  2.6 66.0 %all_to_all.15.w_ref.w1_ref = bf16[32,144,512]{2,1,0:T(8,128)(2,1)} all-to-all(bf16[32,144,512]{2,1,0:T(8,128)(2,1)S(1)} %broadcast_in_dim.13), channel_id=1, replica_groups=mesh['dp'=4,'fsdp'=32] {'fsdp'}, dimensions={0} | all-to-all | bytes 9437184 | tf_op jit(solution)/shard_map/all_to_all | solution.py:32
  68.7 0.0 collective-permute-start
  68.7 0.0 copy-done.1
  68.7 0.5 multiply_reduce_fusion
  69.2 0.7 copy.35.inv_rms_ref
  69.9 1.0 convert_bitcast_fusion
  70.9 0.2 copy.33
  71.2 1.2 copy.42
  72.3 0.0 copy-start.2
  72.3 9.1 %shard_map.77.acc_in_ref = f32[1152,512]{1,0:T(8,128)} custom-call(s32[1]{0:T(128)} %bitcast.core_ref, bf16[128,8192]{1,0:T(8,128)(2,1)} %act_ref.5, f32[128,1]{1,0:T(8,128)} %copy.35.inv_rms_ref, f32[9,8192]{1,0:T(8,128)} %bitcast.27, bf16[32,144,512]{2,1,0:T(8,128)(2,1)} %all_to_all.15.w_ref.w1_ref), custom_call_target="tpu_custom_call" | custom-call | tf_op jit(solution)/shard_map/pallas_call | solution.py:154
  81.5 0.0 collective-permute-done.w_ref.w2_ref
  81.5 0.0 copy-done.2
  81.5 0.6 tile.2
  82.1 12.9 %shard_map.78.back_ref = bf16[1152,512]{1,0:T(8,128)(2,1)} custom-call(s32[1]{0:T(128)} %bitcast.core_ref, bf16[128,8192]{1,0:T(8,128)(2,1)} %act_ref.5, f32[128,1]{1,0:T(8,128)} %copy.35.inv_rms_ref, f32[9,8192]{1,0:T(8,128)} %bitcast.28, bf16[32,144,512]{2,1,0:T(8,128)(2,1)} %collective-permute-done.w_ref.w2_ref, f32[1152,512]{1,0:T(8,128)} %shard_map.77.acc_in_ref, ...), custom_call_target="tpu_custom_call" | custom-call | tf_op jit(solution)/shard_map/pallas_call | solution.py:166
  95.0 13.5 %shard_map.79 = f32[9,8192]{1,0:T(8,128)} custom-call(s32[1]{0:T(128)} %bitcast.core_ref, bf16[1152,512]{1,0:T(8,128)(2,1)} %shard_map.78.back_ref, bf16[32,144,512]{2,1,0:T(8,128)(2,1)} %all_to_all.15.w_ref.w1_ref, bf16[32,144,512]{2,1,0:T(8,128)(2,1)} %collective-permute-done.w_ref.w2_ref, bf16[128,8192]{1,0:T(8,128)(2,1)} %act_ref.5, ...), custom_call_target="tpu_custom_call" | custom-call | tf_op jit(solution)/shard_map/pallas_call | solution.py:221
  108.5 1.2 copy.43
  109.7 0.2 copy.45
  109.9 16.1 %all_to_all.16 = f32[32,9,256]{2,1,0:T(8,128)S(1)} all-to-all(f32[32,9,256]{2,1,0:T(8,128)S(1)} %bitcast.31), channel_id=1, replica_groups=mesh['dp'=4,'fsdp'=32] {'fsdp'}, dimensions={0} | all-to-all | bytes 589824 | tf_op jit(solution)/shard_map/all_to_all | solution.py:26
  126.0 0.1 reduce_sum.28
  126.1 0.1 collective-permute-start.1
  126.2 1.2 collective-permute-done.1
  127.3 2.9 %collective-permute-start.2 = (f32[9,256]{1,0:T(8,128)S(1)}, f32[9,256]{1,0:T(8,128)S(1)}, u32[]{:S(2)}, u32[]{:S(2)}) collective-permute-start(f32[9,256]{1,0:T(8,128)S(1)} %add.47), channel_id=1, source_target_pairs={{0,64},{32,96},{64,0},{96,32},{1,65},{33,97},{65,1},{97,33},{2,66}... | collective-permute-start | bytes 27656 | tf_op jit(solution)/shard_map/ppermute | solution.py:43
  130.2 2.3 %collective-permute-done.2 = f32[9,256]{1,0:T(8,128)S(1)} collective-permute-done((f32[9,256]{1,0:T(8,128)S(1)}, f32[9,256]{1,0:T(8,128)S(1)}, u32[]{:S(2)}, u32[]{:S(2)}) %collective-permute-start.2) | collective-permute-done | bytes 9248 | tf_op jit(solution)/shard_map/ppermute | solution.py:43
  132.6 0.1 fusion.7
  132.7 0.7 broadcast_in_dim.14
  133.4 4.1 %all-to-all-start.2 = ((f32[32,8,8]{2,1,0:T(8,128)}), f32[32,8,8]{2,1,0:T(8,128)S(1)}, u32[]{:S(2)}, u32[]{:S(2)}) async-start(f32[32,8,8]{2,1,0:T(8,128)} %broadcast_in_dim.14), calls=%async_computation.2 | async-start | bytes 262144 | tf_op jit(solution)/shard_map/all_to_all | solution.py:32
  137.5 0.6 slice.23
  138.1 8.2 %all-to-all-done.2 = f32[32,8,8]{2,1,0:T(8,128)S(1)} async-done(((f32[32,8,8]{2,1,0:T(8,128)}), f32[32,8,8]{2,1,0:T(8,128)S(1)}, u32[]{:S(2)}, u32[]{:S(2)}) %all-to-all-start.2) | async-done | bytes 8224 | tf_op jit(solution)/shard_map/all_to_all | solution.py:32
  146.3 0.1 copy.39
  146.4 0.7 cholesky.16
  147.1 0.6 compare_reduce_fusion
  147.8 0.6 fusion.9
  148.4 0.6 custom-call.7
  149.0 0.8 convolution_multiply_fusion
  (10 shorter events, 0.2 us)
Async XLA Ops:
  0.6 1.4 copy-start
  2.6 66.0 %copy-start.1 = (bf16[128,8192]{1,0:T(8,128)(2,1)S(1)}, bf16[128,8192]{1,0:T(8,128)(2,1)}, u32[]{:S(2)}) copy-start(bf16[128,8192]{1,0:T(8,128)(2,1)} %act_ref.5) | copy-start | bytes 6291460
  68.7 12.8 %collective-permute-start = (bf16[32,144,512]{2,1,0:T(8,128)(2,1)}, bf16[32,144,512]{2,1,0:T(8,128)(2,1)}, u32[]{:S(2)}, u32[]{:S(2)}) collective-permute-start(bf16[32,144,512]{2,1,0:T(8,128)(2,1)} %all_to_all.15.w_ref.w1_ref), channel_id=1, source_target_pairs={{0,32},{32,0},{64,96},{96,64},{1,33},{33,1},{65,97},{97,65},{2,34}... | collective-permute-start | bytes 14155784 | tf_op jit(solution)/shard_map/ppermute | solution.py:58
  72.3 9.2 %copy-start.2 = (f32[128]{0:T(128)S(1)}, f32[128]{0:T(128)}, u32[]{:S(2)}) copy-start(f32[128]{0:T(128)} %param.9) | copy-start | bytes 1540
  126.1 1.3 collective-permute-start.1
  127.3 5.2 %collective-permute-start.2 = (f32[9,256]{1,0:T(8,128)S(1)}, f32[9,256]{1,0:T(8,128)S(1)}, u32[]{:S(2)}, u32[]{:S(2)}) collective-permute-start(f32[9,256]{1,0:T(8,128)S(1)} %add.47), channel_id=1, source_target_pairs={{0,64},{32,96},{64,0},{96,32},{1,65},{33,97},{65,1},{97,33},{2,66}... | collective-permute-start | bytes 27656 | tf_op jit(solution)/shard_map/ppermute | solution.py:43
  133.4 12.9 %all-to-all-start.2 = ((f32[32,8,8]{2,1,0:T(8,128)}), f32[32,8,8]{2,1,0:T(8,128)S(1)}, u32[]{:S(2)}, u32[]{:S(2)}) async-start(f32[32,8,8]{2,1,0:T(8,128)} %broadcast_in_dim.14), calls=%async_computation.2 | async-start | bytes 262144 | tf_op jit(solution)/shard_map/all_to_all | solution.py:32

commit v7 on v5

--- a/solution.py
+++ b/solution.py
@@ -11,6 +11,7 @@
 HEADS_KV = 4
 HEAD_DIM = 128
 HALF = 128
+EXTRA_ROWS = 8
 FWD_TILE = 1024
 BWD_TILE = 1024
 
@@ -51,13 +52,19 @@
     core = lax.axis_index("dp") % 2
     mine = lax.dynamic_slice_in_dim(key_weight, core * half, half, 0)
     extra = jnp.concatenate([gain[None, :], directions.T], axis=0)
-    extra = jnp.pad(extra, ((0, 16 - extra.shape[0]), (0, width - rows)))
+    count = extra.shape[0]
+    per_row = width // rows
+    packed_rows = -(-count // per_row)
+    extra = jnp.pad(extra, ((0, packed_rows * per_row - count), (0, 0)))
+    extra = extra.reshape(packed_rows, width)
+    extra = jnp.pad(extra, ((0, EXTRA_ROWS - packed_rows), (0, 0)))
     piece = jnp.concatenate([mine, extra], axis=0)
     first = copy_for_each(piece, "fsdp")
     dp = lax.axis_size("dp")
     second = lax.ppermute(first, "dp", [(i, i ^ 1) for i in range(dp)])
-    extras = first[:, half : half + 1 + directions.shape[1], :rows]
-    extras = jnp.transpose(extras, (1, 0, 2)).reshape(extras.shape[1], -1)
+    devices = first.shape[0]
+    extras = first[:, half : half + packed_rows, :].reshape(devices, packed_rows * per_row, rows)
+    extras = jnp.transpose(extras[:, :count, :], (1, 0, 2)).reshape(count, -1)
     return first, second, extras.astype(jnp.float32)
 
 

time: 150 us -> 147 us (0.980)
  blocking collectives: 82.1 us -> 79.3 us
    all_to_all x1, blocking collectives: 66 us -> 63.7 us  [copy_for_each(): return lax.all_to_all(copies, axis, split_axis=0, concat_axis=0, tiled=True)]
where the time goes in v7:
time: 147 us
  blocking collectives  79.3 us (54%)
  Pallas kernels  35.4 us (24%)
  waiting for transfers between devices  11.7 us (8%)
  local copies, waits for them, and re-layouts  7.46 us (5%)
  starting transfers between devices  7.14 us (5%)
  other arithmetic  4.02 us (3%)
    all_to_all x1, blocking collectives, copy_for_each(): return lax.all_to_all(copies, axis, split_axis=0, concat_axis=0, tiled=True)  63.7 us
    all_to_all x1, blocking collectives, sum_at_owner(): lax.all_to_all(in_blocks(shard, dim, devices), axis, 0, 0, tiled=True)  15.7 us
    pallas_call x1, Pallas kernels, backward_terms(): pl.pallas_call(backward_kernel, grid_spec=pltpu.PrefetchScalarGridSpec(nu...  13.5 us
    pallas_call x1, Pallas kernels, forward_rows(): pl.pallas_call(forward_second_kernel, grid_spec=pltpu.PrefetchScalarGridS...  12.8 us
    pallas_call x1, Pallas kernels, forward_rows(): pl.pallas_call(forward_first_kernel, grid_spec=pltpu.PrefetchScalarGridSp...  9.13 us
    all_to_all x1, waiting for transfers between devices, copy_for_each(): return lax.all_to_all(copies, axis, split_axis=0, concat_axis=0, tiled=True)  8.18 us
    all_to_all x1, starting transfers between devices, copy_for_each(): return lax.all_to_all(copies, axis, split_axis=0, concat_axis=0, tiled=True)  4.17 us
    ppermute x2, waiting for transfers between devices, sum_over_pairs(): lax.ppermute(shard, axis, [(i, i ^ step) for i in range(devices)])  3.53 us
  transfers between devices with their start and end apart: 4, of which 3 were waited for; matrix products, arithmetic and copies ran while one was open for 3% of the time, Pallas kernels for 6%

profile of v7, /device:TPU:0, one launch (start us, length us, event | category | flops | bytes accessed | tf_op | source)
XLA Modules:
  0.0 146.8 jit_solution(6610674131509242722)
XLA Ops:
  0.6 0.0 copy-start
  0.7 0.7 broadcast_in_dim.12
  1.4 0.7 fusion.4
  2.1 0.0 copy-done
  2.1 0.3 broadcast_in_dim.13
  2.4 0.0 copy-start.1
  2.4 63.7 %all_to_all.15.w_ref.w1_ref = bf16[32,136,512]{2,1,0:T(8,128)(2,1)} all-to-all(bf16[32,136,512]{2,1,0:T(8,128)(2,1)S(1)} %broadcast_in_dim.13), channel_id=1, replica_groups=mesh['dp'=4,'fsdp'=32] {'fsdp'}, dimensions={0} | all-to-all | bytes 8912896 | tf_op jit(solution)/shard_map/all_to_all | solution.py:33
  66.1 0.0 collective-permute-start
  66.1 0.0 copy-done.1
  66.1 0.5 multiply_reduce_fusion
  66.6 0.7 copy.36.rms_ref
  67.3 1.0 slice.26
  68.3 0.1 reshape.53
  68.5 0.2 copy.34
  68.7 1.1 copy.43
  69.8 0.0 copy-start.2
  69.8 9.1 %shard_map.77.acc_in_ref = f32[1152,512]{1,0:T(8,128)} custom-call(s32[1]{0:T(128)} %bitcast.core_ref, bf16[128,8192]{1,0:T(8,128)(2,1)} %act_ref.5, f32[128,1]{1,0:T(8,128)} %copy.36.rms_ref, f32[9,8192]{1,0:T(8,128)} %bitcast.27, bf16[32,136,512]{2,1,0:T(8,128)(2,1)} %all_to_all.15.w_ref.w1_ref), custom_call_target="tpu_custom_call" | custom-call | tf_op jit(solution)/shard_map/pallas_call | solution.py:159
  79.0 0.0 collective-permute-done.w_ref.w2_ref
  79.0 0.0 copy-done.2
  79.0 0.6 tile.2
  79.5 12.8 %shard_map.78.back_ref = bf16[1152,512]{1,0:T(8,128)(2,1)} custom-call(s32[1]{0:T(128)} %bitcast.core_ref, bf16[128,8192]{1,0:T(8,128)(2,1)} %act_ref.5, f32[128,1]{1,0:T(8,128)} %copy.36.rms_ref, f32[9,8192]{1,0:T(8,128)} %bitcast.28, bf16[32,136,512]{2,1,0:T(8,128)(2,1)} %collective-permute-done.w_ref.w2_ref, f32[1152,512]{1,0:T(8,128)} %shard_map.77.acc_in_ref, ...), custom_call_target="tpu_custom_call" | custom-call | tf_op jit(solution)/shard_map/pallas_call | solution.py:171
  92.4 13.5 %shard_map.79 = f32[9,8192]{1,0:T(8,128)} custom-call(s32[1]{0:T(128)} %bitcast.core_ref, bf16[1152,512]{1,0:T(8,128)(2,1)} %shard_map.78.back_ref, bf16[32,136,512]{2,1,0:T(8,128)(2,1)} %all_to_all.15.w_ref.w1_ref, bf16[32,136,512]{2,1,0:T(8,128)(2,1)} %collective-permute-done.w_ref.w2_ref, bf16[128,8192]{1,0:T(8,128)(2,1)} %act_ref.5, f32[128,1]{1,0:T(8,128)} %copy.36.rms_ref), custom_call_target="tpu_custom_call" | custom-call | tf_op jit(solution)/shard_map/pallas_call | solution.py:226
  105.9 1.2 copy.44
  107.1 0.2 copy.46
  107.3 15.7 %all_to_all.16 = f32[32,9,256]{2,1,0:T(8,128)S(1)} all-to-all(f32[32,9,256]{2,1,0:T(8,128)S(1)} %bitcast.31), channel_id=1, replica_groups=mesh['dp'=4,'fsdp'=32] {'fsdp'}, dimensions={0} | all-to-all | bytes 589824 | tf_op jit(solution)/shard_map/all_to_all | solution.py:27
  122.9 0.1 reduce_sum.28
  123.0 0.1 collective-permute-start.1
  123.1 1.2 collective-permute-done.1
  124.3 2.9 %collective-permute-start.2 = (f32[9,256]{1,0:T(8,128)S(1)}, f32[9,256]{1,0:T(8,128)S(1)}, u32[]{:S(2)}, u32[]{:S(2)}) collective-permute-start(f32[9,256]{1,0:T(8,128)S(1)} %add.49), channel_id=1, source_target_pairs={{0,64},{32,96},{64,0},{96,32},{1,65},{33,97},{65,1},{97,33},{2,66}... | collective-permute-start | bytes 27656 | tf_op jit(solution)/shard_map/ppermute | solution.py:44
  127.1 2.4 %collective-permute-done.2 = f32[9,256]{1,0:T(8,128)S(1)} collective-permute-done((f32[9,256]{1,0:T(8,128)S(1)}, f32[9,256]{1,0:T(8,128)S(1)}, u32[]{:S(2)}, u32[]{:S(2)}) %collective-permute-start.2) | collective-permute-done | bytes 9248 | tf_op jit(solution)/shard_map/ppermute | solution.py:44
  129.5 0.1 fusion.6
  129.6 0.7 broadcast_in_dim.14
  130.3 4.2 %all-to-all-start.2 = ((f32[32,8,8]{2,1,0:T(8,128)}), f32[32,8,8]{2,1,0:T(8,128)S(1)}, u32[]{:S(2)}, u32[]{:S(2)}) async-start(f32[32,8,8]{2,1,0:T(8,128)} %broadcast_in_dim.14), calls=%async_computation.2 | async-start | bytes 262144 | tf_op jit(solution)/shard_map/all_to_all | solution.py:33
  134.5 0.6 slice.28
  135.0 8.2 %all-to-all-done.2 = f32[32,8,8]{2,1,0:T(8,128)S(1)} async-done(((f32[32,8,8]{2,1,0:T(8,128)}), f32[32,8,8]{2,1,0:T(8,128)S(1)}, u32[]{:S(2)}, u32[]{:S(2)}) %all-to-all-start.2) | async-done | bytes 8224 | tf_op jit(solution)/shard_map/all_to_all | solution.py:33
  143.3 0.1 copy.40
  143.3 0.7 cholesky.16
  144.1 0.6 compare_reduce_fusion
  144.7 0.6 fusion.8
  145.4 0.6 custom-call.7
  146.0 0.8 convolution_multiply_fusion
  (12 shorter events, 0.3 us)
Async XLA Ops:
  0.6 1.4 copy-start
  2.4 63.7 %copy-start.1 = (bf16[128,8192]{1,0:T(8,128)(2,1)S(1)}, bf16[128,8192]{1,0:T(8,128)(2,1)}, u32[]{:S(2)}) copy-start(bf16[128,8192]{1,0:T(8,128)(2,1)} %act_ref.5) | copy-start | bytes 6291460
  66.1 12.9 %collective-permute-start = (bf16[32,136,512]{2,1,0:T(8,128)(2,1)}, bf16[32,136,512]{2,1,0:T(8,128)(2,1)}, u32[]{:S(2)}, u32[]{:S(2)}) collective-permute-start(bf16[32,136,512]{2,1,0:T(8,128)(2,1)} %all_to_all.15.w_ref.w1_ref), channel_id=1, source_target_pairs={{0,32},{32,0},{64,96},{96,64},{1,33},{33,1},{65,97},{97,65},{2,34}... | collective-permute-start | bytes 13369352 | tf_op jit(solution)/shard_map/ppermute | solution.py:64
  69.8 9.1 %copy-start.2 = (f32[128]{0:T(128)S(1)}, f32[128]{0:T(128)}, u32[]{:S(2)}) copy-start(f32[128]{0:T(128)} %param.9) | copy-start | bytes 1540
  123.0 1.3 collective-permute-start.1
  124.3 5.2 %collective-permute-start.2 = (f32[9,256]{1,0:T(8,128)S(1)}, f32[9,256]{1,0:T(8,128)S(1)}, u32[]{:S(2)}, u32[]{:S(2)}) collective-permute-start(f32[9,256]{1,0:T(8,128)S(1)} %add.49), channel_id=1, source_target_pairs={{0,64},{32,96},{64,0},{96,32},{1,65},{33,97},{65,1},{97,33},{2,66}... | collective-permute-start | bytes 27656 | tf_op jit(solution)/shard_map/ppermute | solution.py:44
  130.3 12.9 %all-to-all-start.2 = ((f32[32,8,8]{2,1,0:T(8,128)}), f32[32,8,8]{2,1,0:T(8,128)S(1)}, u32[]{:S(2)}, u32[]{:S(2)}) async-start(f32[32,8,8]{2,1,0:T(8,128)} %broadcast_in_dim.14), calls=%async_computation.2 | async-start | bytes 262144 | tf_op jit(solution)/shard_map/all_to_all | solution.py:33

commit v8 on v7

--- a/solution.py
+++ b/solution.py
@@ -12,6 +12,7 @@
 HEAD_DIM = 128
 HALF = 128
 EXTRA_ROWS = 8
+SUBS = 2
 FWD_TILE = 1024
 BWD_TILE = 1024
 
@@ -92,22 +93,32 @@
             back_ref[j * tokens : (j + 1) * tokens, cols] = second.astype(back_ref.dtype)
 
 
-def build_lhs(act_ref, rms_ref, gd_ref, lhs_ref, offset):
+def build_lhs(act_ref, rms_ref, gd_ref, lhs_ref, offset, sub, shards):
     tokens = act_ref.shape[0]
     shard = 2 * HALF
-    for g in range(act_ref.shape[1] // shard):
+    for n in range(shards):
+        g = sub * shards + n
         cols = pl.ds(pl.multiple_of(g * shard + offset, HALF), HALF)
         normed = act_ref[:, cols].astype(jnp.float32) / rms_ref[...]
         gd = gd_ref[:, cols]
         for j in range(gd_ref.shape[0]):
-            lhs_ref[j * tokens : (j + 1) * tokens, g * HALF : (g + 1) * HALF] = (
+            lhs_ref[sub, j * tokens : (j + 1) * tokens, n * HALF : (n + 1) * HALF] = (
                 normed * gd[j : j + 1, :]
             ).astype(jnp.bfloat16)
 
 
-def build_for(core_ref, act_ref, rms_ref, gd_ref, lhs_ref, own):
+def forward_step(core_ref, act_ref, rms_ref, gd_ref, w_ref, lhs_ref, own):
     core = core_ref[0] if own else 1 - core_ref[0]
-    build_lhs(act_ref, rms_ref, gd_ref, lhs_ref, core * HALF)
+    subs = lhs_ref.shape[0]
+    shards = w_ref.shape[0] // subs
+    total = None
+    for sub in range(subs):
+        build_lhs(act_ref, rms_ref, gd_ref, lhs_ref, core * HALF, sub, shards)
+        w = w_ref[sub * shards : (sub + 1) * shards]
+        w = w.reshape(shards * w.shape[1], w.shape[2])
+        part = jnp.dot(lhs_ref[sub], w, preferred_element_type=jnp.float32)
+        total = part if total is None else total + part
+    return total
 
 
 def weight_tile(w_ref):
@@ -122,8 +133,7 @@
     def _():
         out_ref[...] = jnp.zeros_like(out_ref)
 
-    build_for(core_ref, act_ref, rms_ref, gd_ref, lhs_ref, True)
-    out_ref[...] += jnp.dot(lhs_ref[...], weight_tile(w_ref), preferred_element_type=jnp.float32)
+    out_ref[...] += forward_step(core_ref, act_ref, rms_ref, gd_ref, w_ref, lhs_ref, True)
 
 
 def forward_second_kernel(
@@ -135,8 +145,7 @@
     def _():
         acc_ref[...] = acc_in_ref[...]
 
-    build_for(core_ref, act_ref, rms_ref, gd_ref, lhs_ref, False)
-    acc_ref[...] += jnp.dot(lhs_ref[...], weight_tile(w_ref), preferred_element_type=jnp.float32)
+    acc_ref[...] += forward_step(core_ref, act_ref, rms_ref, gd_ref, w_ref, lhs_ref, False)
 
     @pl.when(k == pl.num_programs(0) - 1)
     def _():
@@ -163,7 +172,7 @@
             grid=(width // tile,),
             in_specs=common,
             out_specs=pl.BlockSpec((groups * tokens, keys), lambda k, c: (0, 0)),
-            scratch_shapes=[pltpu.VMEM((groups * tokens, FWD_TILE), jnp.bfloat16)],
+            scratch_shapes=[pltpu.VMEM((SUBS, groups * tokens, FWD_TILE // SUBS), jnp.bfloat16)],
         ),
         out_shape=jax.ShapeDtypeStruct((groups * tokens, keys), jnp.float32),
         compiler_params=params,
@@ -181,7 +190,7 @@
             ],
             out_specs=pl.BlockSpec((groups * tokens, keys), lambda k, c: (0, 0)),
             scratch_shapes=[
-                pltpu.VMEM((groups * tokens, FWD_TILE), jnp.bfloat16),
+                pltpu.VMEM((SUBS, groups * tokens, FWD_TILE // SUBS), jnp.bfloat16),
                 pltpu.VMEM((groups * tokens, keys), jnp.float32),
             ],
         ),

time: 147 us -> 147 us (level)
  no operation moved by 1% of the time
where the time goes in v8:
time: 147 us
  blocking collectives  79.3 us (54%)
  Pallas kernels  35.5 us (24%)
  waiting for transfers between devices  11.7 us (8%)
  local copies, waits for them, and re-layouts  7.46 us (5%)
  starting transfers between devices  7.13 us (5%)
  other arithmetic  4.02 us (3%)
    all_to_all x1, blocking collectives, copy_for_each(): return lax.all_to_all(copies, axis, split_axis=0, concat_axis=0, tiled=True)  63.7 us
    all_to_all x1, blocking collectives, sum_at_owner(): lax.all_to_all(in_blocks(shard, dim, devices), axis, 0, 0, tiled=True)  15.6 us
    pallas_call x1, Pallas kernels, backward_terms(): pl.pallas_call(backward_kernel, grid_spec=pltpu.PrefetchScalarGridSpec(nu...  13.5 us
    pallas_call x1, Pallas kernels, forward_rows(): pl.pallas_call(forward_second_kernel, grid_spec=pltpu.PrefetchScalarGridS...  12.8 us
    pallas_call x1, Pallas kernels, forward_rows(): pl.pallas_call(forward_first_kernel, grid_spec=pltpu.PrefetchScalarGridSp...  9.2 us
    all_to_all x1, waiting for transfers between devices, copy_for_each(): return lax.all_to_all(copies, axis, split_axis=0, concat_axis=0, tiled=True)  8.18 us
    all_to_all x1, starting transfers between devices, copy_for_each(): return lax.all_to_all(copies, axis, split_axis=0, concat_axis=0, tiled=True)  4.15 us
    ppermute x2, waiting for transfers between devices, sum_over_pairs(): lax.ppermute(shard, axis, [(i, i ^ step) for i in range(devices)])  3.52 us
  transfers between devices with their start and end apart: 4, of which 3 were waited for; matrix products, arithmetic and copies ran while one was open for 3% of the time, Pallas kernels for 6%

profile of v8, /device:TPU:0, one launch (start us, length us, event | category | flops | bytes accessed | tf_op | source)
XLA Modules:
  0.0 146.9 jit_solution(7279551868730252756)
XLA Ops:
  0.6 0.0 copy-start
  0.7 0.7 broadcast_in_dim.12
  1.4 0.7 fusion.4
  2.1 0.0 copy-done
  2.1 0.3 broadcast_in_dim.13
  2.4 0.0 copy-start.1
  2.4 63.7 %all_to_all.15.w_ref.w1_ref = bf16[32,136,512]{2,1,0:T(8,128)(2,1)} all-to-all(bf16[32,136,512]{2,1,0:T(8,128)(2,1)S(1)} %broadcast_in_dim.13), channel_id=1, replica_groups=mesh['dp'=4,'fsdp'=32] {'fsdp'}, dimensions={0} | all-to-all | bytes 8912896 | tf_op jit(solution)/shard_map/all_to_all | solution.py:34
  66.1 0.0 collective-permute-start
  66.1 0.0 copy-done.1
  66.1 0.5 multiply_reduce_fusion
  66.6 0.7 copy.36.rms_ref
  67.3 1.0 slice.26
  68.3 0.1 reshape.53
  68.5 0.2 copy.34
  68.7 1.1 copy.43
  69.8 0.0 copy-start.2
  69.8 9.2 %shard_map.77.acc_in_ref = f32[1152,512]{1,0:T(8,128)} custom-call(s32[1]{0:T(128)} %bitcast.core_ref, bf16[128,8192]{1,0:T(8,128)(2,1)} %act_ref.5, f32[128,1]{1,0:T(8,128)} %copy.36.rms_ref, f32[9,8192]{1,0:T(8,128)} %bitcast.27, bf16[32,136,512]{2,1,0:T(8,128)(2,1)} %all_to_all.15.w_ref.w1_ref), custom_call_target="tpu_custom_call" | custom-call | tf_op jit(solution)/shard_map/pallas_call | solution.py:168
  79.0 0.0 collective-permute-done.w_ref.w2_ref
  79.0 0.0 copy-done.2
  79.0 0.6 tile.2
  79.6 12.8 %shard_map.78.back_ref = bf16[1152,512]{1,0:T(8,128)(2,1)} custom-call(s32[1]{0:T(128)} %bitcast.core_ref, bf16[128,8192]{1,0:T(8,128)(2,1)} %act_ref.5, f32[128,1]{1,0:T(8,128)} %copy.36.rms_ref, f32[9,8192]{1,0:T(8,128)} %bitcast.28, bf16[32,136,512]{2,1,0:T(8,128)(2,1)} %collective-permute-done.w_ref.w2_ref, f32[1152,512]{1,0:T(8,128)} %shard_map.77.acc_in_ref, ...), custom_call_target="tpu_custom_call" | custom-call | tf_op jit(solution)/shard_map/pallas_call | solution.py:180
  92.5 13.5 %shard_map.79 = f32[9,8192]{1,0:T(8,128)} custom-call(s32[1]{0:T(128)} %bitcast.core_ref, bf16[1152,512]{1,0:T(8,128)(2,1)} %shard_map.78.back_ref, bf16[32,136,512]{2,1,0:T(8,128)(2,1)} %all_to_all.15.w_ref.w1_ref, bf16[32,136,512]{2,1,0:T(8,128)(2,1)} %collective-permute-done.w_ref.w2_ref, bf16[128,8192]{1,0:T(8,128)(2,1)} %act_ref.5, f32[128,1]{1,0:T(8,128)} %copy.36.rms_ref), custom_call_target="tpu_custom_call" | custom-call | tf_op jit(solution)/shard_map/pallas_call | solution.py:235
  106.0 1.2 copy.44
  107.2 0.2 copy.46
  107.4 15.6 %all_to_all.16 = f32[32,9,256]{2,1,0:T(8,128)S(1)} all-to-all(f32[32,9,256]{2,1,0:T(8,128)S(1)} %bitcast.31), channel_id=1, replica_groups=mesh['dp'=4,'fsdp'=32] {'fsdp'}, dimensions={0} | all-to-all | bytes 589824 | tf_op jit(solution)/shard_map/all_to_all | solution.py:28
  123.0 0.1 reduce_sum.28
  123.1 0.1 collective-permute-start.1
  123.2 1.2 collective-permute-done.1
  124.3 2.9 %collective-permute-start.2 = (f32[9,256]{1,0:T(8,128)S(1)}, f32[9,256]{1,0:T(8,128)S(1)}, u32[]{:S(2)}, u32[]{:S(2)}) collective-permute-start(f32[9,256]{1,0:T(8,128)S(1)} %add.49), channel_id=1, source_target_pairs={{0,64},{32,96},{64,0},{96,32},{1,65},{33,97},{65,1},{97,33},{2,66}... | collective-permute-start | bytes 27656 | tf_op jit(solution)/shard_map/ppermute | solution.py:45
  127.2 2.3 %collective-permute-done.2 = f32[9,256]{1,0:T(8,128)S(1)} collective-permute-done((f32[9,256]{1,0:T(8,128)S(1)}, f32[9,256]{1,0:T(8,128)S(1)}, u32[]{:S(2)}, u32[]{:S(2)}) %collective-permute-start.2) | collective-permute-done | bytes 9248 | tf_op jit(solution)/shard_map/ppermute | solution.py:45
  129.6 0.1 fusion.6
  129.7 0.7 broadcast_in_dim.14
  130.4 4.1 %all-to-all-start.2 = ((f32[32,8,8]{2,1,0:T(8,128)}), f32[32,8,8]{2,1,0:T(8,128)S(1)}, u32[]{:S(2)}, u32[]{:S(2)}) async-start(f32[32,8,8]{2,1,0:T(8,128)} %broadcast_in_dim.14), calls=%async_computation.2 | async-start | bytes 262144 | tf_op jit(solution)/shard_map/all_to_all | solution.py:34
  134.5 0.6 slice.28
  135.1 8.2 %all-to-all-done.2 = f32[32,8,8]{2,1,0:T(8,128)S(1)} async-done(((f32[32,8,8]{2,1,0:T(8,128)}), f32[32,8,8]{2,1,0:T(8,128)S(1)}, u32[]{:S(2)}, u32[]{:S(2)}) %all-to-all-start.2) | async-done | bytes 8224 | tf_op jit(solution)/shard_map/all_to_all | solution.py:34
  143.3 0.1 copy.40
  143.4 0.7 cholesky.16
  144.1 0.6 compare_reduce_fusion
  144.8 0.6 fusion.8
  145.4 0.6 custom-call.7
  146.1 0.8 convolution_multiply_fusion
  (12 shorter events, 0.3 us)
Async XLA Ops:
  0.6 1.4 copy-start
  2.4 63.7 %copy-start.1 = (bf16[128,8192]{1,0:T(8,128)(2,1)S(1)}, bf16[128,8192]{1,0:T(8,128)(2,1)}, u32[]{:S(2)}) copy-start(bf16[128,8192]{1,0:T(8,128)(2,1)} %act_ref.5) | copy-start | bytes 6291460
  66.1 12.9 %collective-permute-start = (bf16[32,136,512]{2,1,0:T(8,128)(2,1)}, bf16[32,136,512]{2,1,0:T(8,128)(2,1)}, u32[]{:S(2)}, u32[]{:S(2)}) collective-permute-start(bf16[32,136,512]{2,1,0:T(8,128)(2,1)} %all_to_all.15.w_ref.w1_ref), channel_id=1, source_target_pairs={{0,32},{32,0},{64,96},{96,64},{1,33},{33,1},{65,97},{97,65},{2,34}... | collective-permute-start | bytes 13369352 | tf_op jit(solution)/shard_map/ppermute | solution.py:65
  69.8 9.2 %copy-start.2 = (f32[128]{0:T(128)S(1)}, f32[128]{0:T(128)}, u32[]{:S(2)}) copy-start(f32[128]{0:T(128)} %param.9) | copy-start | bytes 1540
  123.1 1.3 collective-permute-start.1
  124.3 5.2 %collective-permute-start.2 = (f32[9,256]{1,0:T(8,128)S(1)}, f32[9,256]{1,0:T(8,128)S(1)}, u32[]{:S(2)}, u32[]{:S(2)}) collective-permute-start(f32[9,256]{1,0:T(8,128)S(1)} %add.49), channel_id=1, source_target_pairs={{0,64},{32,96},{64,0},{96,32},{1,65},{33,97},{65,1},{97,33},{2,66}... | collective-permute-start | bytes 27656 | tf_op jit(solution)/shard_map/ppermute | solution.py:45
  130.4 12.9 %all-to-all-start.2 = ((f32[32,8,8]{2,1,0:T(8,128)}), f32[32,8,8]{2,1,0:T(8,128)S(1)}, u32[]{:S(2)}, u32[]{:S(2)}) async-start(f32[32,8,8]{2,1,0:T(8,128)} %broadcast_in_dim.14), calls=%async_computation.2 | async-start | bytes 262144 | tf_op jit(solution)/shard_map/all_to_all | solution.py:34

commit v9 on v7

--- a/solution.py
+++ b/solution.py
@@ -12,6 +12,7 @@
 HEAD_DIM = 128
 HALF = 128
 EXTRA_ROWS = 8
+GROUPS = 9
 FWD_TILE = 1024
 BWD_TILE = 1024
 
@@ -62,10 +63,7 @@
     first = copy_for_each(piece, "fsdp")
     dp = lax.axis_size("dp")
     second = lax.ppermute(first, "dp", [(i, i ^ 1) for i in range(dp)])
-    devices = first.shape[0]
-    extras = first[:, half : half + packed_rows, :].reshape(devices, packed_rows * per_row, rows)
-    extras = jnp.transpose(extras[:, :count, :], (1, 0, 2)).reshape(count, -1)
-    return first, second, extras.astype(jnp.float32)
+    return first, second
 
 
 def middle_rows(acc, cot, key_gain_row, back_ref):
@@ -92,22 +90,24 @@
             back_ref[j * tokens : (j + 1) * tokens, cols] = second.astype(back_ref.dtype)
 
 
-def build_lhs(act_ref, rms_ref, gd_ref, lhs_ref, offset):
+def build_lhs(act_ref, rms_ref, ext_ref, lhs_ref, offset):
     tokens = act_ref.shape[0]
     shard = 2 * HALF
+    per_row = ext_ref.shape[2] // shard
     for g in range(act_ref.shape[1] // shard):
         cols = pl.ds(pl.multiple_of(g * shard + offset, HALF), HALF)
         normed = act_ref[:, cols].astype(jnp.float32) / rms_ref[...]
-        gd = gd_ref[:, cols]
-        for j in range(gd_ref.shape[0]):
+        for j in range(GROUPS):
+            lanes = pl.ds(pl.multiple_of((j % per_row) * shard + offset, HALF), HALF)
+            scale = ext_ref[g, pl.ds(j // per_row, 1), lanes].astype(jnp.float32)
             lhs_ref[j * tokens : (j + 1) * tokens, g * HALF : (g + 1) * HALF] = (
-                normed * gd[j : j + 1, :]
+                normed * scale
             ).astype(jnp.bfloat16)
 
 
-def build_for(core_ref, act_ref, rms_ref, gd_ref, lhs_ref, own):
+def build_for(core_ref, act_ref, rms_ref, ext_ref, lhs_ref, own):
     core = core_ref[0] if own else 1 - core_ref[0]
-    build_lhs(act_ref, rms_ref, gd_ref, lhs_ref, core * HALF)
+    build_lhs(act_ref, rms_ref, ext_ref, lhs_ref, core * HALF)
 
 
 def weight_tile(w_ref):
@@ -143,16 +143,16 @@
         middle_rows(acc_ref[...], cot_ref[...], kg_ref[...], back_ref)
 
 
-def forward_rows(core, activations, rms, gd, first, second, cot, kg_row):
+def forward_rows(core, activations, rms, first, second, cot, kg_row):
     tokens, width = activations.shape
-    groups = gd.shape[0]
+    groups = GROUPS
     keys = first.shape[2]
     tile = 2 * FWD_TILE
     shards = tile // (2 * HALF)
     common = [
         pl.BlockSpec((tokens, tile), lambda k, c: (0, k)),
         pl.BlockSpec((tokens, 1), lambda k, c: (0, 0)),
-        pl.BlockSpec((groups, tile), lambda k, c: (0, k)),
+        pl.BlockSpec((shards, EXTRA_ROWS, keys), lambda k, c: (k, HALF // EXTRA_ROWS, 0)),
         pl.BlockSpec((shards, HALF, keys), lambda k, c: (k, 0, 0)),
     ]
     params = pltpu.CompilerParams(dimension_semantics=("arbitrary",))
@@ -167,7 +167,7 @@
         ),
         out_shape=jax.ShapeDtypeStruct((groups * tokens, keys), jnp.float32),
         compiler_params=params,
-    )(core, activations, rms, gd, first)
+    )(core, activations, rms, first, first)
     return pl.pallas_call(
         forward_second_kernel,
         grid_spec=pltpu.PrefetchScalarGridSpec(
@@ -187,12 +187,12 @@
         ),
         out_shape=jax.ShapeDtypeStruct((groups * tokens, keys), jnp.bfloat16),
         compiler_params=params,
-    )(core, activations, rms, gd, second, acc, cot, kg_row)
+    )(core, activations, rms, first, second, acc, cot, kg_row)
 
 
 def backward_kernel(core_ref, back_ref, w1_ref, w2_ref, act_ref, rms_ref, out_ref):
     tokens = act_ref.shape[0]
-    groups = out_ref.shape[0]
+    groups = out_ref.shape[1]
     shard = 2 * HALF
 
     def product_of(w_ref):
@@ -211,7 +211,9 @@
             cols = pl.ds(pl.multiple_of(g * shard + offset, HALF), HALF)
             normed = act_ref[:, cols].astype(jnp.float32) / rms_ref[...]
             part = product[:, g * HALF : (g + 1) * HALF].reshape(groups, tokens, HALF)
-            out_ref[:, cols] = jnp.sum(part * normed[None], axis=1)
+            out_ref[g, :, pl.ds(pl.multiple_of(offset, HALF), HALF)] = jnp.sum(
+                part * normed[None], axis=1
+            )
 
     core = core_ref[0]
     emit(own, core * HALF)
@@ -235,9 +237,9 @@
                 pl.BlockSpec((tokens, tile), lambda k, c: (0, k)),
                 pl.BlockSpec((tokens, 1), lambda k, c: (0, 0)),
             ],
-            out_specs=pl.BlockSpec((groups, tile), lambda k, c: (0, k)),
+            out_specs=pl.BlockSpec((shards, groups, 2 * HALF), lambda k, c: (k, 0, 0)),
         ),
-        out_shape=jax.ShapeDtypeStruct((groups, width), jnp.float32),
+        out_shape=jax.ShapeDtypeStruct((width // (2 * HALF), groups, 2 * HALF), jnp.float32),
         compiler_params=pltpu.CompilerParams(dimension_semantics=("arbitrary",)),
     )(core, back_rows, first, second, activations, rms)
 
@@ -250,12 +252,12 @@
     groups = directions.shape[1] + 1
     core = (lax.axis_index("dp") % 2).astype(jnp.int32).reshape(1)
 
-    first, second, gd = gather_weight(key_weight, gain, directions)
+    first, second = gather_weight(key_weight, gain, directions)
     kg_row = jnp.tile(key_gain, HEADS_KV)[None, :]
 
-    back_rows = forward_rows(core, activations, rms, gd, first, second, cotangent, kg_row)
+    back_rows = forward_rows(core, activations, rms, first, second, cotangent, kg_row)
     partial_terms = backward_terms(core, back_rows, first, second, activations, rms, groups)
-    shared_rows = sum_at_owner(partial_terms, "fsdp", 1)
+    shared_rows = jnp.sum(lax.all_to_all(partial_terms, "fsdp", 0, 0, tiled=True), axis=0)
     summed = sum_over_pairs(shared_rows, "dp") / math.sqrt(total_tokens)
     images = summed[1:]
     gram_matrix = of_everyone(

time: 147 us -> 144 us (0.980)
  local copies, waits for them, and re-layouts: 7.46 us -> 3.66 us
    unnamed x9 -> x6, local copies, waits for them, and re-layouts: 2.38 us -> 0.02 us
  transfers between devices with their start and end apart: 4 -> 4, of which waited for: 3 -> 3; matrix products, arithmetic and copies ran while one was open for 3% -> 1% of each run, Pallas kernels for 6% -> 6%
where the time goes in v9:
time: 144 us
  blocking collectives  79.8 us (55%)
  Pallas kernels  35.4 us (25%)
  waiting for transfers between devices  11.7 us (8%)
  starting transfers between devices  7.36 us (5%)
  other arithmetic  3.97 us (3%)
  local copies, waits for them, and re-layouts  3.66 us (3%)
    all_to_all x1, blocking collectives, copy_for_each(): return lax.all_to_all(copies, axis, split_axis=0, concat_axis=0, tiled=True)  63.7 us
    all_to_all x1, blocking collectives, per_device(): lax.all_to_all(partial_terms, 'fsdp', 0, 0, tiled=True)  16.1 us
    pallas_call x1, Pallas kernels, backward_terms(): pl.pallas_call(backward_kernel, grid_spec=pltpu.PrefetchScalarGridSpec(nu...  13.5 us
    pallas_call x1, Pallas kernels, forward_rows(): pl.pallas_call(forward_second_kernel, grid_spec=pltpu.PrefetchScalarGridS...  12.8 us
    pallas_call x1, Pallas kernels, forward_rows(): pl.pallas_call(forward_first_kernel, grid_spec=pltpu.PrefetchScalarGridSp...  9.14 us
    all_to_all x1, waiting for transfers between devices, copy_for_each(): return lax.all_to_all(copies, axis, split_axis=0, concat_axis=0, tiled=True)  8.18 us
    all_to_all x1, starting transfers between devices, copy_for_each(): return lax.all_to_all(copies, axis, split_axis=0, concat_axis=0, tiled=True)  4.35 us
    ppermute x2, waiting for transfers between devices, sum_over_pairs(): lax.ppermute(shard, axis, [(i, i ^ step) for i in range(devices)])  3.5 us
  transfers between devices with their start and end apart: 4, of which 3 were waited for; matrix products, arithmetic and copies ran while one was open for 1% of the time, Pallas kernels for 6%

profile of v9, /device:TPU:0, one launch (start us, length us, event | category | flops | bytes accessed | tf_op | source)
XLA Modules:
  0.0 143.5 jit_solution(9105001462049170784)
XLA Ops:
  0.6 0.0 copy-start
  0.7 0.7 broadcast_in_dim.12
  1.4 0.7 fusion.4
  2.1 0.0 copy-done
  2.1 0.3 broadcast_in_dim.13
  2.4 0.0 copy-start.1
  2.4 63.7 %all_to_all.15.gd_ref.w_ref.w1_ref = bf16[32,136,512]{2,1,0:T(8,128)(2,1)} all-to-all(bf16[32,136,512]{2,1,0:T(8,128)(2,1)S(1)} %broadcast_in_dim.13), channel_id=1, replica_groups=mesh['dp'=4,'fsdp'=32] {'fsdp'}, dimensions={0} | all-to-all | bytes 8912896 | tf_op jit(solution)/shard_map/all_to_all | solution.py:34
  66.1 0.0 collective-permute-start
  66.1 0.0 copy-done.1
  66.1 0.5 multiply_reduce_fusion
  66.6 0.7 copy.19.rms_ref
  67.3 0.0 copy-start.2
  67.3 9.1 %shard_map.77.acc_in_ref = f32[1152,512]{1,0:T(8,128)} custom-call(s32[1]{0:T(128)} %bitcast.core_ref, bf16[128,8192]{1,0:T(8,128)(2,1)} %act_ref.5, f32[128,1]{1,0:T(8,128)} %copy.19.rms_ref, bf16[32,136,512]{2,1,0:T(8,128)(2,1)} %all_to_all.15.gd_ref.w_ref.w1_ref, bf16[32,136,512]{2,1,0:T(8,128)(2,1)} %all_to_all.15.gd_ref.w_ref.w1_ref), custom_call_target="tpu_custom_call" | custom-call | tf_op jit(solution)/shard_map/pallas_call | solution.py:159
  76.5 0.0 collective-permute-done.w_ref.w2_ref
  76.5 0.0 copy-done.2
  76.5 0.6 tile.2
  77.1 12.8 %shard_map.78.back_ref = bf16[1152,512]{1,0:T(8,128)(2,1)} custom-call(s32[1]{0:T(128)} %bitcast.core_ref, bf16[128,8192]{1,0:T(8,128)(2,1)} %act_ref.5, f32[128,1]{1,0:T(8,128)} %copy.19.rms_ref, bf16[32,136,512]{2,1,0:T(8,128)(2,1)} %all_to_all.15.gd_ref.w_ref.w1_ref, bf16[32,136,512]{2,1,0:T(8,128)(2,1)} %collective-permute-done.w_ref.w2_ref, ...), custom_call_target="tpu_custom_call" | custom-call | tf_op jit(solution)/shard_map/pallas_call | solution.py:171
  89.9 13.5 %shard_map.79 = f32[32,9,256]{2,1,0:T(8,128)} custom-call(s32[1]{0:T(128)} %bitcast.core_ref, bf16[1152,512]{1,0:T(8,128)(2,1)} %shard_map.78.back_ref, bf16[32,136,512]{2,1,0:T(8,128)(2,1)} %all_to_all.15.gd_ref.w_ref.w1_ref, bf16[32,136,512]{2,1,0:T(8,128)(2,1)} %collective-permute-done.w_ref.w2_ref, bf16[128,8192]{1,0:T(8,128)(2,1)} %act_ref.5, ...), custom_call_target="tpu_custom_call" | custom-call | tf_op jit(solution)/shard_map/pallas_call | solution.py:228
  103.4 16.1 %all_to_all.16 = f32[32,9,256]{2,1,0:T(8,128)S(1)} all-to-all(f32[32,9,256]{2,1,0:T(8,128)} %shard_map.79), channel_id=1, replica_groups=mesh['dp'=4,'fsdp'=32] {'fsdp'}, dimensions={0} | all-to-all | bytes 589824 | tf_op jit(solution)/shard_map/all_to_all | solution.py:260
  119.5 0.1 reduce_sum.28
  119.5 0.1 collective-permute-start.1
  119.6 1.2 collective-permute-done.1
  120.8 2.9 %collective-permute-start.2 = (f32[9,256]{1,0:T(8,128)S(1)}, f32[9,256]{1,0:T(8,128)S(1)}, u32[]{:S(2)}, u32[]{:S(2)}) collective-permute-start(f32[9,256]{1,0:T(8,128)S(1)} %add.49), channel_id=1, source_target_pairs={{0,64},{32,96},{64,0},{96,32},{1,65},{33,97},{65,1},{97,33},{2,66}... | collective-permute-start | bytes 27656 | tf_op jit(solution)/shard_map/ppermute | solution.py:45
  123.7 2.3 %collective-permute-done.2 = f32[9,256]{1,0:T(8,128)S(1)} collective-permute-done((f32[9,256]{1,0:T(8,128)S(1)}, f32[9,256]{1,0:T(8,128)S(1)}, u32[]{:S(2)}, u32[]{:S(2)}) %collective-permute-start.2) | collective-permute-done | bytes 9248 | tf_op jit(solution)/shard_map/ppermute | solution.py:45
  126.0 0.1 fusion.6
  126.1 0.7 broadcast_in_dim.14
  126.8 4.4 %all-to-all-start.2 = ((f32[32,8,8]{2,1,0:T(8,128)}), f32[32,8,8]{2,1,0:T(8,128)S(1)}, u32[]{:S(2)}, u32[]{:S(2)}) async-start(f32[32,8,8]{2,1,0:T(8,128)} %broadcast_in_dim.14), calls=%async_computation.2 | async-start | bytes 262144 | tf_op jit(solution)/shard_map/all_to_all | solution.py:34
  131.2 0.6 slice.18
  131.7 8.2 %all-to-all-done.2 = f32[32,8,8]{2,1,0:T(8,128)S(1)} async-done(((f32[32,8,8]{2,1,0:T(8,128)}), f32[32,8,8]{2,1,0:T(8,128)S(1)}, u32[]{:S(2)}, u32[]{:S(2)}) %all-to-all-start.2) | async-done | bytes 8224 | tf_op jit(solution)/shard_map/all_to_all | solution.py:34
  140.0 0.1 copy.22
  140.0 0.7 cholesky.16
  140.8 0.6 compare_reduce_fusion
  141.4 0.6 fusion.8
  142.1 0.6 custom-call.7
  142.7 0.8 convolution_multiply_fusion
  (9 shorter events, 0.2 us)
Async XLA Ops:
  0.6 1.4 %copy-start = (bf16[256,512]{1,0:T(8,128)(2,1)S(1)}, bf16[256,512]{1,0:T(8,128)(2,1)}, u32[]{:S(2)}) copy-start(bf16[256,512]{1,0:T(8,128)(2,1)} %param.8) | copy-start | bytes 786436
  2.4 63.7 %copy-start.1 = (bf16[128,8192]{1,0:T(8,128)(2,1)S(1)}, bf16[128,8192]{1,0:T(8,128)(2,1)}, u32[]{:S(2)}) copy-start(bf16[128,8192]{1,0:T(8,128)(2,1)} %act_ref.5) | copy-start | bytes 6291460
  66.1 10.4 %collective-permute-start = (bf16[32,136,512]{2,1,0:T(8,128)(2,1)}, bf16[32,136,512]{2,1,0:T(8,128)(2,1)}, u32[]{:S(2)}, u32[]{:S(2)}) collective-permute-start(bf16[32,136,512]{2,1,0:T(8,128)(2,1)} %all_to_all.15.gd_ref.w_ref.w1_ref), channel_id=1, source_target_pairs={{0,32},{32,0},{64,96},{96,64},{1,33},{33,1},{65,97},{97,65},{2,34}... | collective-permute-start | bytes 13369352 | tf_op jit(solution)/shard_map/ppermute | solution.py:65
  67.3 9.2 %copy-start.2 = (f32[128]{0:T(128)S(1)}, f32[128]{0:T(128)}, u32[]{:S(2)}) copy-start(f32[128]{0:T(128)} %param.9) | copy-start | bytes 1540
  119.5 1.3 collective-permute-start.1
  120.8 5.2 %collective-permute-start.2 = (f32[9,256]{1,0:T(8,128)S(1)}, f32[9,256]{1,0:T(8,128)S(1)}, u32[]{:S(2)}, u32[]{:S(2)}) collective-permute-start(f32[9,256]{1,0:T(8,128)S(1)} %add.49), channel_id=1, source_target_pairs={{0,64},{32,96},{64,0},{96,32},{1,65},{33,97},{65,1},{97,33},{2,66}... | collective-permute-start | bytes 27656 | tf_op jit(solution)/shard_map/ppermute | solution.py:45
  126.8 13.1 %all-to-all-start.2 = ((f32[32,8,8]{2,1,0:T(8,128)}), f32[32,8,8]{2,1,0:T(8,128)S(1)}, u32[]{:S(2)}, u32[]{:S(2)}) async-start(f32[32,8,8]{2,1,0:T(8,128)} %broadcast_in_dim.14), calls=%async_computation.2 | async-start | bytes 262144 | tf_op jit(solution)/shard_map/all_to_all | solution.py:34

commit v10 on v9

--- a/solution.py
+++ b/solution.py
@@ -69,11 +69,10 @@
 def middle_rows(acc, cot, key_gain_row, back_ref):
     tokens = cot.shape[0]
     groups = acc.shape[0] // tokens
-    weighted_all = cot.astype(jnp.float32) * key_gain_row
     for h in range(HEADS_KV):
         cols = slice(h * HEAD_DIM, (h + 1) * HEAD_DIM)
         key = acc[0:tokens, cols]
-        weighted = weighted_all[:, cols]
+        weighted = cot[:, cols].astype(jnp.float32) * key_gain_row
         key_scale = jnp.sqrt(jnp.sum(key * key, axis=-1, keepdims=True) / HEAD_DIM + 1e-05)
         unit_keys = key / key_scale
         inner_sum = jnp.sum(unit_keys * weighted, axis=-1, keepdims=True)
@@ -151,7 +150,7 @@
     shards = tile // (2 * HALF)
     common = [
         pl.BlockSpec((tokens, tile), lambda k, c: (0, k)),
-        pl.BlockSpec((tokens, 1), lambda k, c: (0, 0)),
+        pl.BlockSpec((tokens, HALF), lambda k, c: (0, 0)),
         pl.BlockSpec((shards, EXTRA_ROWS, keys), lambda k, c: (k, HALF // EXTRA_ROWS, 0)),
         pl.BlockSpec((shards, HALF, keys), lambda k, c: (k, 0, 0)),
     ]
@@ -177,7 +176,7 @@
             + [
                 pl.BlockSpec((groups * tokens, keys), lambda k, c: (0, 0)),
                 pl.BlockSpec((tokens, keys), lambda k, c: (0, 0)),
-                pl.BlockSpec((1, keys), lambda k, c: (0, 0)),
+                pl.BlockSpec((1, HEAD_DIM), lambda k, c: (0, 0)),
             ],
             out_specs=pl.BlockSpec((groups * tokens, keys), lambda k, c: (0, 0)),
             scratch_shapes=[
@@ -235,7 +234,7 @@
                 pl.BlockSpec((shards, HALF, keys), lambda k, c: (k, 0, 0)),
                 pl.BlockSpec((shards, HALF, keys), lambda k, c: (k, 0, 0)),
                 pl.BlockSpec((tokens, tile), lambda k, c: (0, k)),
-                pl.BlockSpec((tokens, 1), lambda k, c: (0, 0)),
+                pl.BlockSpec((tokens, HALF), lambda k, c: (0, 0)),
             ],
             out_specs=pl.BlockSpec((shards, groups, 2 * HALF), lambda k, c: (k, 0, 0)),
         ),
@@ -249,11 +248,12 @@
     total_tokens = tokens_dev * lax.axis_size("dp") * lax.axis_size("fsdp")
     values = activations.astype(jnp.float32)
     rms = jnp.sqrt(jnp.mean(values * values, axis=1, keepdims=True) + 1e-05)
+    rms = jnp.broadcast_to(rms, (tokens_dev, HALF))
     groups = directions.shape[1] + 1
     core = (lax.axis_index("dp") % 2).astype(jnp.int32).reshape(1)
 
     first, second = gather_weight(key_weight, gain, directions)
-    kg_row = jnp.tile(key_gain, HEADS_KV)[None, :]
+    kg_row = key_gain[None, :]
 
     back_rows = forward_rows(core, activations, rms, first, second, cotangent, kg_row)
     partial_terms = backward_terms(core, back_rows, first, second, activations, rms, groups)

time: 144 us -> 143 us (level)
  no operation moved by 1% of the time
where the time goes in v10:
time: 143 us; the launch traced here: 142 us
  blocking collectives  79.7 us (56%)
  Pallas kernels  34.7 us (24%)
  waiting for transfers between devices  11.7 us (8%)
  starting transfers between devices  7.33 us (5%)
  other arithmetic  3.97 us (3%)
  local copies, waits for them, and re-layouts  3.04 us (2%)
    all_to_all x1, blocking collectives, copy_for_each(): return lax.all_to_all(copies, axis, split_axis=0, concat_axis=0, tiled=True)  63.7 us
    all_to_all x1, blocking collectives, per_device(): lax.all_to_all(partial_terms, 'fsdp', 0, 0, tiled=True)  16.1 us
    pallas_call x1, Pallas kernels, backward_terms(): pl.pallas_call(backward_kernel, grid_spec=pltpu.PrefetchScalarGridSpec(nu...  13.5 us
    pallas_call x1, Pallas kernels, forward_rows(): pl.pallas_call(forward_second_kernel, grid_spec=pltpu.PrefetchScalarGridS...  12.4 us
    pallas_call x1, Pallas kernels, forward_rows(): pl.pallas_call(forward_first_kernel, grid_spec=pltpu.PrefetchScalarGridSp...  8.74 us
    all_to_all x1, waiting for transfers between devices, copy_for_each(): return lax.all_to_all(copies, axis, split_axis=0, concat_axis=0, tiled=True)  8.18 us
    all_to_all x1, starting transfers between devices, copy_for_each(): return lax.all_to_all(copies, axis, split_axis=0, concat_axis=0, tiled=True)  4.34 us
    ppermute x2, waiting for transfers between devices, sum_over_pairs(): lax.ppermute(shard, axis, [(i, i ^ step) for i in range(devices)])  3.51 us
  transfers between devices with their start and end apart: 4, of which 3 were waited for; matrix products, arithmetic and copies ran while one was open for 1% of the time, Pallas kernels for 6%

profile of v10, /device:TPU:0, one launch (start us, length us, event | category | flops | bytes accessed | tf_op | source)
XLA Modules:
  0.0 142.1 jit_solution(2855297443710628442)
XLA Ops:
  0.6 0.0 copy-start
  0.7 0.7 broadcast_in_dim.21
  1.4 0.7 fusion.4
  2.1 0.0 copy-done
  2.1 0.3 broadcast_in_dim.22
  2.4 0.0 copy-start.1
  2.4 63.7 %all_to_all.15.gd_ref.w_ref.w1_ref = bf16[32,136,512]{2,1,0:T(8,128)(2,1)} all-to-all(bf16[32,136,512]{2,1,0:T(8,128)(2,1)S(1)} %broadcast_in_dim.22), channel_id=1, replica_groups=mesh['dp'=4,'fsdp'=32] {'fsdp'}, dimensions={0} | all-to-all | bytes 8912896 | tf_op jit(solution)/shard_map/all_to_all | solution.py:34
  66.1 0.0 collective-permute-start
  66.1 0.0 copy-done.1
  66.1 0.5 multiply_reduce_fusion
  66.6 0.7 broadcast_in_dim.20.rms_ref
  67.3 8.7 %shard_map.77.acc_in_ref = f32[1152,512]{1,0:T(8,128)} custom-call(s32[1]{0:T(128)} %bitcast.core_ref, bf16[128,8192]{1,0:T(8,128)(2,1)} %act_ref.5, f32[128,128]{1,0:T(8,128)} %broadcast_in_dim.20.rms_ref, bf16[32,136,512]{2,1,0:T(8,128)(2,1)} %all_to_all.15.gd_ref.w_ref.w1_ref, bf16[32,136,512]{2,1,0:T(8,128)(2,1)} %all_to_all.15.gd_ref.w_ref.w1_ref), custom_call_target="tpu_custom_call" | custom-call | tf_op jit(solution)/shard_map/pallas_call | solution.py:158
  76.1 0.0 collective-permute-done.w_ref.w2_ref
  76.1 12.4 %shard_map.78.back_ref = bf16[1152,512]{1,0:T(8,128)(2,1)} custom-call(s32[1]{0:T(128)} %bitcast.core_ref, bf16[128,8192]{1,0:T(8,128)(2,1)} %act_ref.5, f32[128,128]{1,0:T(8,128)} %broadcast_in_dim.20.rms_ref, bf16[32,136,512]{2,1,0:T(8,128)(2,1)} %all_to_all.15.gd_ref.w_ref.w1_ref, bf16[32,136,512]{2,1,0:T(8,128)(2,1)} %collective-permute-done.w_ref.w2_ref, ...), custom_call_target="tpu_custom_call" | custom-call | tf_op jit(solution)/shard_map/pallas_call | solution.py:170
  88.5 13.5 %shard_map.79 = f32[32,9,256]{2,1,0:T(8,128)} custom-call(s32[1]{0:T(128)} %bitcast.core_ref, bf16[1152,512]{1,0:T(8,128)(2,1)} %shard_map.78.back_ref, bf16[32,136,512]{2,1,0:T(8,128)(2,1)} %all_to_all.15.gd_ref.w_ref.w1_ref, bf16[32,136,512]{2,1,0:T(8,128)(2,1)} %collective-permute-done.w_ref.w2_ref, bf16[128,8192]{1,0:T(8,128)(2,1)} %act_ref.5, ...), custom_call_target="tpu_custom_call" | custom-call | tf_op jit(solution)/shard_map/pallas_call | solution.py:227
  102.0 16.1 %all_to_all.16 = f32[32,9,256]{2,1,0:T(8,128)S(1)} all-to-all(f32[32,9,256]{2,1,0:T(8,128)} %shard_map.79), channel_id=1, replica_groups=mesh['dp'=4,'fsdp'=32] {'fsdp'}, dimensions={0} | all-to-all | bytes 589824 | tf_op jit(solution)/shard_map/all_to_all | solution.py:260
  118.1 0.1 reduce_sum.28
  118.1 0.1 collective-permute-start.1
  118.2 1.2 collective-permute-done.1
  119.4 2.9 %collective-permute-start.2 = (f32[9,256]{1,0:T(8,128)S(1)}, f32[9,256]{1,0:T(8,128)S(1)}, u32[]{:S(2)}, u32[]{:S(2)}) collective-permute-start(f32[9,256]{1,0:T(8,128)S(1)} %add.45), channel_id=1, source_target_pairs={{0,64},{32,96},{64,0},{96,32},{1,65},{33,97},{65,1},{97,33},{2,66}... | collective-permute-start | bytes 27656 | tf_op jit(solution)/shard_map/ppermute | solution.py:45
  122.3 2.3 %collective-permute-done.2 = f32[9,256]{1,0:T(8,128)S(1)} collective-permute-done((f32[9,256]{1,0:T(8,128)S(1)}, f32[9,256]{1,0:T(8,128)S(1)}, u32[]{:S(2)}, u32[]{:S(2)}) %collective-permute-start.2) | collective-permute-done | bytes 9248 | tf_op jit(solution)/shard_map/ppermute | solution.py:45
  124.6 0.1 fusion.6
  124.8 0.7 broadcast_in_dim.24
  125.4 4.3 %all-to-all-start.2 = ((f32[32,8,8]{2,1,0:T(8,128)}), f32[32,8,8]{2,1,0:T(8,128)S(1)}, u32[]{:S(2)}, u32[]{:S(2)}) async-start(f32[32,8,8]{2,1,0:T(8,128)} %broadcast_in_dim.24), calls=%async_computation.2 | async-start | bytes 262144 | tf_op jit(solution)/shard_map/all_to_all | solution.py:34
  129.8 0.6 slice.18
  130.3 8.2 %all-to-all-done.2 = f32[32,8,8]{2,1,0:T(8,128)S(1)} async-done(((f32[32,8,8]{2,1,0:T(8,128)}), f32[32,8,8]{2,1,0:T(8,128)S(1)}, u32[]{:S(2)}, u32[]{:S(2)}) %all-to-all-start.2) | async-done | bytes 8224 | tf_op jit(solution)/shard_map/all_to_all | solution.py:34
  138.5 0.1 copy.13
  138.6 0.7 cholesky.16
  139.4 0.6 compare_reduce_fusion
  140.0 0.6 fusion.8
  140.7 0.6 custom-call.7
  141.3 0.8 convolution_multiply_fusion
  (9 shorter events, 0.2 us)
Async XLA Ops:
  0.6 1.4 %copy-start = (bf16[256,512]{1,0:T(8,128)(2,1)S(1)}, bf16[256,512]{1,0:T(8,128)(2,1)}, u32[]{:S(2)}) copy-start(bf16[256,512]{1,0:T(8,128)(2,1)} %param.8) | copy-start | bytes 786436
  2.4 63.7 %copy-start.1 = (bf16[128,8192]{1,0:T(8,128)(2,1)S(1)}, bf16[128,8192]{1,0:T(8,128)(2,1)}, u32[]{:S(2)}) copy-start(bf16[128,8192]{1,0:T(8,128)(2,1)} %act_ref.5) | copy-start | bytes 6291460
  66.1 10.0 %collective-permute-start = (bf16[32,136,512]{2,1,0:T(8,128)(2,1)}, bf16[32,136,512]{2,1,0:T(8,128)(2,1)}, u32[]{:S(2)}, u32[]{:S(2)}) collective-permute-start(bf16[32,136,512]{2,1,0:T(8,128)(2,1)} %all_to_all.15.gd_ref.w_ref.w1_ref), channel_id=1, source_target_pairs={{0,32},{32,0},{64,96},{96,64},{1,33},{33,1},{65,97},{97,65},{2,34}... | collective-permute-start | bytes 13369352 | tf_op jit(solution)/shard_map/ppermute | solution.py:65
  118.1 1.3 collective-permute-start.1
  119.4 5.2 %collective-permute-start.2 = (f32[9,256]{1,0:T(8,128)S(1)}, f32[9,256]{1,0:T(8,128)S(1)}, u32[]{:S(2)}, u32[]{:S(2)}) collective-permute-start(f32[9,256]{1,0:T(8,128)S(1)} %add.45), channel_id=1, source_target_pairs={{0,64},{32,96},{64,0},{96,32},{1,65},{33,97},{65,1},{97,33},{2,66}... | collective-permute-start | bytes 27656 | tf_op jit(solution)/shard_map/ppermute | solution.py:45
  125.4 13.1 %all-to-all-start.2 = ((f32[32,8,8]{2,1,0:T(8,128)}), f32[32,8,8]{2,1,0:T(8,128)S(1)}, u32[]{:S(2)}, u32[]{:S(2)}) async-start(f32[32,8,8]{2,1,0:T(8,128)} %broadcast_in_dim.24), calls=%async_computation.2 | async-start | bytes 262144 | tf_op jit(solution)/shard_map/all_to_all | solution.py:34

commit v11 on v10

--- a/solution.py
+++ b/solution.py
@@ -14,7 +14,7 @@
 EXTRA_ROWS = 8
 GROUPS = 9
 FWD_TILE = 1024
-BWD_TILE = 1024
+BWD_TILE = 512
 
 
 def in_blocks(shard, dim, devices):

time: 143 us -> 143 us (level)
  no operation moved by 1% of the time
where the time goes in v11:
time: 143 us
  blocking collectives  79.7 us (56%)
  Pallas kernels  35.2 us (25%)
  waiting for transfers between devices  11.7 us (8%)
  starting transfers between devices  7.33 us (5%)
  other arithmetic  3.97 us (3%)
  local copies, waits for them, and re-layouts  3.04 us (2%)
    all_to_all x1, blocking collectives, copy_for_each(): return lax.all_to_all(copies, axis, split_axis=0, concat_axis=0, tiled=True)  63.7 us
    all_to_all x1, blocking collectives, per_device(): lax.all_to_all(partial_terms, 'fsdp', 0, 0, tiled=True)  16.1 us
    pallas_call x1, Pallas kernels, backward_terms(): pl.pallas_call(backward_kernel, grid_spec=pltpu.PrefetchScalarGridSpec(nu...  14.1 us
    pallas_call x1, Pallas kernels, forward_rows(): pl.pallas_call(forward_second_kernel, grid_spec=pltpu.PrefetchScalarGridS...  12.4 us
    pallas_call x1, Pallas kernels, forward_rows(): pl.pallas_call(forward_first_kernel, grid_spec=pltpu.PrefetchScalarGridSp...  8.74 us
    all_to_all x1, waiting for transfers between devices, copy_for_each(): return lax.all_to_all(copies, axis, split_axis=0, concat_axis=0, tiled=True)  8.18 us
    all_to_all x1, starting transfers between devices, copy_for_each(): return lax.all_to_all(copies, axis, split_axis=0, concat_axis=0, tiled=True)  4.34 us
    ppermute x2, waiting for transfers between devices, sum_over_pairs(): lax.ppermute(shard, axis, [(i, i ^ step) for i in range(devices)])  3.51 us
  transfers between devices with their start and end apart: 4, of which 3 were waited for; matrix products, arithmetic and copies ran while one was open for 1% of the time, Pallas kernels for 6%

profile of v11, /device:TPU:0, one launch (start us, length us, event | category | flops | bytes accessed | tf_op | source)
XLA Modules:
  0.0 142.7 jit_solution(14038909918365558346)
XLA Ops:
  0.6 0.0 copy-start
  0.7 0.7 broadcast_in_dim.21
  1.4 0.7 fusion.4
  2.1 0.0 copy-done
  2.1 0.3 broadcast_in_dim.22
  2.4 0.0 copy-start.1
  2.4 63.7 %all_to_all.15.gd_ref.w_ref.w1_ref = bf16[32,136,512]{2,1,0:T(8,128)(2,1)} all-to-all(bf16[32,136,512]{2,1,0:T(8,128)(2,1)S(1)} %broadcast_in_dim.22), channel_id=1, replica_groups=mesh['dp'=4,'fsdp'=32] {'fsdp'}, dimensions={0} | all-to-all | bytes 8912896 | tf_op jit(solution)/shard_map/all_to_all | solution.py:34
  66.1 0.0 collective-permute-start
  66.1 0.0 copy-done.1
  66.1 0.5 multiply_reduce_fusion
  66.6 0.7 broadcast_in_dim.20.rms_ref
  67.3 8.7 %shard_map.77.acc_in_ref = f32[1152,512]{1,0:T(8,128)} custom-call(s32[1]{0:T(128)} %bitcast.core_ref, bf16[128,8192]{1,0:T(8,128)(2,1)} %act_ref.5, f32[128,128]{1,0:T(8,128)} %broadcast_in_dim.20.rms_ref, bf16[32,136,512]{2,1,0:T(8,128)(2,1)} %all_to_all.15.gd_ref.w_ref.w1_ref, bf16[32,136,512]{2,1,0:T(8,128)(2,1)} %all_to_all.15.gd_ref.w_ref.w1_ref), custom_call_target="tpu_custom_call" | custom-call | tf_op jit(solution)/shard_map/pallas_call | solution.py:158
  76.1 0.0 collective-permute-done.w_ref.w2_ref
  76.1 12.4 %shard_map.78.back_ref = bf16[1152,512]{1,0:T(8,128)(2,1)} custom-call(s32[1]{0:T(128)} %bitcast.core_ref, bf16[128,8192]{1,0:T(8,128)(2,1)} %act_ref.5, f32[128,128]{1,0:T(8,128)} %broadcast_in_dim.20.rms_ref, bf16[32,136,512]{2,1,0:T(8,128)(2,1)} %all_to_all.15.gd_ref.w_ref.w1_ref, bf16[32,136,512]{2,1,0:T(8,128)(2,1)} %collective-permute-done.w_ref.w2_ref, ...), custom_call_target="tpu_custom_call" | custom-call | tf_op jit(solution)/shard_map/pallas_call | solution.py:170
  88.5 14.1 %shard_map.79 = f32[32,9,256]{2,1,0:T(8,128)} custom-call(s32[1]{0:T(128)} %bitcast.core_ref, bf16[1152,512]{1,0:T(8,128)(2,1)} %shard_map.78.back_ref, bf16[32,136,512]{2,1,0:T(8,128)(2,1)} %all_to_all.15.gd_ref.w_ref.w1_ref, bf16[32,136,512]{2,1,0:T(8,128)(2,1)} %collective-permute-done.w_ref.w2_ref, bf16[128,8192]{1,0:T(8,128)(2,1)} %act_ref.5, ...), custom_call_target="tpu_custom_call" | custom-call | tf_op jit(solution)/shard_map/pallas_call | solution.py:227
  102.5 16.1 %all_to_all.16 = f32[32,9,256]{2,1,0:T(8,128)S(1)} all-to-all(f32[32,9,256]{2,1,0:T(8,128)} %shard_map.79), channel_id=1, replica_groups=mesh['dp'=4,'fsdp'=32] {'fsdp'}, dimensions={0} | all-to-all | bytes 589824 | tf_op jit(solution)/shard_map/all_to_all | solution.py:260
  118.6 0.1 reduce_sum.28
  118.7 0.1 collective-permute-start.1
  118.8 1.2 collective-permute-done.1
  119.9 2.9 %collective-permute-start.2 = (f32[9,256]{1,0:T(8,128)S(1)}, f32[9,256]{1,0:T(8,128)S(1)}, u32[]{:S(2)}, u32[]{:S(2)}) collective-permute-start(f32[9,256]{1,0:T(8,128)S(1)} %add.45), channel_id=1, source_target_pairs={{0,64},{32,96},{64,0},{96,32},{1,65},{33,97},{65,1},{97,33},{2,66}... | collective-permute-start | bytes 27656 | tf_op jit(solution)/shard_map/ppermute | solution.py:45
  122.8 2.3 %collective-permute-done.2 = f32[9,256]{1,0:T(8,128)S(1)} collective-permute-done((f32[9,256]{1,0:T(8,128)S(1)}, f32[9,256]{1,0:T(8,128)S(1)}, u32[]{:S(2)}, u32[]{:S(2)}) %collective-permute-start.2) | collective-permute-done | bytes 9248 | tf_op jit(solution)/shard_map/ppermute | solution.py:45
  125.2 0.1 fusion.6
  125.3 0.7 broadcast_in_dim.24
  126.0 4.3 %all-to-all-start.2 = ((f32[32,8,8]{2,1,0:T(8,128)}), f32[32,8,8]{2,1,0:T(8,128)S(1)}, u32[]{:S(2)}, u32[]{:S(2)}) async-start(f32[32,8,8]{2,1,0:T(8,128)} %broadcast_in_dim.24), calls=%async_computation.2 | async-start | bytes 262144 | tf_op jit(solution)/shard_map/all_to_all | solution.py:34
  130.3 0.6 slice.18
  130.9 8.2 %all-to-all-done.2 = f32[32,8,8]{2,1,0:T(8,128)S(1)} async-done(((f32[32,8,8]{2,1,0:T(8,128)}), f32[32,8,8]{2,1,0:T(8,128)S(1)}, u32[]{:S(2)}, u32[]{:S(2)}) %all-to-all-start.2) | async-done | bytes 8224 | tf_op jit(solution)/shard_map/all_to_all | solution.py:34
  139.1 0.1 copy.13
  139.2 0.7 cholesky.16
  139.9 0.6 compare_reduce_fusion
  140.6 0.6 fusion.8
  141.2 0.6 custom-call.7
  141.9 0.8 convolution_multiply_fusion
  (9 shorter events, 0.2 us)
Async XLA Ops:
  0.6 1.4 %copy-start = (bf16[256,512]{1,0:T(8,128)(2,1)S(1)}, bf16[256,512]{1,0:T(8,128)(2,1)}, u32[]{:S(2)}) copy-start(bf16[256,512]{1,0:T(8,128)(2,1)} %param.8) | copy-start | bytes 786436
  2.4 63.7 %copy-start.1 = (bf16[128,8192]{1,0:T(8,128)(2,1)S(1)}, bf16[128,8192]{1,0:T(8,128)(2,1)}, u32[]{:S(2)}) copy-start(bf16[128,8192]{1,0:T(8,128)(2,1)} %act_ref.5) | copy-start | bytes 6291460
  66.1 10.0 %collective-permute-start = (bf16[32,136,512]{2,1,0:T(8,128)(2,1)}, bf16[32,136,512]{2,1,0:T(8,128)(2,1)}, u32[]{:S(2)}, u32[]{:S(2)}) collective-permute-start(bf16[32,136,512]{2,1,0:T(8,128)(2,1)} %all_to_all.15.gd_ref.w_ref.w1_ref), channel_id=1, source_target_pairs={{0,32},{32,0},{64,96},{96,64},{1,33},{33,1},{65,97},{97,65},{2,34}... | collective-permute-start | bytes 13369352 | tf_op jit(solution)/shard_map/ppermute | solution.py:65
  118.7 1.3 collective-permute-start.1
  119.9 5.2 %collective-permute-start.2 = (f32[9,256]{1,0:T(8,128)S(1)}, f32[9,256]{1,0:T(8,128)S(1)}, u32[]{:S(2)}, u32[]{:S(2)}) collective-permute-start(f32[9,256]{1,0:T(8,128)S(1)} %add.45), channel_id=1, source_target_pairs={{0,64},{32,96},{64,0},{96,32},{1,65},{33,97},{65,1},{97,33},{2,66}... | collective-permute-start | bytes 27656 | tf_op jit(solution)/shard_map/ppermute | solution.py:45
  126.0 13.1 %all-to-all-start.2 = ((f32[32,8,8]{2,1,0:T(8,128)}), f32[32,8,8]{2,1,0:T(8,128)S(1)}, u32[]{:S(2)}, u32[]{:S(2)}) async-start(f32[32,8,8]{2,1,0:T(8,128)} %broadcast_in_dim.24), calls=%async_computation.2 | async-start | bytes 262144 | tf_op jit(solution)/shard_map/all_to_all | solution.py:34

commit v12 on v10

--- a/solution.py
+++ b/solution.py
@@ -13,7 +13,7 @@
 HALF = 128
 EXTRA_ROWS = 8
 GROUPS = 9
-FWD_TILE = 1024
+FWD_TILE = 2048
 BWD_TILE = 1024
 
 

time: 143 us -> 143 us (level)
  no operation moved by 1% of the time
where the time goes in v12:
time: 143 us; the launch traced here: 142 us
  blocking collectives  79.7 us (56%)
  Pallas kernels  34.8 us (24%)
  waiting for transfers between devices  11.7 us (8%)
  starting transfers between devices  7.33 us (5%)
  other arithmetic  3.97 us (3%)
  local copies, waits for them, and re-layouts  3.04 us (2%)
    all_to_all x1, blocking collectives, copy_for_each(): return lax.all_to_all(copies, axis, split_axis=0, concat_axis=0, tiled=True)  63.7 us
    all_to_all x1, blocking collectives, per_device(): lax.all_to_all(partial_terms, 'fsdp', 0, 0, tiled=True)  16.1 us
    pallas_call x1, Pallas kernels, backward_terms(): pl.pallas_call(backward_kernel, grid_spec=pltpu.PrefetchScalarGridSpec(nu...  13.5 us
    pallas_call x1, Pallas kernels, forward_rows(): pl.pallas_call(forward_second_kernel, grid_spec=pltpu.PrefetchScalarGridS...  12.5 us
    pallas_call x1, Pallas kernels, forward_rows(): pl.pallas_call(forward_first_kernel, grid_spec=pltpu.PrefetchScalarGridSp...  8.88 us
    all_to_all x1, waiting for transfers between devices, copy_for_each(): return lax.all_to_all(copies, axis, split_axis=0, concat_axis=0, tiled=True)  8.18 us
    all_to_all x1, starting transfers between devices, copy_for_each(): return lax.all_to_all(copies, axis, split_axis=0, concat_axis=0, tiled=True)  4.34 us
    ppermute x2, waiting for transfers between devices, sum_over_pairs(): lax.ppermute(shard, axis, [(i, i ^ step) for i in range(devices)])  3.51 us
  transfers between devices with their start and end apart: 4, of which 3 were waited for; matrix products, arithmetic and copies ran while one was open for 1% of the time, Pallas kernels for 6%

profile of v12, /device:TPU:0, one launch (start us, length us, event | category | flops | bytes accessed | tf_op | source)
XLA Modules:
  0.0 142.3 jit_solution(16171331769738844368)
XLA Ops:
  0.6 0.0 copy-start
  0.7 0.7 broadcast_in_dim.21
  1.4 0.7 fusion.4
  2.1 0.0 copy-done
  2.1 0.3 broadcast_in_dim.22
  2.4 0.0 copy-start.1
  2.4 63.7 %all_to_all.15.gd_ref.w_ref.w1_ref = bf16[32,136,512]{2,1,0:T(8,128)(2,1)} all-to-all(bf16[32,136,512]{2,1,0:T(8,128)(2,1)S(1)} %broadcast_in_dim.22), channel_id=1, replica_groups=mesh['dp'=4,'fsdp'=32] {'fsdp'}, dimensions={0} | all-to-all | bytes 8912896 | tf_op jit(solution)/shard_map/all_to_all | solution.py:34
  66.1 0.0 collective-permute-start
  66.1 0.0 copy-done.1
  66.1 0.5 multiply_reduce_fusion
  66.6 0.7 broadcast_in_dim.20.rms_ref
  67.3 8.9 %shard_map.77.acc_in_ref = f32[1152,512]{1,0:T(8,128)} custom-call(s32[1]{0:T(128)} %bitcast.core_ref, bf16[128,8192]{1,0:T(8,128)(2,1)} %act_ref.5, f32[128,128]{1,0:T(8,128)} %broadcast_in_dim.20.rms_ref, bf16[32,136,512]{2,1,0:T(8,128)(2,1)} %all_to_all.15.gd_ref.w_ref.w1_ref, bf16[32,136,512]{2,1,0:T(8,128)(2,1)} %all_to_all.15.gd_ref.w_ref.w1_ref), custom_call_target="tpu_custom_call" | custom-call | tf_op jit(solution)/shard_map/pallas_call | solution.py:158
  76.2 0.0 collective-permute-done.w_ref.w2_ref
  76.2 12.5 %shard_map.78.back_ref = bf16[1152,512]{1,0:T(8,128)(2,1)} custom-call(s32[1]{0:T(128)} %bitcast.core_ref, bf16[128,8192]{1,0:T(8,128)(2,1)} %act_ref.5, f32[128,128]{1,0:T(8,128)} %broadcast_in_dim.20.rms_ref, bf16[32,136,512]{2,1,0:T(8,128)(2,1)} %all_to_all.15.gd_ref.w_ref.w1_ref, bf16[32,136,512]{2,1,0:T(8,128)(2,1)} %collective-permute-done.w_ref.w2_ref, ...), custom_call_target="tpu_custom_call" | custom-call | tf_op jit(solution)/shard_map/pallas_call | solution.py:170
  88.6 13.5 %shard_map.79 = f32[32,9,256]{2,1,0:T(8,128)} custom-call(s32[1]{0:T(128)} %bitcast.core_ref, bf16[1152,512]{1,0:T(8,128)(2,1)} %shard_map.78.back_ref, bf16[32,136,512]{2,1,0:T(8,128)(2,1)} %all_to_all.15.gd_ref.w_ref.w1_ref, bf16[32,136,512]{2,1,0:T(8,128)(2,1)} %collective-permute-done.w_ref.w2_ref, bf16[128,8192]{1,0:T(8,128)(2,1)} %act_ref.5, ...), custom_call_target="tpu_custom_call" | custom-call | tf_op jit(solution)/shard_map/pallas_call | solution.py:227
  102.2 16.1 %all_to_all.16 = f32[32,9,256]{2,1,0:T(8,128)S(1)} all-to-all(f32[32,9,256]{2,1,0:T(8,128)} %shard_map.79), channel_id=1, replica_groups=mesh['dp'=4,'fsdp'=32] {'fsdp'}, dimensions={0} | all-to-all | bytes 589824 | tf_op jit(solution)/shard_map/all_to_all | solution.py:260
  118.2 0.1 reduce_sum.28
  118.3 0.1 collective-permute-start.1
  118.4 1.2 collective-permute-done.1
  119.6 2.9 %collective-permute-start.2 = (f32[9,256]{1,0:T(8,128)S(1)}, f32[9,256]{1,0:T(8,128)S(1)}, u32[]{:S(2)}, u32[]{:S(2)}) collective-permute-start(f32[9,256]{1,0:T(8,128)S(1)} %add.45), channel_id=1, source_target_pairs={{0,64},{32,96},{64,0},{96,32},{1,65},{33,97},{65,1},{97,33},{2,66}... | collective-permute-start | bytes 27656 | tf_op jit(solution)/shard_map/ppermute | solution.py:45
  122.5 2.3 %collective-permute-done.2 = f32[9,256]{1,0:T(8,128)S(1)} collective-permute-done((f32[9,256]{1,0:T(8,128)S(1)}, f32[9,256]{1,0:T(8,128)S(1)}, u32[]{:S(2)}, u32[]{:S(2)}) %collective-permute-start.2) | collective-permute-done | bytes 9248 | tf_op jit(solution)/shard_map/ppermute | solution.py:45
  124.8 0.1 fusion.6
  124.9 0.7 broadcast_in_dim.24
  125.6 4.3 %all-to-all-start.2 = ((f32[32,8,8]{2,1,0:T(8,128)}), f32[32,8,8]{2,1,0:T(8,128)S(1)}, u32[]{:S(2)}, u32[]{:S(2)}) async-start(f32[32,8,8]{2,1,0:T(8,128)} %broadcast_in_dim.24), calls=%async_computation.2 | async-start | bytes 262144 | tf_op jit(solution)/shard_map/all_to_all | solution.py:34
  129.9 0.6 slice.18
  130.5 8.2 %all-to-all-done.2 = f32[32,8,8]{2,1,0:T(8,128)S(1)} async-done(((f32[32,8,8]{2,1,0:T(8,128)}), f32[32,8,8]{2,1,0:T(8,128)S(1)}, u32[]{:S(2)}, u32[]{:S(2)}) %all-to-all-start.2) | async-done | bytes 8224 | tf_op jit(solution)/shard_map/all_to_all | solution.py:34
  138.7 0.1 copy.13
  138.8 0.7 cholesky.16
  139.6 0.6 compare_reduce_fusion
  140.2 0.6 fusion.8
  140.9 0.6 custom-call.7
  141.5 0.8 convolution_multiply_fusion
  (9 shorter events, 0.2 us)
Async XLA Ops:
  0.6 1.4 %copy-start = (bf16[256,512]{1,0:T(8,128)(2,1)S(1)}, bf16[256,512]{1,0:T(8,128)(2,1)}, u32[]{:S(2)}) copy-start(bf16[256,512]{1,0:T(8,128)(2,1)} %param.8) | copy-start | bytes 786436
  2.4 63.7 %copy-start.1 = (bf16[128,8192]{1,0:T(8,128)(2,1)S(1)}, bf16[128,8192]{1,0:T(8,128)(2,1)}, u32[]{:S(2)}) copy-start(bf16[128,8192]{1,0:T(8,128)(2,1)} %act_ref.5) | copy-start | bytes 6291460
  66.1 10.1 %collective-permute-start = (bf16[32,136,512]{2,1,0:T(8,128)(2,1)}, bf16[32,136,512]{2,1,0:T(8,128)(2,1)}, u32[]{:S(2)}, u32[]{:S(2)}) collective-permute-start(bf16[32,136,512]{2,1,0:T(8,128)(2,1)} %all_to_all.15.gd_ref.w_ref.w1_ref), channel_id=1, source_target_pairs={{0,32},{32,0},{64,96},{96,64},{1,33},{33,1},{65,97},{97,65},{2,34}... | collective-permute-start | bytes 13369352 | tf_op jit(solution)/shard_map/ppermute | solution.py:65
  118.3 1.3 collective-permute-start.1
  119.6 5.2 %collective-permute-start.2 = (f32[9,256]{1,0:T(8,128)S(1)}, f32[9,256]{1,0:T(8,128)S(1)}, u32[]{:S(2)}, u32[]{:S(2)}) collective-permute-start(f32[9,256]{1,0:T(8,128)S(1)} %add.45), channel_id=1, source_target_pairs={{0,64},{32,96},{64,0},{96,32},{1,65},{33,97},{65,1},{97,33},{2,66}... | collective-permute-start | bytes 27656 | tf_op jit(solution)/shard_map/ppermute | solution.py:45
  125.6 13.1 %all-to-all-start.2 = ((f32[32,8,8]{2,1,0:T(8,128)}), f32[32,8,8]{2,1,0:T(8,128)S(1)}, u32[]{:S(2)}, u32[]{:S(2)}) async-start(f32[32,8,8]{2,1,0:T(8,128)} %broadcast_in_dim.24), calls=%async_computation.2 | async-start | bytes 262144 | tf_op jit(solution)/shard_map/all_to_all | solution.py:34

commit v13 on v10

--- a/solution.py
+++ b/solution.py
@@ -117,12 +117,16 @@
 def forward_first_kernel(core_ref, act_ref, rms_ref, gd_ref, w_ref, out_ref, lhs_ref):
     k = pl.program_id(0)
 
+    build_for(core_ref, act_ref, rms_ref, gd_ref, lhs_ref, True)
+    part = jnp.dot(lhs_ref[...], weight_tile(w_ref), preferred_element_type=jnp.float32)
+
     @pl.when(k == 0)
     def _():
-        out_ref[...] = jnp.zeros_like(out_ref)
-
-    build_for(core_ref, act_ref, rms_ref, gd_ref, lhs_ref, True)
-    out_ref[...] += jnp.dot(lhs_ref[...], weight_tile(w_ref), preferred_element_type=jnp.float32)
+        out_ref[...] = part
+
+    @pl.when(k > 0)
+    def _():
+        out_ref[...] += part
 
 
 def forward_second_kernel(
@@ -130,12 +134,16 @@
 ):
     k = pl.program_id(0)
 
+    build_for(core_ref, act_ref, rms_ref, gd_ref, lhs_ref, False)
+    part = jnp.dot(lhs_ref[...], weight_tile(w_ref), preferred_element_type=jnp.float32)
+
     @pl.when(k == 0)
     def _():
-        acc_ref[...] = acc_in_ref[...]
-
-    build_for(core_ref, act_ref, rms_ref, gd_ref, lhs_ref, False)
-    acc_ref[...] += jnp.dot(lhs_ref[...], weight_tile(w_ref), preferred_element_type=jnp.float32)
+        acc_ref[...] = acc_in_ref[...] + part
+
+    @pl.when(k > 0)
+    def _():
+        acc_ref[...] += part
 
     @pl.when(k == pl.num_programs(0) - 1)
     def _():

time: 143 us -> 144 us (level)
  transfers between devices with their start and end apart: 4 -> 4, of which waited for: 3 -> 3; matrix products, arithmetic and copies ran while one was open for 1% -> 1% of each run, Pallas kernels for 6% -> 7%
where the time goes in v13:
time: 144 us
  blocking collectives  79.7 us (55%)
  Pallas kernels  36.1 us (25%)
  waiting for transfers between devices  11.7 us (8%)
  starting transfers between devices  7.32 us (5%)
  other arithmetic  3.97 us (3%)
  local copies, waits for them, and re-layouts  3.04 us (2%)
    all_to_all x1, blocking collectives, copy_for_each(): return lax.all_to_all(copies, axis, split_axis=0, concat_axis=0, tiled=True)  63.7 us
    all_to_all x1, blocking collectives, per_device(): lax.all_to_all(partial_terms, 'fsdp', 0, 0, tiled=True)  16.1 us
    pallas_call x1, Pallas kernels, backward_terms(): pl.pallas_call(backward_kernel, grid_spec=pltpu.PrefetchScalarGridSpec(nu...  13.5 us
    pallas_call x1, Pallas kernels, forward_rows(): pl.pallas_call(forward_second_kernel, grid_spec=pltpu.PrefetchScalarGridS...  13.2 us
    pallas_call x1, Pallas kernels, forward_rows(): pl.pallas_call(forward_first_kernel, grid_spec=pltpu.PrefetchScalarGridSp...  9.38 us
    all_to_all x1, waiting for transfers between devices, copy_for_each(): return lax.all_to_all(copies, axis, split_axis=0, concat_axis=0, tiled=True)  8.18 us
    all_to_all x1, starting transfers between devices, copy_for_each(): return lax.all_to_all(copies, axis, split_axis=0, concat_axis=0, tiled=True)  4.34 us
    ppermute x2, waiting for transfers between devices, sum_over_pairs(): lax.ppermute(shard, axis, [(i, i ^ step) for i in range(devices)])  3.52 us
  transfers between devices with their start and end apart: 4, of which 3 were waited for; matrix products, arithmetic and copies ran while one was open for 1% of the time, Pallas kernels for 7%

profile of v13, /device:TPU:0, one launch (start us, length us, event | category | flops | bytes accessed | tf_op | source)
XLA Modules:
  0.0 143.5 jit_solution(16161271827380237810)
XLA Ops:
  0.6 0.0 copy-start
  0.7 0.7 broadcast_in_dim.21
  1.4 0.7 fusion.4
  2.1 0.0 copy-done
  2.1 0.3 broadcast_in_dim.22
  2.4 0.0 copy-start.1
  2.4 63.7 %all_to_all.15.gd_ref.w_ref.w1_ref = bf16[32,136,512]{2,1,0:T(8,128)(2,1)} all-to-all(bf16[32,136,512]{2,1,0:T(8,128)(2,1)S(1)} %broadcast_in_dim.22), channel_id=1, replica_groups=mesh['dp'=4,'fsdp'=32] {'fsdp'}, dimensions={0} | all-to-all | bytes 8912896 | tf_op jit(solution)/shard_map/all_to_all | solution.py:34
  66.1 0.0 collective-permute-start
  66.1 0.0 copy-done.1
  66.1 0.5 multiply_reduce_fusion
  66.6 0.7 broadcast_in_dim.20.rms_ref
  67.3 9.4 %shard_map.77.acc_in_ref = f32[1152,512]{1,0:T(8,128)} custom-call(s32[1]{0:T(128)} %bitcast.core_ref, bf16[128,8192]{1,0:T(8,128)(2,1)} %act_ref.5, f32[128,128]{1,0:T(8,128)} %broadcast_in_dim.20.rms_ref, bf16[32,136,512]{2,1,0:T(8,128)(2,1)} %all_to_all.15.gd_ref.w_ref.w1_ref, bf16[32,136,512]{2,1,0:T(8,128)(2,1)} %all_to_all.15.gd_ref.w_ref.w1_ref), custom_call_target="tpu_custom_call" | custom-call | tf_op jit(solution)/shard_map/pallas_call | solution.py:166
  76.7 0.0 collective-permute-done.w_ref.w2_ref
  76.7 13.2 %shard_map.78.back_ref = bf16[1152,512]{1,0:T(8,128)(2,1)} custom-call(s32[1]{0:T(128)} %bitcast.core_ref, bf16[128,8192]{1,0:T(8,128)(2,1)} %act_ref.5, f32[128,128]{1,0:T(8,128)} %broadcast_in_dim.20.rms_ref, bf16[32,136,512]{2,1,0:T(8,128)(2,1)} %all_to_all.15.gd_ref.w_ref.w1_ref, bf16[32,136,512]{2,1,0:T(8,128)(2,1)} %collective-permute-done.w_ref.w2_ref, ...), custom_call_target="tpu_custom_call" | custom-call | tf_op jit(solution)/shard_map/pallas_call | solution.py:178
  89.9 13.5 %shard_map.79 = f32[32,9,256]{2,1,0:T(8,128)} custom-call(s32[1]{0:T(128)} %bitcast.core_ref, bf16[1152,512]{1,0:T(8,128)(2,1)} %shard_map.78.back_ref, bf16[32,136,512]{2,1,0:T(8,128)(2,1)} %all_to_all.15.gd_ref.w_ref.w1_ref, bf16[32,136,512]{2,1,0:T(8,128)(2,1)} %collective-permute-done.w_ref.w2_ref, bf16[128,8192]{1,0:T(8,128)(2,1)} %act_ref.5, ...), custom_call_target="tpu_custom_call" | custom-call | tf_op jit(solution)/shard_map/pallas_call | solution.py:235
  103.4 16.1 %all_to_all.16 = f32[32,9,256]{2,1,0:T(8,128)S(1)} all-to-all(f32[32,9,256]{2,1,0:T(8,128)} %shard_map.79), channel_id=1, replica_groups=mesh['dp'=4,'fsdp'=32] {'fsdp'}, dimensions={0} | all-to-all | bytes 589824 | tf_op jit(solution)/shard_map/all_to_all | solution.py:268
  119.5 0.1 reduce_sum.28
  119.5 0.1 collective-permute-start.1
  119.6 1.2 collective-permute-done.1
  120.8 2.9 %collective-permute-start.2 = (f32[9,256]{1,0:T(8,128)S(1)}, f32[9,256]{1,0:T(8,128)S(1)}, u32[]{:S(2)}, u32[]{:S(2)}) collective-permute-start(f32[9,256]{1,0:T(8,128)S(1)} %add.45), channel_id=1, source_target_pairs={{0,64},{32,96},{64,0},{96,32},{1,65},{33,97},{65,1},{97,33},{2,66}... | collective-permute-start | bytes 27656 | tf_op jit(solution)/shard_map/ppermute | solution.py:45
  123.7 2.4 %collective-permute-done.2 = f32[9,256]{1,0:T(8,128)S(1)} collective-permute-done((f32[9,256]{1,0:T(8,128)S(1)}, f32[9,256]{1,0:T(8,128)S(1)}, u32[]{:S(2)}, u32[]{:S(2)}) %collective-permute-start.2) | collective-permute-done | bytes 9248 | tf_op jit(solution)/shard_map/ppermute | solution.py:45
  126.0 0.1 fusion.6
  126.2 0.7 broadcast_in_dim.24
  126.8 4.3 %all-to-all-start.2 = ((f32[32,8,8]{2,1,0:T(8,128)}), f32[32,8,8]{2,1,0:T(8,128)S(1)}, u32[]{:S(2)}, u32[]{:S(2)}) async-start(f32[32,8,8]{2,1,0:T(8,128)} %broadcast_in_dim.24), calls=%async_computation.2 | async-start | bytes 262144 | tf_op jit(solution)/shard_map/all_to_all | solution.py:34
  131.2 0.6 slice.18
  131.7 8.2 %all-to-all-done.2 = f32[32,8,8]{2,1,0:T(8,128)S(1)} async-done(((f32[32,8,8]{2,1,0:T(8,128)}), f32[32,8,8]{2,1,0:T(8,128)S(1)}, u32[]{:S(2)}, u32[]{:S(2)}) %all-to-all-start.2) | async-done | bytes 8224 | tf_op jit(solution)/shard_map/all_to_all | solution.py:34
  140.0 0.1 copy.13
  140.0 0.7 cholesky.16
  140.8 0.6 compare_reduce_fusion
  141.4 0.6 fusion.8
  142.1 0.6 custom-call.7
  142.7 0.8 convolution_multiply_fusion
  (9 shorter events, 0.2 us)
Async XLA Ops:
  0.6 1.4 %copy-start = (bf16[256,512]{1,0:T(8,128)(2,1)S(1)}, bf16[256,512]{1,0:T(8,128)(2,1)}, u32[]{:S(2)}) copy-start(bf16[256,512]{1,0:T(8,128)(2,1)} %param.8) | copy-start | bytes 786436
  2.4 63.7 %copy-start.1 = (bf16[128,8192]{1,0:T(8,128)(2,1)S(1)}, bf16[128,8192]{1,0:T(8,128)(2,1)}, u32[]{:S(2)}) copy-start(bf16[128,8192]{1,0:T(8,128)(2,1)} %act_ref.5) | copy-start | bytes 6291460
  66.1 10.6 %collective-permute-start = (bf16[32,136,512]{2,1,0:T(8,128)(2,1)}, bf16[32,136,512]{2,1,0:T(8,128)(2,1)}, u32[]{:S(2)}, u32[]{:S(2)}) collective-permute-start(bf16[32,136,512]{2,1,0:T(8,128)(2,1)} %all_to_all.15.gd_ref.w_ref.w1_ref), channel_id=1, source_target_pairs={{0,32},{32,0},{64,96},{96,64},{1,33},{33,1},{65,97},{97,65},{2,34}... | collective-permute-start | bytes 13369352 | tf_op jit(solution)/shard_map/ppermute | solution.py:65
  119.5 1.3 collective-permute-start.1
  120.8 5.2 %collective-permute-start.2 = (f32[9,256]{1,0:T(8,128)S(1)}, f32[9,256]{1,0:T(8,128)S(1)}, u32[]{:S(2)}, u32[]{:S(2)}) collective-permute-start(f32[9,256]{1,0:T(8,128)S(1)} %add.45), channel_id=1, source_target_pairs={{0,64},{32,96},{64,0},{96,32},{1,65},{33,97},{65,1},{97,33},{2,66}... | collective-permute-start | bytes 27656 | tf_op jit(solution)/shard_map/ppermute | solution.py:45
  126.8 13.1 %all-to-all-start.2 = ((f32[32,8,8]{2,1,0:T(8,128)}), f32[32,8,8]{2,1,0:T(8,128)S(1)}, u32[]{:S(2)}, u32[]{:S(2)}) async-start(f32[32,8,8]{2,1,0:T(8,128)} %broadcast_in_dim.24), calls=%async_computation.2 | async-start | bytes 262144 | tf_op jit(solution)/shard_map/all_to_all | solution.py:34

commit v14 on v10

--- a/solution.py
+++ b/solution.py
@@ -202,8 +202,6 @@
             preferred_element_type=jnp.float32,
         )
 
-    own = product_of(w1_ref)
-    other = product_of(w2_ref)
 
     def emit(product, offset):
         for g in range(act_ref.shape[1] // shard):
@@ -215,8 +213,8 @@
             )
 
     core = core_ref[0]
-    emit(own, core * HALF)
-    emit(other, (1 - core) * HALF)
+    emit(product_of(w1_ref), core * HALF)
+    emit(product_of(w2_ref), (1 - core) * HALF)
 
 
 def backward_terms(core, back_rows, first, second, activations, rms, groups):

time: 143 us -> 143 us (level)
  no operation moved by 1% of the time
where the time goes in v14:
time: 143 us; the launch traced here: 142 us
  blocking collectives  79.7 us (56%)
  Pallas kernels  34.7 us (24%)
  waiting for transfers between devices  11.7 us (8%)
  starting transfers between devices  7.33 us (5%)
  other arithmetic  3.97 us (3%)
  local copies, waits for them, and re-layouts  3.04 us (2%)
    all_to_all x1, blocking collectives, copy_for_each(): return lax.all_to_all(copies, axis, split_axis=0, concat_axis=0, tiled=True)  63.7 us
    all_to_all x1, blocking collectives, per_device(): lax.all_to_all(partial_terms, 'fsdp', 0, 0, tiled=True)  16.1 us
    pallas_call x1, Pallas kernels, backward_terms(): pl.pallas_call(backward_kernel, grid_spec=pltpu.PrefetchScalarGridSpec(nu...  13.5 us
    pallas_call x1, Pallas kernels, forward_rows(): pl.pallas_call(forward_second_kernel, grid_spec=pltpu.PrefetchScalarGridS...  12.4 us
    pallas_call x1, Pallas kernels, forward_rows(): pl.pallas_call(forward_first_kernel, grid_spec=pltpu.PrefetchScalarGridSp...  8.74 us
    all_to_all x1, waiting for transfers between devices, copy_for_each(): return lax.all_to_all(copies, axis, split_axis=0, concat_axis=0, tiled=True)  8.18 us
    all_to_all x1, starting transfers between devices, copy_for_each(): return lax.all_to_all(copies, axis, split_axis=0, concat_axis=0, tiled=True)  4.34 us
    ppermute x2, waiting for transfers between devices, sum_over_pairs(): lax.ppermute(shard, axis, [(i, i ^ step) for i in range(devices)])  3.51 us
  transfers between devices with their start and end apart: 4, of which 3 were waited for; matrix products, arithmetic and copies ran while one was open for 1% of the time, Pallas kernels for 6%

profile of v14, /device:TPU:0, one launch (start us, length us, event | category | flops | bytes accessed | tf_op | source)
XLA Modules:
  0.0 142.1 jit_solution(3506299698049371263)
XLA Ops:
  0.6 0.0 copy-start
  0.7 0.7 broadcast_in_dim.21
  1.4 0.7 fusion.4
  2.1 0.0 copy-done
  2.1 0.3 broadcast_in_dim.22
  2.4 0.0 copy-start.1
  2.4 63.7 %all_to_all.15.gd_ref.w_ref.w1_ref = bf16[32,136,512]{2,1,0:T(8,128)(2,1)} all-to-all(bf16[32,136,512]{2,1,0:T(8,128)(2,1)S(1)} %broadcast_in_dim.22), channel_id=1, replica_groups=mesh['dp'=4,'fsdp'=32] {'fsdp'}, dimensions={0} | all-to-all | bytes 8912896 | tf_op jit(solution)/shard_map/all_to_all | solution.py:34
  66.1 0.0 collective-permute-start
  66.1 0.0 copy-done.1
  66.1 0.5 multiply_reduce_fusion
  66.6 0.7 broadcast_in_dim.20.rms_ref
  67.3 8.7 %shard_map.77.acc_in_ref = f32[1152,512]{1,0:T(8,128)} custom-call(s32[1]{0:T(128)} %bitcast.core_ref, bf16[128,8192]{1,0:T(8,128)(2,1)} %act_ref.5, f32[128,128]{1,0:T(8,128)} %broadcast_in_dim.20.rms_ref, bf16[32,136,512]{2,1,0:T(8,128)(2,1)} %all_to_all.15.gd_ref.w_ref.w1_ref, bf16[32,136,512]{2,1,0:T(8,128)(2,1)} %all_to_all.15.gd_ref.w_ref.w1_ref), custom_call_target="tpu_custom_call" | custom-call | tf_op jit(solution)/shard_map/pallas_call | solution.py:158
  76.1 0.0 collective-permute-done.w_ref.w2_ref
  76.1 12.4 %shard_map.78.back_ref = bf16[1152,512]{1,0:T(8,128)(2,1)} custom-call(s32[1]{0:T(128)} %bitcast.core_ref, bf16[128,8192]{1,0:T(8,128)(2,1)} %act_ref.5, f32[128,128]{1,0:T(8,128)} %broadcast_in_dim.20.rms_ref, bf16[32,136,512]{2,1,0:T(8,128)(2,1)} %all_to_all.15.gd_ref.w_ref.w1_ref, bf16[32,136,512]{2,1,0:T(8,128)(2,1)} %collective-permute-done.w_ref.w2_ref, ...), custom_call_target="tpu_custom_call" | custom-call | tf_op jit(solution)/shard_map/pallas_call | solution.py:170
  88.5 13.5 %shard_map.79 = f32[32,9,256]{2,1,0:T(8,128)} custom-call(s32[1]{0:T(128)} %bitcast.core_ref, bf16[1152,512]{1,0:T(8,128)(2,1)} %shard_map.78.back_ref, bf16[32,136,512]{2,1,0:T(8,128)(2,1)} %all_to_all.15.gd_ref.w_ref.w1_ref, bf16[32,136,512]{2,1,0:T(8,128)(2,1)} %collective-permute-done.w_ref.w2_ref, bf16[128,8192]{1,0:T(8,128)(2,1)} %act_ref.5, ...), custom_call_target="tpu_custom_call" | custom-call | tf_op jit(solution)/shard_map/pallas_call | solution.py:225
  102.0 16.1 %all_to_all.16 = f32[32,9,256]{2,1,0:T(8,128)S(1)} all-to-all(f32[32,9,256]{2,1,0:T(8,128)} %shard_map.79), channel_id=1, replica_groups=mesh['dp'=4,'fsdp'=32] {'fsdp'}, dimensions={0} | all-to-all | bytes 589824 | tf_op jit(solution)/shard_map/all_to_all | solution.py:258
  118.1 0.1 reduce_sum.28
  118.1 0.1 collective-permute-start.1
  118.2 1.2 collective-permute-done.1
  119.4 2.9 %collective-permute-start.2 = (f32[9,256]{1,0:T(8,128)S(1)}, f32[9,256]{1,0:T(8,128)S(1)}, u32[]{:S(2)}, u32[]{:S(2)}) collective-permute-start(f32[9,256]{1,0:T(8,128)S(1)} %add.45), channel_id=1, source_target_pairs={{0,64},{32,96},{64,0},{96,32},{1,65},{33,97},{65,1},{97,33},{2,66}... | collective-permute-start | bytes 27656 | tf_op jit(solution)/shard_map/ppermute | solution.py:45
  122.3 2.3 %collective-permute-done.2 = f32[9,256]{1,0:T(8,128)S(1)} collective-permute-done((f32[9,256]{1,0:T(8,128)S(1)}, f32[9,256]{1,0:T(8,128)S(1)}, u32[]{:S(2)}, u32[]{:S(2)}) %collective-permute-start.2) | collective-permute-done | bytes 9248 | tf_op jit(solution)/shard_map/ppermute | solution.py:45
  124.6 0.1 fusion.6
  124.8 0.7 broadcast_in_dim.24
  125.4 4.3 %all-to-all-start.2 = ((f32[32,8,8]{2,1,0:T(8,128)}), f32[32,8,8]{2,1,0:T(8,128)S(1)}, u32[]{:S(2)}, u32[]{:S(2)}) async-start(f32[32,8,8]{2,1,0:T(8,128)} %broadcast_in_dim.24), calls=%async_computation.2 | async-start | bytes 262144 | tf_op jit(solution)/shard_map/all_to_all | solution.py:34
  129.8 0.6 slice.18
  130.3 8.2 %all-to-all-done.2 = f32[32,8,8]{2,1,0:T(8,128)S(1)} async-done(((f32[32,8,8]{2,1,0:T(8,128)}), f32[32,8,8]{2,1,0:T(8,128)S(1)}, u32[]{:S(2)}, u32[]{:S(2)}) %all-to-all-start.2) | async-done | bytes 8224 | tf_op jit(solution)/shard_map/all_to_all | solution.py:34
  138.6 0.1 copy.13
  138.6 0.7 cholesky.16
  139.4 0.6 compare_reduce_fusion
  140.0 0.6 fusion.8
  140.7 0.6 custom-call.7
  141.3 0.8 convolution_multiply_fusion
  (9 shorter events, 0.2 us)
Async XLA Ops:
  0.6 1.4 %copy-start = (bf16[256,512]{1,0:T(8,128)(2,1)S(1)}, bf16[256,512]{1,0:T(8,128)(2,1)}, u32[]{:S(2)}) copy-start(bf16[256,512]{1,0:T(8,128)(2,1)} %param.8) | copy-start | bytes 786436
  2.4 63.7 %copy-start.1 = (bf16[128,8192]{1,0:T(8,128)(2,1)S(1)}, bf16[128,8192]{1,0:T(8,128)(2,1)}, u32[]{:S(2)}) copy-start(bf16[128,8192]{1,0:T(8,128)(2,1)} %act_ref.5) | copy-start | bytes 6291460
  66.1 10.0 %collective-permute-start = (bf16[32,136,512]{2,1,0:T(8,128)(2,1)}, bf16[32,136,512]{2,1,0:T(8,128)(2,1)}, u32[]{:S(2)}, u32[]{:S(2)}) collective-permute-start(bf16[32,136,512]{2,1,0:T(8,128)(2,1)} %all_to_all.15.gd_ref.w_ref.w1_ref), channel_id=1, source_target_pairs={{0,32},{32,0},{64,96},{96,64},{1,33},{33,1},{65,97},{97,65},{2,34}... | collective-permute-start | bytes 13369352 | tf_op jit(solution)/shard_map/ppermute | solution.py:65
  118.1 1.3 collective-permute-start.1
  119.4 5.2 %collective-permute-start.2 = (f32[9,256]{1,0:T(8,128)S(1)}, f32[9,256]{1,0:T(8,128)S(1)}, u32[]{:S(2)}, u32[]{:S(2)}) collective-permute-start(f32[9,256]{1,0:T(8,128)S(1)} %add.45), channel_id=1, source_target_pairs={{0,64},{32,96},{64,0},{96,32},{1,65},{33,97},{65,1},{97,33},{2,66}... | collective-permute-start | bytes 27656 | tf_op jit(solution)/shard_map/ppermute | solution.py:45
  125.4 13.1 %all-to-all-start.2 = ((f32[32,8,8]{2,1,0:T(8,128)}), f32[32,8,8]{2,1,0:T(8,128)S(1)}, u32[]{:S(2)}, u32[]{:S(2)}) async-start(f32[32,8,8]{2,1,0:T(8,128)} %broadcast_in_dim.24), calls=%async_computation.2 | async-start | bytes 262144 | tf_op jit(solution)/shard_map/all_to_all | solution.py:34
